TPU v7x, 32 devices: a whole 2x2x4 slice. The times are simulated.
32 devices in a mesh: ctx: 8 (over z, x), dp: 4 (over y, core).
Axes of the slice: x: 2, y: 2, z: 4, core: 2. Of those that a mesh axis runs over, the one named last changes fastest.
Arguments:
- query: bfloat16 [4, 4096, 2048], P('dp', 'ctx'), may hold values from -0.75 to 0.75
- keys: bfloat16 [4, 4096, 2048], P('dp', 'ctx'), may hold values from -0.75 to 0.75
- values: bfloat16 [4, 4096, 2048], P('dp', 'ctx'), may hold values from -6 to 6
- upstream: bfloat16 [4, 4096, 2048], P('dp', 'ctx'), may hold values from -0.75 to 0.75
- out_weight: bfloat16 [2048, 2048], replicated, may hold values from -0.125 to 0.125
- log_decay: float32 [4, 4096, 16], P('dp', 'ctx'), may hold values from -0.9 to 0, as said below
- signs: int32 [4, 4096], P('dp', 'ctx'), may hold values 0 or 1
- magnitude: float32 [4, 4096], P('dp', 'ctx'), may hold values from 0.5 to 2
Outputs:
- grad_query: bfloat16 [4, 4096, 2048], P('dp', 'ctx')
- grad_keys: bfloat16 [4, 4096, 2048], P('dp', 'ctx')
- grad_values: bfloat16 [4, 4096, 2048], P('dp', 'ctx')
- grad_out_weight: float32 [2048, 2048], P(('ctx', 'dp'))
Inputs may be any that keep to these rules, and one draw needn't show every extreme that they name: `log_decay`: every entry is negative.
All inputs are finite; a program needn't handle non-finite values. No bound on the sum of `signs` on one device may be relied on, other than what follows from the above.
Results may differ from a plain program's by a relative error of at most 0.006.
Values sent between devices are 32-bit elements; how exact they have to be, the bound alone decides.
No kernel may reach another device: no remote copies, remote signals or barrier semaphores. Data moves between devices by JAX's collectives and lax.ppermute only.
A program may use at most 192 MiB of HBM per device.

v0:
```python
import jax
import jax.numpy as jnp
from jax import lax
from jax.sharding import PartitionSpec as P

LOCAL_HEADS = 16
HD = 128
BLOCK = 512


def carried_in(value, axis, join, backward):
    count = lax.axis_size(axis)
    step = -1 if backward else 1
    partial = value
    gathered = None
    distance = 1
    while distance < count:
        pairs = [(i, i + step * distance) for i in range(count) if 0 <= i + step * distance < count]
        arrived = jax.tree.map(lambda part: lax.ppermute(part, axis, pairs), partial)
        gathered = arrived if gathered is None else join(arrived, gathered)
        if distance * 2 < count:
            partial = join(arrived, partial)
        distance *= 2
    if gathered is None:
        gathered = jax.tree.map(jnp.zeros_like, value)
    return gathered


def decay_weights(cumulate, lower_mask):
    spread = cumulate.T[:, :, None] - cumulate.T[:, None, :]
    return jnp.where(lower_mask, jnp.exp(jnp.where(lower_mask, spread, 0.0)), 0.0)


def chain_join(earlier, later):
    return (earlier[0] + later[0], jnp.exp(later[0])[:, None, None] * earlier[1] + later[1])


def on_device(query, keys, values, upstream, out_weight, log_decay, signs, magnitude):
    tokens = query.shape[1]
    width = query.shape[2]
    scale = HD ** (-0.5)

    def to_heads(array):
        return array.reshape(tokens, LOCAL_HEADS, HD)

    decay_here = log_decay[0]
    running = jnp.cumsum(decay_here, axis=0)
    total = running[-1]
    growth = jnp.exp(running)[:, :, None]
    remain = jnp.exp(total[None, :] - running)[:, :, None]
    query_heads = to_heads(query[0])
    key_heads = to_heads(keys[0])
    value_heads = to_heads(values[0])
    query_f32 = query_heads.astype(jnp.float32)
    key_f32 = key_heads.astype(jnp.float32)
    value_f32 = value_heads.astype(jnp.float32)

    state_end = jnp.einsum(
        "shd,she->hde", key_f32 * remain, value_f32, precision=lax.Precision.HIGHEST
    )
    state_in = carried_in((total, state_end), "ctx", chain_join, False)[1]
    state_end, upstream, query_heads = lax.optimization_barrier((state_end, upstream, query_heads))

    advantage = (2 * signs[0] - 1).astype(jnp.float32) * magnitude[0]
    weighted = (advantage[:, None] * upstream[0].astype(jnp.float32)).astype(jnp.bfloat16)
    dout = lax.dot_general(
        weighted, out_weight, (((1,), (1,)), ((), ())), preferred_element_type=jnp.float32
    ).astype(jnp.bfloat16)
    dout_heads = to_heads(dout)
    dout_f32 = dout_heads.astype(jnp.float32)
    back_end = jnp.einsum(
        "thd,the->hde", query_f32 * growth, dout_f32, precision=lax.Precision.HIGHEST
    )

    lower_mask = (jnp.arange(BLOCK)[:, None] >= jnp.arange(BLOCK)[None, :])[None]
    weight = decay_weights(running, lower_mask)
    scores = jnp.einsum("thd,shd->hts", query_heads, key_heads, preferred_element_type=jnp.float32)
    probs = (scale * scores * weight).astype(jnp.bfloat16)
    attend = jnp.einsum("hts,shd->thd", probs, value_heads, preferred_element_type=jnp.float32)
    attend = attend + scale * growth * jnp.einsum(
        "thd,hde->the", query_f32, state_in, precision=lax.Precision.HIGHEST
    )
    attn = attend.reshape(tokens, width).astype(jnp.bfloat16)
    partial = lax.dot_general(
        attn, weighted, (((0,), (0,)), ((), ())), preferred_element_type=jnp.float32
    )
    partial, back_end = lax.optimization_barrier((partial, back_end))
    grad_weight = lax.psum_scatter(partial, ("ctx", "dp"), scatter_dimension=0, tiled=True)
    back_in = carried_in((total, back_end), "ctx", chain_join, True)[1]

    dscores = jnp.einsum(
        "thd,shd->hts", dout_heads, value_heads, preferred_element_type=jnp.float32
    )
    dprobs = (scale * dscores * weight).astype(jnp.bfloat16)
    grad_q = jnp.einsum("hts,shd->thd", dprobs, key_heads, preferred_element_type=jnp.float32)
    grad_k = jnp.einsum("hts,thd->shd", dprobs, query_heads, preferred_element_type=jnp.float32)
    grad_v = jnp.einsum("hts,thd->shd", probs, dout_heads, preferred_element_type=jnp.float32)
    grad_q = grad_q + scale * growth * jnp.einsum(
        "hde,the->thd", state_in, dout_f32, precision=lax.Precision.HIGHEST
    )
    grad_k = grad_k + scale * remain * jnp.einsum(
        "hde,she->shd", back_in, value_f32, precision=lax.Precision.HIGHEST
    )
    grad_v = grad_v + scale * remain * jnp.einsum(
        "hde,shd->she", back_in, key_f32, precision=lax.Precision.HIGHEST
    )
    shape_out = (1, tokens, width)
    return (
        grad_q.reshape(shape_out).astype(jnp.bfloat16),
        grad_k.reshape(shape_out).astype(jnp.bfloat16),
        grad_v.reshape(shape_out).astype(jnp.bfloat16),
        grad_weight,
    )


def solution(mesh):
    in_specs = (
        P("dp", "ctx", None),
        P("dp", "ctx", None),
        P("dp", "ctx", None),
        P("dp", "ctx", None),
        P(),
        P("dp", "ctx", None),
        P("dp", "ctx"),
        P("dp", "ctx"),
    )
    out_specs = (
        P("dp", "ctx", None),
        P("dp", "ctx", None),
        P("dp", "ctx", None),
        P(("ctx", "dp"), None),
    )
    return jax.shard_map(
        on_device, mesh=mesh, in_specs=in_specs, out_specs=out_specs, check_vma=False
    )
```

profile of v0, /device:TPU:11, one launch (start us, length us, event | category | flops | bytes accessed | tf_op | source)
XLA Modules:
  0.0 375.2 jit_solution(7502809985674137489)
XLA Ops:
  7.2 0.7 copy-done
  7.9 1.1 reduce-window.6
  9.5 2.2 collective-permute-start.5
  11.7 4.0 %collective-permute-start = (f32[16]{0:T(128)S(1)}, f32[16]{0:T(128)}, u32[]{:S(2)}, u32[]{:S(2)}) collective-permute-start(f32[16]{0:T(128)S(1)} %slice_reduce_fusion.1), channel_id=1, source_target_pairs={{0,4},{4,8},{8,12},{12,16},{16,20},{20,24},{24,28},{1,5},{5,9},{9,... | collective-permute-start | bytes 200 | tf_op jit(solution)/shard_map/ppermute | solution.py:19
  15.8 2.9 copy.88
  18.7 3.0 copy.92
  21.8 3.7 fusion.14
  25.5 2.3 collective-permute-start.2
  28.5 3.0 copy.77
  31.5 9.9 %convolution_convert_fusion = bf16[512,2048]{1,0:T(8,128)(2,1)} fusion(bf16[2048,2048]{1,0:T(8,128)(2,1)} %param.12, bf16[1,512,2048]{2,1,0:T(8,128)(2,1)} %param.11, f32[512]{0:T(512)S(1)} %bitcast.126), kind=kOutput, calls=%fused_computation.26 | convolution fusion | flops 4299161600 | bytes 12584960 | tf_op jit(solution)/shard_map/dot_general | solution.py:66
  41.4 2.9 copy.89
  44.3 1.2 fusion.34
  45.6 5.4 %collective-permute-done.2 = f32[16,128,128]{2,1,0:T(8,128)S(1)} collective-permute-done((f32[16,128,128]{2,1,0:T(8,128)}, f32[16,128,128]{2,1,0:T(8,128)S(1)}, u32[]{:S(2)}, u32[]{:S(2)}) %collective-permute-start.2) | collective-permute-done | bytes 1048608 | tf_op jit(solution)/shard_map/ppermute | solution.py:19
  51.0 1.8 multiply_add_fusion.3
  52.8 3.4 collective-permute-start.3
  56.2 7.5 %multiply_convert_fusion = bf16[16,512,512]{2,1,0:T(8,128)(2,1)S(1)} fusion(bf16[512,16,128]{0,2,1:T(8,128)(2,1)} %bitcast.113, f32[16,512]{1,0:T(8,128)S(1)} %get-tuple-element.32, pred[512,512]{1,0:T(8,128)(4,1)S(1)} %iota_compare_fusion, bf16[512,16,128]{2,1,0:T(8,128)(2,1)} %bitcast.110), kind=kOutput, calls=%fused_computation | convolution fusion | flops 1098907648 | bytes 12877824 | tf_op jit(solution)/shard_map/thd,shd->hts/dot_general | solution.py:77
  63.7 13.4 %collective-permute-done.3 = f32[16,128,128]{2,1,0:T(8,128)S(1)} collective-permute-done((f32[16,128,128]{2,1,0:T(8,128)S(1)}, f32[16,128,128]{2,1,0:T(8,128)S(1)}, u32[]{:S(2)}, u32[]{:S(2)}) %collective-permute-start.3) | collective-permute-done | bytes 1048608 | tf_op jit(solution)/shard_map/ppermute | solution.py:19
  77.2 1.0 copy-done.20
  78.1 1.1 multiply_add_fusion.2
  79.3 4.3 %collective-permute-start.4 = (f32[16,128,128]{2,1,0:T(8,128)}, f32[16,128,128]{2,1,0:T(8,128)}, u32[]{:S(2)}, u32[]{:S(2)}) collective-permute-start(f32[16,128,128]{2,1,0:T(8,128)} %multiply_add_fusion.2), channel_id=1, source_target_pairs={{0,16},{4,20},{8,24},{12,28},{1,17},{5,21},{9,25},{13,29},{2,18},{... | collective-permute-start | bytes 3145736 | tf_op jit(solution)/shard_map/ppermute | solution.py:19
  83.6 4.9 %fusion.28 = f32[16,512,128]{1,2,0:T(8,128)} fusion(bf16[16,512,512]{2,1,0:T(8,128)(2,1)S(1)} %multiply_convert_fusion, bf16[512,16,128]{2,1,0:T(8,128)(2,1)S(1)} %bitcast.118), kind=kOutput, calls=%fused_computation.36 | convolution fusion | flops 1073741824 | bytes 14680064 | tf_op jit(solution)/shard_map/hts,shd->thd/dot_general | solution.py:79
  88.5 2.1 collective-permute-start.1
  90.6 4.9 %fusion.11 = f32[16,128,128]{2,1,0:T(8,128)} fusion(bf16[512,16,128]{0,2,1:T(8,128)(2,1)S(1)} %bitcast.105, bf16[512,16,128]{0,2,1:T(8,128)(2,1)} %copy.77, f32[512,16]{0,1:T(8,128)S(1)} %get-tuple-element.30), kind=kOutput, calls=%fused_computation.20 | convolution fusion | flops 1612709888 | bytes 5275648 | tf_op jit(solution)/shard_map/thd,the->hde/dot_general | solution.py:71
  95.5 31.9 %collective-permute-done.1 = f32[16]{0:T(128)S(1)} collective-permute-done((f32[16]{0:T(128)S(1)}, f32[16]{0:T(128)S(1)}, u32[]{:S(2)}, u32[]{:S(2)}) %collective-permute-start.1) | collective-permute-done | bytes 96 | tf_op jit(solution)/shard_map/ppermute | solution.py:19
  128.0 1.5 add_add_fusion.1
  129.5 2.1 fusion.8
  131.6 8.2 %fusion.18 = f32[2048,2048]{1,0:T(8,128)} fusion(bf16[512,2048]{0,1:T(8,128)(2,1)S(1)} %bitcast.125, bf16[1,512,2048]{2,1,0:T(8,128)(2,1)S(1)} %copy-done.28, f32[512]{0:T(512)S(1)} %bitcast.127), kind=kOutput, calls=%fused_computation.28 | convolution fusion | flops 4298113024 | bytes 20973568 | tf_op jit(solution)/shard_map/dot_general | solution.py:84
  139.8 4.3 %collective-permute-start.7 = (f32[16,128,128]{2,1,0:T(8,128)}, f32[16,128,128]{2,1,0:T(8,128)S(1)}, u32[]{:S(2)}, u32[]{:S(2)}) collective-permute-start(f32[16,128,128]{2,1,0:T(8,128)} %fusion.11), channel_id=1, source_target_pairs={{4,0},{8,4},{12,8},{16,12},{20,16},{24,20},{28,24},{5,1},{9,5},{13... | collective-permute-start | bytes 3145736 | tf_op jit(solution)/shard_map/ppermute | solution.py:19
  144.1 7.7 %multiply_convert_fusion.1 = bf16[16,512,512]{2,1,0:T(8,128)(2,1)S(1)} fusion(bf16[512,16,128]{0,2,1:T(8,128)(2,1)S(1)} %bitcast.106, f32[16,512]{1,0:T(8,128)S(1)} %get-tuple-element.32, pred[512,512]{1,0:T(8,128)(4,1)S(1)} %iota_compare_fusion, bf16[512,16,128]{2,1,0:T(8,128)(2,1)} %bitcast.117), kind=kOutput, calls=%fused_computation.1 | convolution fusion | flops 1098907648 | bytes 12877824 | tf_op jit(solution)/shard_map/thd,shd->hts/dot_general | solution.py:91
  151.8 25.3 %collective-permute-done.7 = f32[16,128,128]{2,1,0:T(8,128)S(1)} collective-permute-done((f32[16,128,128]{2,1,0:T(8,128)}, f32[16,128,128]{2,1,0:T(8,128)S(1)}, u32[]{:S(2)}, u32[]{:S(2)}) %collective-permute-start.7) | collective-permute-done | bytes 1048608 | tf_op jit(solution)/shard_map/ppermute | solution.py:19
  177.1 0.9 copy-done.17
  178.3 2.3 collective-permute-start.8
  180.6 3.7 fusion.25
  184.3 8.3 %fusion.36 = f32[16,512,128]{1,2,0:T(8,128)} fusion(bf16[16,512,512]{2,1,0:T(8,128)(2,1)} %copy-done.3, bf16[512,16,128]{0,2,1:T(8,128)(2,1)S(1)} %bitcast.115), kind=kOutput, calls=%fused_computation.63 | convolution fusion | flops 1073741824 | bytes 14680064 | tf_op jit(solution)/shard_map/hts,shd->thd/dot_general | solution.py:95
  192.6 1.9 collective-permute-start.6
  194.5 8.2 %collective-permute-done.8 = f32[16,128,128]{2,1,0:T(8,128)S(1)} collective-permute-done((f32[16,128,128]{2,1,0:T(8,128)S(1)}, f32[16,128,128]{2,1,0:T(8,128)S(1)}, u32[]{:S(2)}, u32[]{:S(2)}) %collective-permute-start.8) | collective-permute-done | bytes 1048608 | tf_op jit(solution)/shard_map/ppermute | solution.py:19
  202.7 1.3 multiply_add_fusion
  204.0 1.8 collective-permute-start.9
  205.9 3.3 fusion.37
  209.8 3.5 fusion.10
  213.3 4.1 %copy.83 = bf16[1,512,2048]{2,1,0:T(8,128)(2,1)} copy(bf16[1,512,2048]{1,2,0:T(8,128)(2,1)} %bitcast.120) | data formatting | bytes 4194304
  217.4 11.5 %collective-permute-done.9 = f32[16,128,128]{2,1,0:T(8,128)} collective-permute-done((f32[16,128,128]{2,1,0:T(8,128)}, f32[16,128,128]{2,1,0:T(8,128)}, u32[]{:S(2)}, u32[]{:S(2)}) %collective-permute-start.9) | collective-permute-done | bytes 1048608 | tf_op jit(solution)/shard_map/ppermute | solution.py:19
  228.9 2.2 add_add_fusion
  231.1 3.9 %fusion.6 = bf16[512,16,128]{0,2,1:T(8,128)(2,1)} fusion(f32[16,128,512]{2,1,0:T(8,128)S(1)} %copy-done.4, f32[16,128,128]{2,1,0:T(8,128)S(1)} %add_add_fusion, f32[512,16]{0,1:T(8,128)S(1)} %get-tuple-element.24, bf16[512,16,128]{2,1,0:T(8,128)(2,1)S(1)} %bitcast.119), kind=kOutput, calls=%fused_computation.13 | convolution fusion | flops 1613758464 | bytes 9469952 | tf_op jit(solution)/shard_map/hde,she->shd/dot_general | solution.py:101
  235.0 3.9 %copy.84 = bf16[1,512,2048]{2,1,0:T(8,128)(2,1)} copy(bf16[1,512,2048]{1,2,0:T(8,128)(2,1)} %bitcast.122) | data formatting | bytes 4194304
  238.9 6.3 %fusion.4 = bf16[512,16,128]{0,2,1:T(8,128)(2,1)} fusion(f32[16,128,512]{2,1,0:T(8,128)} %fusion.37, f32[16,128,128]{2,1,0:T(8,128)S(1)} %add_add_fusion, bf16[512,16,128]{0,2,1:T(8,128)(2,1)} %bitcast.114, f32[512,16]{0,1:T(8,128)S(1)} %get-tuple-element.24), kind=kOutput, calls=%fused_computation.10 | convolution fusion | flops 1613758464 | bytes 9469952 | tf_op jit(solution)/shard_map/hde,shd->she/dot_general | solution.py:104
  245.2 3.9 %copy.85 = bf16[1,512,2048]{2,1,0:T(8,128)(2,1)} copy(bf16[1,512,2048]{1,2,0:T(8,128)(2,1)} %bitcast.121) | data formatting | bytes 4194304
  249.1 118.8 %reduce-scatter.2.cloned.1.call-done = f32[64,2048]{1,0:T(8,128)} async-done(((f32[2048,2048]{1,0:T(8,128)}), f32[64,2048]{1,0:T(8,128)}) %reduce-scatter.2.cloned.1.call-update) | async-done | bytes 524304 | tf_op jit(solution)/shard_map/reduce_scatter | solution.py:88
  (79 shorter events, 2.9 us)
Async XLA Ops:
  7.2 0.8 copy-start
  7.2 360.7 %reduce-scatter.2.cloned.1.call-start = ((), (), s32[]{:S(2)}) async-start(), calls=%async_computation.1 | async-start | bytes 17301504 | tf_op jit(solution)/shard_map/reduce_scatter | solution.py:88
  9.5 34.8 %collective-permute-start.5 = (f32[16]{0:T(128)S(1)}, f32[16]{0:T(128)}, u32[]{:S(2)}, u32[]{:S(2)}) collective-permute-start(f32[16]{0:T(128)S(1)} %slice_reduce_fusion.1), channel_id=1, source_target_pairs={{4,0},{8,4},{12,8},{16,12},{20,16},{24,20},{28,24},{5,1},{9,5},{13... | collective-permute-start | bytes 200 | tf_op jit(solution)/shard_map/ppermute | solution.py:19
  11.7 32.6 %collective-permute-start = (f32[16]{0:T(128)S(1)}, f32[16]{0:T(128)}, u32[]{:S(2)}, u32[]{:S(2)}) collective-permute-start(f32[16]{0:T(128)S(1)} %slice_reduce_fusion.1), channel_id=1, source_target_pairs={{0,4},{4,8},{8,12},{12,16},{16,20},{20,24},{24,28},{1,5},{5,9},{9,... | collective-permute-start | bytes 200 | tf_op jit(solution)/shard_map/ppermute | solution.py:19
  18.7 6.8 %copy-start.7 = (bf16[1,512,2048]{1,2,0:T(8,128)(2,1)}, bf16[1,512,2048]{1,2,0:T(8,128)(2,1)S(1)}, u32[]{:S(2)}) copy-start(bf16[1,512,2048]{1,2,0:T(8,128)(2,1)S(1)} %copy.88) | copy-start | bytes 6291460
  18.7 9.1 %copy-start.22 = (bf16[1,512,2048]{2,1,0:T(8,128)(2,1)S(1)}, bf16[1,512,2048]{2,1,0:T(8,128)(2,1)}, u32[]{:S(2)}) copy-start(bf16[1,512,2048]{2,1,0:T(8,128)(2,1)} %param.8) | copy-start | bytes 6291460
  21.7 6.8 %copy-start.9 = (bf16[64,8,16,128]{3,2,1,0:T(8,128)(2,1)}, bf16[64,8,16,128]{3,2,1,0:T(8,128)(2,1)S(1)}, u32[]{:S(2)}) copy-start(bf16[64,8,16,128]{3,2,1,0:T(8,128)(2,1)S(1)} %copy.92) | copy-start | bytes 6291460
  25.5 25.5 %collective-permute-start.2 = (f32[16,128,128]{2,1,0:T(8,128)}, f32[16,128,128]{2,1,0:T(8,128)S(1)}, u32[]{:S(2)}, u32[]{:S(2)}) collective-permute-start(f32[16,128,128]{2,1,0:T(8,128)} %fusion.14), channel_id=1, source_target_pairs={{0,4},{4,8},{8,12},{12,16},{16,20},{20,24},{24,28},{1,5},{5,9},{9,... | collective-permute-start | bytes 3145736 | tf_op jit(solution)/shard_map/ppermute | solution.py:19
  27.9 3.7 copy-start.23
  27.9 3.7 copy-start.24
  28.5 3.0 copy-start.5
  51.0 5.2 %copy-start.15 = (f32[16,128,128]{2,1,0:T(8,128)}, f32[16,128,128]{2,1,0:T(8,128)S(1)}, u32[]{:S(2)}) copy-start(f32[16,128,128]{2,1,0:T(8,128)S(1)} %collective-permute-done.2) | copy-start | bytes 3145732
  52.8 24.4 %collective-permute-start.3 = (f32[16,128,128]{2,1,0:T(8,128)S(1)}, f32[16,128,128]{2,1,0:T(8,128)S(1)}, u32[]{:S(2)}, u32[]{:S(2)}) collective-permute-start(f32[16,128,128]{2,1,0:T(8,128)S(1)} %multiply_add_fusion.3), channel_id=1, source_target_pairs={{0,8},{4,12},{8,16},{12,20},{16,24},{20,28},{1,9},{5,13},{9,17},{1... | collective-permute-start | bytes 3145736 | tf_op jit(solution)/shard_map/ppermute | solution.py:19
  63.7 24.8 %copy-start.2 = (bf16[16,512,512]{2,1,0:T(8,128)(2,1)}, bf16[16,512,512]{2,1,0:T(8,128)(2,1)S(1)}, u32[]{:S(2)}) copy-start(bf16[16,512,512]{2,1,0:T(8,128)(2,1)S(1)} %multiply_convert_fusion) | copy-start | bytes 25165828
  63.7 19.9 %copy-start.10 = (bf16[64,8,16,128]{3,2,1,0:T(8,128)(2,1)S(1)}, bf16[64,8,16,128]{3,2,1,0:T(8,128)(2,1)}, u32[]{:S(2)}) copy-start(bf16[64,8,16,128]{3,2,1,0:T(8,128)(2,1)} %copy-done.9) | copy-start | bytes 6291460
  77.2 1.0 copy-start.20
  79.3 9.2 %copy-start.27 = (f32[16]{0:T(128)S(1)}, f32[16]{0:T(128)}, u32[]{:S(2)}) copy-start(f32[16]{0:T(128)} %get-tuple-element.38) | copy-start | bytes 196
  79.3 48.7 %collective-permute-start.4 = (f32[16,128,128]{2,1,0:T(8,128)}, f32[16,128,128]{2,1,0:T(8,128)}, u32[]{:S(2)}, u32[]{:S(2)}) collective-permute-start(f32[16,128,128]{2,1,0:T(8,128)} %multiply_add_fusion.2), channel_id=1, source_target_pairs={{0,16},{4,20},{8,24},{12,28},{1,17},{5,21},{9,25},{13,29},{2,18},{... | collective-permute-start | bytes 3145736 | tf_op jit(solution)/shard_map/ppermute | solution.py:19
  88.5 39.5 %copy-start.16 = (f32[16,128,128]{2,1,0:T(8,128)S(1)}, f32[16,128,128]{2,1,0:T(8,128)}, u32[]{:S(2)}) copy-start(f32[16,128,128]{2,1,0:T(8,128)} %copy-done.15) | copy-start | bytes 3145732
  88.5 39.5 %copy-start.21 = (f32[16,128,128]{2,1,0:T(8,128)S(1)}, f32[16,128,128]{2,1,0:T(8,128)}, u32[]{:S(2)}) copy-start(f32[16,128,128]{2,1,0:T(8,128)} %copy-done.20) | copy-start | bytes 3145732
  88.5 38.9 %collective-permute-start.1 = (f32[16]{0:T(128)S(1)}, f32[16]{0:T(128)S(1)}, u32[]{:S(2)}, u32[]{:S(2)}) collective-permute-start(f32[16]{0:T(128)S(1)} %copy-done.27), channel_id=1, source_target_pairs={{0,8},{4,12},{8,16},{12,20},{16,24},{20,28},{1,9},{5,13},{9,17},{1... | collective-permute-start | bytes 200 | tf_op jit(solution)/shard_map/ppermute | solution.py:19
  90.5 38.9 %copy-start.12 = (bf16[512,16,128]{0,2,1:T(8,128)(2,1)S(1)}, bf16[512,16,128]{0,2,1:T(8,128)(2,1)}, u32[]{:S(2)}) copy-start(bf16[512,16,128]{0,2,1:T(8,128)(2,1)} %copy.77) | copy-start | bytes 6291460
  90.5 38.9 %copy-start.14 = (f32[16,512,128]{1,2,0:T(8,128)S(1)}, f32[16,512,128]{1,2,0:T(8,128)}, u32[]{:S(2)}) copy-start(f32[16,512,128]{1,2,0:T(8,128)} %fusion.28) | copy-start | bytes 12582916
  129.5 2.1 copy-start.28
  139.8 38.3 %copy-start.18 = (f32[16,128,128]{2,1,0:T(8,128)S(1)}, f32[16,128,128]{2,1,0:T(8,128)}, u32[]{:S(2)}) copy-start(f32[16,128,128]{2,1,0:T(8,128)} %fusion.11) | copy-start | bytes 3145732
  139.8 37.3 %collective-permute-start.7 = (f32[16,128,128]{2,1,0:T(8,128)}, f32[16,128,128]{2,1,0:T(8,128)S(1)}, u32[]{:S(2)}, u32[]{:S(2)}) collective-permute-start(f32[16,128,128]{2,1,0:T(8,128)} %fusion.11), channel_id=1, source_target_pairs={{4,0},{8,4},{12,8},{16,12},{20,16},{24,20},{28,24},{5,1},{9,5},{13... | collective-permute-start | bytes 3145736 | tf_op jit(solution)/shard_map/ppermute | solution.py:19
  151.8 28.8 %copy-start.3 = (bf16[16,512,512]{2,1,0:T(8,128)(2,1)}, bf16[16,512,512]{2,1,0:T(8,128)(2,1)S(1)}, u32[]{:S(2)}) copy-start(bf16[16,512,512]{2,1,0:T(8,128)(2,1)S(1)} %multiply_convert_fusion.1) | copy-start | bytes 25165828
  151.8 28.8 %copy-start.6 = (bf16[64,8,16,128]{3,2,1,0:T(8,128)(2,1)S(1)}, bf16[64,8,16,128]{3,2,1,0:T(8,128)(2,1)}, u32[]{:S(2)}) copy-start(bf16[64,8,16,128]{3,2,1,0:T(8,128)(2,1)} %copy-done.5) | copy-start | bytes 6291460
  177.1 0.9 copy-start.17
  178.0 27.8 %slice-start = ((s8[8388608]{0:T(1024)(128)(4,1)}), s8[4194304]{0:T(1024)(128)(4,1)S(1)}, s32[]{:S(2)}) async-start(s8[8388608]{0:T(1024)(128)(4,1)} %bitcast.103), calls=%async_computation.2 | async-start | bytes 8388608
  178.2 6.1 %copy-start.8 = (bf16[1,512,2048]{1,2,0:T(8,128)(2,1)S(1)}, bf16[1,512,2048]{1,2,0:T(8,128)(2,1)}, u32[]{:S(2)}) copy-start(bf16[1,512,2048]{1,2,0:T(8,128)(2,1)} %copy-done.7) | copy-start | bytes 6291460
  178.2 27.6 %slice-start.1 = ((s8[8388608]{0:T(1024)(128)(4,1)}), s8[4194304]{0:T(1024)(128)(4,1)S(1)}, s32[]{:S(2)}) async-start(s8[8388608]{0:T(1024)(128)(4,1)} %bitcast.103), calls=%async_computation.3 | async-start | bytes 8388608
  178.3 24.5 %collective-permute-start.8 = (f32[16,128,128]{2,1,0:T(8,128)S(1)}, f32[16,128,128]{2,1,0:T(8,128)S(1)}, u32[]{:S(2)}, u32[]{:S(2)}) collective-permute-start(f32[16,128,128]{2,1,0:T(8,128)S(1)} %multiply_add_fusion.1), channel_id=1, source_target_pairs={{8,0},{12,4},{16,8},{20,12},{24,16},{28,20},{9,1},{13,5},{17,9},{2... | collective-permute-start | bytes 3145736 | tf_op jit(solution)/shard_map/ppermute | solution.py:19
  184.3 8.3 %copy-start.26 = (f32[16]{0:T(128)S(1)}, f32[16]{0:T(128)}, u32[]{:S(2)}) copy-start(f32[16]{0:T(128)} %get-tuple-element.27) | copy-start | bytes 196
  184.3 18.4 %copy-start.25 = (f32[16]{0:T(128)S(1)}, f32[16]{0:T(128)}, u32[]{:S(2)}) copy-start(f32[16]{0:T(128)} %get-tuple-element.26) | copy-start | bytes 196
  192.6 16.5 %collective-permute-start.6 = (f32[16]{0:T(128)S(1)}, f32[16]{0:T(128)S(1)}, u32[]{:S(2)}, u32[]{:S(2)}) collective-permute-start(f32[16]{0:T(128)S(1)} %copy-done.26), channel_id=1, source_target_pairs={{8,0},{12,4},{16,8},{20,12},{24,16},{28,20},{9,1},{13,5},{17,9},{2... | collective-permute-start | bytes 200 | tf_op jit(solution)/shard_map/ppermute | solution.py:19
  202.7 6.4 %copy-start.19 = (f32[16,128,128]{2,1,0:T(8,128)}, f32[16,128,128]{2,1,0:T(8,128)S(1)}, u32[]{:S(2)}) copy-start(f32[16,128,128]{2,1,0:T(8,128)S(1)} %collective-permute-done.8) | copy-start | bytes 3145732
  204.0 5.8 %copy-start.13 = (f32[16,512,128]{1,2,0:T(8,128)S(1)}, f32[16,512,128]{1,2,0:T(8,128)}, u32[]{:S(2)}) copy-start(f32[16,512,128]{1,2,0:T(8,128)} %fusion.36) | copy-start | bytes 12582916
  204.0 24.8 %collective-permute-start.9 = (f32[16,128,128]{2,1,0:T(8,128)}, f32[16,128,128]{2,1,0:T(8,128)}, u32[]{:S(2)}, u32[]{:S(2)}) collective-permute-start(f32[16,128,128]{2,1,0:T(8,128)} %multiply_add_fusion), channel_id=1, source_target_pairs={{16,0},{20,4},{24,8},{28,12},{17,1},{21,5},{25,9},{29,13},{18,2},{... | collective-permute-start | bytes 3145736 | tf_op jit(solution)/shard_map/ppermute | solution.py:19
  213.3 17.8 %copy-start.11 = (bf16[64,8,16,128]{3,2,1,0:T(8,128)(2,1)S(1)}, bf16[64,8,16,128]{3,2,1,0:T(8,128)(2,1)}, u32[]{:S(2)}) copy-start(bf16[64,8,16,128]{3,2,1,0:T(8,128)(2,1)} %copy-done.9) | copy-start | bytes 6291460
  217.4 13.7 %copy-start.4 = (f32[16,128,512]{2,1,0:T(8,128)S(1)}, f32[16,128,512]{2,1,0:T(8,128)}, u32[]{:S(2)}) copy-start(f32[16,128,512]{2,1,0:T(8,128)} %fusion.25) | copy-start | bytes 12582916
  238.9 129.0 %copy-start.1 = (f32[1,512,16]{1,2,0:T(8,128)S(1)}, f32[1,512,16]{1,2,0:T(8,128)}, u32[]{:S(2)}) copy-start(f32[1,512,16]{1,2,0:T(8,128)} %param.13) | copy-start | bytes 98308
Sparse Core Ops, SparseCore 0:
  139.9 227.9 reduce-scatter.1
where the time goes:
time: 383 us; the launch traced here: 375 us
  waiting for transfers between devices  215 us (56%)
  matrix products  77.8 us (20%)
  starting transfers between devices  28.6 us (7%)
  local copies, waits for them, and re-layouts  27.3 us (7%)
  between operations  15 us (4%)
  other arithmetic  12 us (3%)
    reduce_scatter x1, waiting for transfers between devices, on_device(): lax.psum_scatter(partial, ('ctx', 'dp'), scatter_dimension=0, tiled=True)  119 us
    ppermute x10, waiting for transfers between devices, carried_in(): lax.ppermute(part, axis, pairs)  95.8 us
    ppermute x10, starting transfers between devices, carried_in(): lax.ppermute(part, axis, pairs)  28.5 us
    unnamed x67, local copies, waits for them, and re-layouts  18.3 us
    dot_general x1, matrix products, on_device(): lax.dot_general(weighted, out_weight, (((1,), (1,)), ((), ())), preferred...  9.89 us
    dot_general x1, matrix products, on_device(): jnp.einsum('hts,shd->thd', dprobs, key_heads, preferred_element_type=jnp....  8.26 us
    dot_general x1, matrix products, on_device(): lax.dot_general(attn, weighted, (((0,), (0,)), ((), ())), preferred_eleme...  8.18 us
    add x6, other arithmetic, chain_join(): jnp.exp(later[0])[:, None, None] * earlier[1] + later[1]  8.08 us
  transfers between devices with their start and end apart: 11, of which 7 were waited for; matrix products, arithmetic and copies ran while one was open for 26% of the time, Pallas kernels for 0%

commit v1 on v0

--- a/solution.py
+++ b/solution.py
@@ -8,15 +8,19 @@
 BLOCK = 512
 
 
-def carried_in(value, axis, join, backward):
-    count = lax.axis_size(axis)
-    step = -1 if backward else 1
+def carried_in(value, join, even_backward):
+    count, groups = lax.axis_size("ctx"), lax.axis_size("dp")
     partial = value
     gathered = None
     distance = 1
     while distance < count:
-        pairs = [(i, i + step * distance) for i in range(count) if 0 <= i + step * distance < count]
-        arrived = jax.tree.map(lambda part: lax.ppermute(part, axis, pairs), partial)
+        pairs = []
+        for place in range(count):
+            for group in range(groups):
+                step = -distance if (group % 2 == 0) == even_backward else distance
+                if 0 <= place + step < count:
+                    pairs.append((place * groups + group, (place + step) * groups + group))
+        arrived = jax.tree.map(lambda part: lax.ppermute(part, ("ctx", "dp"), pairs), partial)
         gathered = arrived if gathered is None else join(arrived, gathered)
         if distance * 2 < count:
             partial = join(arrived, partial)
@@ -58,8 +62,6 @@
     state_end = jnp.einsum(
         "shd,she->hde", key_f32 * remain, value_f32, precision=lax.Precision.HIGHEST
     )
-    state_in = carried_in((total, state_end), "ctx", chain_join, False)[1]
-    state_end, upstream, query_heads = lax.optimization_barrier((state_end, upstream, query_heads))
 
     advantage = (2 * signs[0] - 1).astype(jnp.float32) * magnitude[0]
     weighted = (advantage[:, None] * upstream[0].astype(jnp.float32)).astype(jnp.bfloat16)
@@ -71,6 +73,12 @@
     back_end = jnp.einsum(
         "thd,the->hde", query_f32 * growth, dout_f32, precision=lax.Precision.HIGHEST
     )
+    even = lax.axis_index("dp") % 2 == 0
+    first = carried_in((total, jnp.where(even, state_end, back_end)), chain_join, False)[1]
+    second_end, first = lax.optimization_barrier((jnp.where(even, back_end, state_end), first))
+    second = carried_in((total, second_end), chain_join, True)[1]
+    state_in = jnp.where(even, first, second)
+    back_in = jnp.where(even, second, first)
 
     lower_mask = (jnp.arange(BLOCK)[:, None] >= jnp.arange(BLOCK)[None, :])[None]
     weight = decay_weights(running, lower_mask)
@@ -84,9 +92,8 @@
     partial = lax.dot_general(
         attn, weighted, (((0,), (0,)), ((), ())), preferred_element_type=jnp.float32
     )
-    partial, back_end = lax.optimization_barrier((partial, back_end))
+    partial, back_in = lax.optimization_barrier((partial, back_in))
     grad_weight = lax.psum_scatter(partial, ("ctx", "dp"), scatter_dimension=0, tiled=True)
-    back_in = carried_in((total, back_end), "ctx", chain_join, True)[1]
 
     dscores = jnp.einsum(
         "thd,shd->hts", dout_heads, value_heads, preferred_element_type=jnp.float32

time: 383 us -> 387 us (1.010); the launches traced: 375 us -> 384 us
  waiting for transfers between devices: 215 us -> 236 us
  starting transfers between devices: 28.6 us -> 22.8 us
  other arithmetic: 12 us -> 7.07 us
    reduce_scatter x1, waiting for transfers between devices: 119 us -> 137 us  [on_device(): lax.psum_scatter(partial, ('ctx', 'dp'), scatter_dimension=0, tiled=True)]
    add x6 -> x5, other arithmetic: 8.08 us -> 2.07 us  [chain_join(): jnp.exp(later[0])[:, None, None] * earlier[1] + later[1]]
    ppermute x10, starting transfers between devices: 28.5 us -> 22.8 us  [carried_in(): lax.ppermute(part, ('ctx', 'dp'), pairs)]
    unnamed x67 -> x40, local copies, waits for them, and re-layouts: 18.3 us -> 15.2 us
  transfers between devices with their start and end apart: 11 -> 11, of which waited for: 7 -> 8; matrix products, arithmetic and copies ran while one was open for 26% -> 17% of each run, Pallas kernels for 0% -> 0%
where the time goes in v1:
time: 387 us; the launch traced here: 384 us
  waiting for transfers between devices  236 us (61%)
  matrix products  77.9 us (20%)
  local copies, waits for them, and re-layouts  26.3 us (7%)
  starting transfers between devices  22.8 us (6%)
  between operations  14.3 us (4%)
  other arithmetic  7.07 us (2%)
    reduce_scatter x1, waiting for transfers between devices, on_device(): lax.psum_scatter(partial, ('ctx', 'dp'), scatter_dimension=0, tiled=True)  137 us
    ppermute x10, waiting for transfers between devices, carried_in(): lax.ppermute(part, ('ctx', 'dp'), pairs)  98.3 us
    ppermute x10, starting transfers between devices, carried_in(): lax.ppermute(part, ('ctx', 'dp'), pairs)  22.8 us
    unnamed x40, local copies, waits for them, and re-layouts  15.2 us
    dot_general x1, matrix products, on_device(): lax.dot_general(weighted, out_weight, (((1,), (1,)), ((), ())), preferred...  9.88 us
    dot_general x1, matrix products, on_device(): lax.dot_general(attn, weighted, (((0,), (0,)), ((), ())), preferred_eleme...  8.49 us
    another operation x2, local copies, waits for them, and re-layouts, to_heads(): return array.reshape(tokens, LOCAL_HEADS, HD)  7.85 us
  transfers between devices with their start and end apart: 11, of which 8 were waited for; matrix products, arithmetic and copies ran while one was open for 17% of the time, Pallas kernels for 0%

profile of v1, /device:TPU:11, one launch (start us, length us, event | category | flops | bytes accessed | tf_op | source)
XLA Modules:
  0.0 384.0 jit_solution(16121544065759571698)
XLA Ops:
  7.2 0.7 copy-done
  7.9 1.1 reduce-window.6
  9.3 0.2 slice_reduce_fusion.1
  9.6 0.7 convert_multiply_fusion.1
  10.4 9.9 %convolution_convert_fusion = bf16[512,2048]{1,0:T(8,128)(2,1)} fusion(bf16[2048,2048]{1,0:T(8,128)(2,1)} %param.12, bf16[1,512,2048]{2,1,0:T(8,128)(2,1)} %param.11, f32[512]{0:T(512)S(1)} %bitcast.122), kind=kOutput, calls=%fused_computation.26 | convolution fusion | flops 4299161600 | bytes 12584960 | tf_op jit(solution)/shard_map/dot_general | solution.py:68
  20.2 2.9 copy.88
  23.1 3.9 %copy.90 = bf16[1,512,2048]{1,2,0:T(8,128)(2,1)} copy(bf16[1,512,2048]{2,1,0:T(8,128)(2,1)} %param.8) | data formatting | bytes 4194304 | tf_op jit(solution)/shard_map/reshape;squeeze | solution.py:48
  27.0 3.9 %copy.89 = bf16[1,512,2048]{1,2,0:T(8,128)(2,1)} copy(bf16[1,512,2048]{2,1,0:T(8,128)(2,1)} %param.9) | data formatting | bytes 4194304 | tf_op jit(solution)/shard_map/reshape;squeeze | solution.py:48
  31.0 2.3 copy.93
  33.3 2.3 fusion.14
  35.6 2.8 broadcast_select_fusion.2
  38.4 2.2 collective-permute-start.2
  40.6 4.0 %collective-permute-start.5 = (f32[16]{0:T(128)S(1)}, f32[16]{0:T(128)S(1)}, u32[]{:S(2)}, u32[]{:S(2)}) collective-permute-start(f32[16]{0:T(128)S(1)} %slice_reduce_fusion.1), channel_id=1, source_target_pairs={{1,5},{3,7},{4,0},{5,9},{6,2},{7,11},{8,4},{9,13},{10,6},{11,15},{... | collective-permute-start | bytes 200 | tf_op jit(solution)/shard_map/ppermute | solution.py:23
  44.6 1.9 collective-permute-start
  46.5 8.7 %collective-permute-done.5 = f32[16]{0:T(128)S(1)} collective-permute-done((f32[16]{0:T(128)S(1)}, f32[16]{0:T(128)S(1)}, u32[]{:S(2)}, u32[]{:S(2)}) %collective-permute-start.5) | collective-permute-done | bytes 96 | tf_op jit(solution)/shard_map/ppermute | solution.py:23
  55.2 8.4 %collective-permute-done = f32[16]{0:T(128)S(1)} collective-permute-done((f32[16]{0:T(128)S(1)}, f32[16]{0:T(128)S(1)}, u32[]{:S(2)}, u32[]{:S(2)}) %collective-permute-start) | collective-permute-done | bytes 96 | tf_op jit(solution)/shard_map/ppermute | solution.py:23
  63.6 0.2 multiply_add_fusion.3
  63.8 1.9 collective-permute-start.3
  65.7 13.9 %collective-permute-done.3 = f32[16,128,128]{2,1,0:T(8,128)S(1)} collective-permute-done((f32[16,128,128]{2,1,0:T(8,128)S(1)}, f32[16,128,128]{2,1,0:T(8,128)S(1)}, u32[]{:S(2)}, u32[]{:S(2)}) %collective-permute-start.3) | collective-permute-done | bytes 1048608 | tf_op jit(solution)/shard_map/ppermute | solution.py:23
  79.6 0.2 multiply_add_fusion.2
  79.8 1.3 collective-permute-start.4
  81.1 1.9 collective-permute-start.1
  83.0 23.0 %collective-permute-done.1 = f32[16]{0:T(128)S(1)} collective-permute-done((f32[16]{0:T(128)S(1)}, f32[16]{0:T(128)S(1)}, u32[]{:S(2)}, u32[]{:S(2)}) %collective-permute-start.1) | collective-permute-done | bytes 96 | tf_op jit(solution)/shard_map/ppermute | solution.py:23
  106.0 0.3 add_add_fusion.1
  106.3 3.2 collective-permute-start.7
  109.4 24.1 %collective-permute-done.7 = f32[16,128,128]{2,1,0:T(8,128)S(1)} collective-permute-done((f32[16,128,128]{2,1,0:T(8,128)S(1)}, f32[16,128,128]{2,1,0:T(8,128)S(1)}, u32[]{:S(2)}, u32[]{:S(2)}) %collective-permute-start.7) | collective-permute-done | bytes 1048608 | tf_op jit(solution)/shard_map/ppermute | solution.py:23
  133.7 2.1 collective-permute-start.8
  135.9 13.6 %collective-permute-done.8 = f32[16,128,128]{2,1,0:T(8,128)S(1)} collective-permute-done((f32[16,128,128]{2,1,0:T(8,128)S(1)}, f32[16,128,128]{2,1,0:T(8,128)S(1)}, u32[]{:S(2)}, u32[]{:S(2)}) %collective-permute-start.8) | collective-permute-done | bytes 1048608 | tf_op jit(solution)/shard_map/ppermute | solution.py:23
  149.5 1.3 multiply_add_fusion
  150.9 2.3 collective-permute-start.9
  153.2 6.3 %multiply_convert_fusion = bf16[16,512,512]{2,1,0:T(8,128)(2,1)S(1)} fusion(bf16[512,16,128]{0,2,1:T(8,128)(2,1)S(1)} %bitcast.106, bf16[512,16,128]{0,2,1:T(8,128)(2,1)S(1)} %bitcast.110, f32[16,512]{1,0:T(8,128)S(1)} %get-tuple-element.37, pred[512,512]{1,0:T(8,128)(4,1)S(1)} %iota_compare_fusion), kind=kOutput, calls=%fused_computation | convolution fusion | flops 1098907648 | bytes 12877824 | tf_op jit(solution)/shard_map/thd,shd->hts/dot_general | solution.py:85
  159.5 1.9 collective-permute-start.6
  161.4 7.3 %fusion.25 = f32[16,512,128]{1,2,0:T(8,128)} fusion(bf16[16,512,512]{2,1,0:T(8,128)(2,1)S(1)} %multiply_convert_fusion, bf16[512,16,128]{2,1,0:T(8,128)(2,1)} %bitcast.114), kind=kOutput, calls=%fused_computation.33 | convolution fusion | flops 1073741824 | bytes 14680064 | tf_op jit(solution)/shard_map/hts,shd->thd/dot_general | solution.py:87
  168.8 6.7 %collective-permute-done.6 = f32[16]{0:T(128)S(1)} collective-permute-done((f32[16]{0:T(128)S(1)}, f32[16]{0:T(128)S(1)}, u32[]{:S(2)}, u32[]{:S(2)}) %collective-permute-start.6) | collective-permute-done | bytes 96 | tf_op jit(solution)/shard_map/ppermute | solution.py:23
  175.4 2.9 broadcast_select_fusion
  178.3 2.1 fusion.8
  180.4 8.5 %fusion.18 = f32[2048,2048]{1,0:T(8,128)} fusion(bf16[512,2048]{0,1:T(8,128)(2,1)S(1)} %bitcast.121, bf16[1,512,2048]{2,1,0:T(8,128)(2,1)S(1)} %copy-done.17, f32[512]{0:T(512)S(1)} %bitcast.123), kind=kOutput, calls=%fused_computation.28 | convolution fusion | flops 4298113024 | bytes 20973568 | tf_op jit(solution)/shard_map/dot_general | solution.py:92
  188.9 6.8 %fusion.34 = f32[16,128,512]{2,1,0:T(8,128)} fusion(bf16[512,16,128]{0,2,1:T(8,128)(2,1)S(1)} %bitcast.102, bf16[16,512,512]{2,1,0:T(8,128)(2,1)} %copy-done.2), kind=kOutput, calls=%fused_computation.65 | convolution fusion | flops 1073741824 | bytes 14680064 | tf_op jit(solution)/shard_map/hts,thd->shd/dot_general | solution.py:104
  195.7 6.9 %multiply_convert_fusion.1 = bf16[16,512,512]{2,1,0:T(8,128)(2,1)S(1)} fusion(bf16[512,16,128]{0,2,1:T(8,128)(2,1)S(1)} %bitcast.103, f32[16,512]{1,0:T(8,128)S(1)} %get-tuple-element.37, pred[512,512]{1,0:T(8,128)(4,1)S(1)} %iota_compare_fusion, bf16[512,16,128]{2,1,0:T(8,128)(2,1)S(1)} %bitcast.115), kind=kOutput, calls=%fused_computation.1 | convolution fusion | flops 1098907648 | bytes 12877824 | tf_op jit(solution)/shard_map/thd,shd->hts/dot_general | solution.py:98
  202.6 3.2 fusion.35
  205.8 4.8 %fusion.33 = f32[16,512,128]{1,2,0:T(8,128)} fusion(bf16[16,512,512]{2,1,0:T(8,128)(2,1)S(1)} %multiply_convert_fusion.1, bf16[512,16,128]{0,2,1:T(8,128)(2,1)S(1)} %bitcast.111), kind=kOutput, calls=%fused_computation.64 | convolution fusion | flops 1073741824 | bytes 14680064 | tf_op jit(solution)/shard_map/hts,shd->thd/dot_general | solution.py:102
  210.6 5.5 %fusion.10 = bf16[512,16,128]{0,2,1:T(8,128)(2,1)} fusion(f32[16,512,128]{1,2,0:T(8,128)} %fusion.33, bf16[512,16,128]{0,2,1:T(8,128)(2,1)S(1)} %bitcast.104, f32[512,16]{0,1:T(8,128)S(1)} %get-tuple-element.35, f32[16,128,128]{2,1,0:T(8,128)S(1)} %add_add_fusion.1, f32[16,128,128]{2,1,0:T(8,128)S(1)} %copy-done.15, pred[]{:T(512)S(6)} %eq.5), kind=kOutput, calls=%fused_computation.19 | convolution fusion | flops 1614020608 | bytes 10518529 | tf_op jit(solution)/shard_map/hde,the->thd/dot_general | solution.py:105
  216.2 4.1 %copy.83 = bf16[1,512,2048]{2,1,0:T(8,128)(2,1)} copy(bf16[1,512,2048]{1,2,0:T(8,128)(2,1)} %bitcast.117) | data formatting | bytes 4194304
  220.3 6.0 %fusion.6 = bf16[512,16,128]{0,2,1:T(8,128)(2,1)} fusion(f32[16,512,128]{1,2,0:T(8,128)} %fusion.35, f32[16,128,128]{2,1,0:T(8,128)S(1)} %copy-done.13, f32[512,16]{0,1:T(8,128)S(1)} %get-tuple-element.24, bf16[512,16,128]{2,1,0:T(8,128)(2,1)S(1)} %bitcast.116), kind=kOutput, calls=%fused_computation.13 | convolution fusion | flops 1613758464 | bytes 9469952 | tf_op jit(solution)/shard_map/hde,she->shd/dot_general | solution.py:108
  226.2 4.1 %copy.84 = bf16[1,512,2048]{2,1,0:T(8,128)(2,1)} copy(bf16[1,512,2048]{1,2,0:T(8,128)(2,1)} %bitcast.119) | data formatting | bytes 4194304
  230.3 5.6 %fusion.4 = bf16[512,16,128]{0,2,1:T(8,128)(2,1)} fusion(f32[16,128,512]{2,1,0:T(8,128)} %fusion.34, f32[16,128,128]{2,1,0:T(8,128)S(1)} %copy-done.13, bf16[512,16,128]{0,2,1:T(8,128)(2,1)S(1)} %bitcast.112, f32[512,16]{0,1:T(8,128)S(1)} %get-tuple-element.24), kind=kOutput, calls=%fused_computation.10 | convolution fusion | flops 1613758464 | bytes 9469952 | tf_op jit(solution)/shard_map/hde,shd->she/dot_general | solution.py:111
  235.9 3.9 %copy.85 = bf16[1,512,2048]{2,1,0:T(8,128)(2,1)} copy(bf16[1,512,2048]{1,2,0:T(8,128)(2,1)} %bitcast.118) | data formatting | bytes 4194304
  239.9 137.3 %reduce-scatter.2.cloned.1.call-done = f32[64,2048]{1,0:T(8,128)} async-done(((f32[2048,2048]{1,0:T(8,128)}), f32[64,2048]{1,0:T(8,128)}) %reduce-scatter.2.cloned.1.call-update) | async-done | bytes 524304 | tf_op jit(solution)/shard_map/reduce_scatter | solution.py:96
  (51 shorter events, 0.8 us)
Async XLA Ops:
  7.2 0.8 copy-start
  7.2 370.0 %reduce-scatter.2.cloned.1.call-start = ((), (), s32[]{:S(2)}) async-start(), calls=%async_computation.1 | async-start | bytes 17301504 | tf_op jit(solution)/shard_map/reduce_scatter | solution.py:96
  31.0 2.4 copy-start.3
  31.0 4.7 %copy-start.6 = (bf16[1,512,2048]{1,2,0:T(8,128)(2,1)S(1)}, bf16[1,512,2048]{1,2,0:T(8,128)(2,1)}, u32[]{:S(2)}) copy-start(bf16[1,512,2048]{1,2,0:T(8,128)(2,1)} %copy.89) | copy-start | bytes 6291460
  33.3 100.4 %copy-start.9 = (bf16[64,8,16,128]{3,2,1,0:T(8,128)(2,1)}, bf16[64,8,16,128]{3,2,1,0:T(8,128)(2,1)S(1)}, u32[]{:S(2)}) copy-start(bf16[64,8,16,128]{3,2,1,0:T(8,128)(2,1)S(1)} %copy.93) | copy-start | bytes 6291460
  38.4 25.2 %collective-permute-start.2 = (f32[16,128,128]{2,1,0:T(8,128)S(1)}, f32[16,128,128]{2,1,0:T(8,128)S(1)}, u32[]{:S(2)}, u32[]{:S(2)}) collective-permute-start(f32[16,128,128]{2,1,0:T(8,128)S(1)} %get-tuple-element.32), channel_id=1, source_target_pairs={{0,4},{2,6},{4,8},{5,1},{6,10},{7,3},{8,12},{9,5},{10,14},{11,7},{... | collective-permute-start | bytes 3145736 | tf_op jit(solution)/shard_map/ppermute | solution.py:23
  40.6 14.6 %collective-permute-start.5 = (f32[16]{0:T(128)S(1)}, f32[16]{0:T(128)S(1)}, u32[]{:S(2)}, u32[]{:S(2)}) collective-permute-start(f32[16]{0:T(128)S(1)} %slice_reduce_fusion.1), channel_id=1, source_target_pairs={{1,5},{3,7},{4,0},{5,9},{6,2},{7,11},{8,4},{9,13},{10,6},{11,15},{... | collective-permute-start | bytes 200 | tf_op jit(solution)/shard_map/ppermute | solution.py:23
  44.6 19.0 %collective-permute-start = (f32[16]{0:T(128)S(1)}, f32[16]{0:T(128)S(1)}, u32[]{:S(2)}, u32[]{:S(2)}) collective-permute-start(f32[16]{0:T(128)S(1)} %slice_reduce_fusion.1), channel_id=1, source_target_pairs={{0,4},{2,6},{4,8},{5,1},{6,10},{7,3},{8,12},{9,5},{10,14},{11,7},{... | collective-permute-start | bytes 200 | tf_op jit(solution)/shard_map/ppermute | solution.py:23
  63.8 15.8 %collective-permute-start.3 = (f32[16,128,128]{2,1,0:T(8,128)S(1)}, f32[16,128,128]{2,1,0:T(8,128)S(1)}, u32[]{:S(2)}, u32[]{:S(2)}) collective-permute-start(f32[16,128,128]{2,1,0:T(8,128)S(1)} %multiply_add_fusion.3), channel_id=1, source_target_pairs={{0,8},{2,10},{4,12},{6,14},{8,16},{9,1},{10,18},{11,3},{12,20},{13... | collective-permute-start | bytes 3145736 | tf_op jit(solution)/shard_map/ppermute | solution.py:23
  79.8 26.2 %collective-permute-start.4 = (f32[16,128,128]{2,1,0:T(8,128)S(1)}, f32[16,128,128]{2,1,0:T(8,128)S(1)}, u32[]{:S(2)}, u32[]{:S(2)}) collective-permute-start(f32[16,128,128]{2,1,0:T(8,128)S(1)} %multiply_add_fusion.2), channel_id=1, source_target_pairs={{0,16},{2,18},{4,20},{6,22},{8,24},{10,26},{12,28},{14,30},{17,1},... | collective-permute-start | bytes 3145736 | tf_op jit(solution)/shard_map/ppermute | solution.py:23
  81.1 24.9 %collective-permute-start.1 = (f32[16]{0:T(128)S(1)}, f32[16]{0:T(128)S(1)}, u32[]{:S(2)}, u32[]{:S(2)}) collective-permute-start(f32[16]{0:T(128)S(1)} %get-tuple-element.42), channel_id=1, source_target_pairs={{0,8},{2,10},{4,12},{6,14},{8,16},{9,1},{10,18},{11,3},{12,20},{13... | collective-permute-start | bytes 200 | tf_op jit(solution)/shard_map/ppermute | solution.py:23
  106.3 27.3 %collective-permute-start.7 = (f32[16,128,128]{2,1,0:T(8,128)S(1)}, f32[16,128,128]{2,1,0:T(8,128)S(1)}, u32[]{:S(2)}, u32[]{:S(2)}) collective-permute-start(f32[16,128,128]{2,1,0:T(8,128)S(1)} %get-tuple-element.9), channel_id=1, source_target_pairs={{1,5},{3,7},{4,0},{5,9},{6,2},{7,11},{8,4},{9,13},{10,6},{11,15},{... | collective-permute-start | bytes 3145736 | tf_op jit(solution)/shard_map/ppermute | solution.py:23
  133.7 15.8 %collective-permute-start.8 = (f32[16,128,128]{2,1,0:T(8,128)S(1)}, f32[16,128,128]{2,1,0:T(8,128)S(1)}, u32[]{:S(2)}, u32[]{:S(2)}) collective-permute-start(f32[16,128,128]{2,1,0:T(8,128)S(1)} %multiply_add_fusion.1), channel_id=1, source_target_pairs={{1,9},{3,11},{5,13},{7,15},{8,0},{9,17},{10,2},{11,19},{12,4},{13,... | collective-permute-start | bytes 3145736 | tf_op jit(solution)/shard_map/ppermute | solution.py:23
  149.5 3.7 copy-start.16
  150.9 24.6 %collective-permute-start.9 = (f32[16,128,128]{2,1,0:T(8,128)}, f32[16,128,128]{2,1,0:T(8,128)}, u32[]{:S(2)}, u32[]{:S(2)}) collective-permute-start(f32[16,128,128]{2,1,0:T(8,128)} %multiply_add_fusion), channel_id=1, source_target_pairs={{1,17},{3,19},{5,21},{7,23},{9,25},{11,27},{13,29},{15,31},{16,0},... | collective-permute-start | bytes 3145736 | tf_op jit(solution)/shard_map/ppermute | solution.py:23
  159.5 9.3 %copy-start.2 = (bf16[16,512,512]{2,1,0:T(8,128)(2,1)}, bf16[16,512,512]{2,1,0:T(8,128)(2,1)S(1)}, u32[]{:S(2)}) copy-start(bf16[16,512,512]{2,1,0:T(8,128)(2,1)S(1)} %multiply_convert_fusion) | copy-start | bytes 25165828
  159.5 15.9 %collective-permute-start.6 = (f32[16]{0:T(128)S(1)}, f32[16]{0:T(128)S(1)}, u32[]{:S(2)}, u32[]{:S(2)}) collective-permute-start(f32[16]{0:T(128)S(1)} %get-tuple-element.29), channel_id=1, source_target_pairs={{1,9},{3,11},{5,13},{7,15},{8,0},{9,17},{10,2},{11,19},{12,4},{13,... | collective-permute-start | bytes 200 | tf_op jit(solution)/shard_map/ppermute | solution.py:23
  168.8 9.5 %copy-start.4 = (bf16[1,512,2048]{1,2,0:T(8,128)(2,1)S(1)}, bf16[1,512,2048]{1,2,0:T(8,128)(2,1)}, u32[]{:S(2)}) copy-start(bf16[1,512,2048]{1,2,0:T(8,128)(2,1)} %copy.90) | copy-start | bytes 6291460
  168.8 9.5 %copy-start.12 = (f32[16,512,128]{1,2,0:T(8,128)S(1)}, f32[16,512,128]{1,2,0:T(8,128)}, u32[]{:S(2)}) copy-start(f32[16,512,128]{1,2,0:T(8,128)} %fusion.25) | copy-start | bytes 12582916
  178.3 2.1 copy-start.14
  178.3 2.1 copy-start.17
  188.9 6.8 %copy-start.10 = (bf16[64,8,16,128]{3,2,1,0:T(8,128)(2,1)S(1)}, bf16[64,8,16,128]{3,2,1,0:T(8,128)(2,1)}, u32[]{:S(2)}) copy-start(bf16[64,8,16,128]{3,2,1,0:T(8,128)(2,1)} %copy-done.9) | copy-start | bytes 6291460
  195.7 6.9 %copy-start.5 = (bf16[1,512,2048]{1,2,0:T(8,128)(2,1)S(1)}, bf16[1,512,2048]{1,2,0:T(8,128)(2,1)}, u32[]{:S(2)}) copy-start(bf16[1,512,2048]{1,2,0:T(8,128)(2,1)} %copy.90) | copy-start | bytes 6291460
  202.6 3.2 copy-start.7
  205.8 4.8 %copy-start.15 = (f32[16,128,128]{2,1,0:T(8,128)S(1)}, f32[16,128,128]{2,1,0:T(8,128)}, u32[]{:S(2)}) copy-start(f32[16,128,128]{2,1,0:T(8,128)} %copy-done.14) | copy-start | bytes 3145732
  216.2 4.1 %copy-start.11 = (bf16[64,8,16,128]{3,2,1,0:T(8,128)(2,1)S(1)}, bf16[64,8,16,128]{3,2,1,0:T(8,128)(2,1)}, u32[]{:S(2)}) copy-start(bf16[64,8,16,128]{3,2,1,0:T(8,128)(2,1)} %copy-done.9) | copy-start | bytes 6291460
  216.2 4.1 %copy-start.13 = (f32[16,128,128]{2,1,0:T(8,128)S(1)}, f32[16,128,128]{2,1,0:T(8,128)}, u32[]{:S(2)}) copy-start(f32[16,128,128]{2,1,0:T(8,128)} %get-tuple-element.10) | copy-start | bytes 3145732
  226.2 4.1 %copy-start.8 = (bf16[1,512,2048]{1,2,0:T(8,128)(2,1)S(1)}, bf16[1,512,2048]{1,2,0:T(8,128)(2,1)}, u32[]{:S(2)}) copy-start(bf16[1,512,2048]{1,2,0:T(8,128)(2,1)} %copy.89) | copy-start | bytes 6291460
  230.3 146.8 %copy-start.1 = (f32[1,512,16]{1,2,0:T(8,128)S(1)}, f32[1,512,16]{1,2,0:T(8,128)}, u32[]{:S(2)}) copy-start(f32[1,512,16]{1,2,0:T(8,128)} %param.13) | copy-start | bytes 98308
Sparse Core Ops, SparseCore 0:
  189.0 188.0 reduce-scatter.1

commit v2 on v0

--- a/solution.py
+++ b/solution.py
@@ -35,6 +35,17 @@
     return (earlier[0] + later[0], jnp.exp(later[0])[:, None, None] * earlier[1] + later[1])
 
 
+def pack_state(total, state):
+    slab = jnp.broadcast_to(total[:, None, None], (state.shape[0], 8, state.shape[2]))
+    return jnp.concatenate([state, slab], axis=1)
+
+
+def packed_join(earlier, later):
+    rows = earlier.shape[1] - 8
+    joined = chain_join((earlier[:, rows, 0], earlier[:, :rows]), (later[:, rows, 0], later[:, :rows]))
+    return pack_state(*joined)
+
+
 def on_device(query, keys, values, upstream, out_weight, log_decay, signs, magnitude):
     tokens = query.shape[1]
     width = query.shape[2]
@@ -58,7 +69,7 @@
     state_end = jnp.einsum(
         "shd,she->hde", key_f32 * remain, value_f32, precision=lax.Precision.HIGHEST
     )
-    state_in = carried_in((total, state_end), "ctx", chain_join, False)[1]
+    state_in = carried_in(pack_state(total, state_end), "ctx", packed_join, False)[:, :HD]
     state_end, upstream, query_heads = lax.optimization_barrier((state_end, upstream, query_heads))
 
     advantage = (2 * signs[0] - 1).astype(jnp.float32) * magnitude[0]
@@ -86,7 +97,7 @@
     )
     partial, back_end = lax.optimization_barrier((partial, back_end))
     grad_weight = lax.psum_scatter(partial, ("ctx", "dp"), scatter_dimension=0, tiled=True)
-    back_in = carried_in((total, back_end), "ctx", chain_join, True)[1]
+    back_in = carried_in(pack_state(total, back_end), "ctx", packed_join, True)[:, :HD]
 
     dscores = jnp.einsum(
         "thd,shd->hts", dout_heads, value_heads, preferred_element_type=jnp.float32

time: 383 us -> 378 us (0.987); the launches traced: 375 us -> 377 us
  waiting for transfers between devices: 215 us -> 232 us
  starting transfers between devices: 28.6 us -> 19.2 us
  matrix products: 77.8 us -> 69.7 us
    ppermute x10 -> x6, waiting for transfers between devices: 95.8 us -> 123 us  [carried_in(): lax.ppermute(part, axis, pairs)]
    reduce_scatter x1, waiting for transfers between devices: 119 us -> 109 us  [on_device(): lax.psum_scatter(partial, ('ctx', 'dp'), scatter_dimension=0, tiled=True)]
    ppermute x10 -> x6, starting transfers between devices: 28.5 us -> 19.2 us  [carried_in(): lax.ppermute(part, axis, pairs)]
    dot_general x1, matrix products: 9.89 us -> 5.8 us  [on_device(): lax.dot_general(weighted, out_weight, (((1,), (1,)), ((), ())), preferred...]
    unnamed x67 -> x71, local copies, waits for them, and re-layouts: 18.3 us -> 19.1 us
  transfers between devices with their start and end apart: 11 -> 7, of which waited for: 7 -> 7; matrix products, arithmetic and copies ran while one was open for 26% -> 22% of each run, Pallas kernels for 0% -> 0%
where the time goes in v2:
time: 378 us; the launch traced here: 377 us
  waiting for transfers between devices  232 us (61%)
  matrix products  69.7 us (18%)
  local copies, waits for them, and re-layouts  28.4 us (8%)
  starting transfers between devices  19.2 us (5%)
  between operations  14.5 us (4%)
  other arithmetic  13.3 us (4%)
    ppermute x6, waiting for transfers between devices, carried_in(): lax.ppermute(part, axis, pairs)  123 us
    reduce_scatter x1, waiting for transfers between devices, on_device(): lax.psum_scatter(partial, ('ctx', 'dp'), scatter_dimension=0, tiled=True)  109 us
    ppermute x6, starting transfers between devices, carried_in(): lax.ppermute(part, axis, pairs)  19.2 us
    unnamed x71, local copies, waits for them, and re-layouts  19.1 us
    dot_general x1, matrix products, on_device(): lax.dot_general(attn, weighted, (((0,), (0,)), ((), ())), preferred_eleme...  8.28 us
    dot_general x1, matrix products, on_device(): jnp.einsum('thd,shd->hts', query_heads, key_heads, preferred_element_type...  7.9 us
  transfers between devices with their start and end apart: 7, of which 7 were waited for; matrix products, arithmetic and copies ran while one was open for 22% of the time, Pallas kernels for 0%

profile of v2, /device:TPU:11, one launch (start us, length us, event | category | flops | bytes accessed | tf_op | source)
XLA Modules:
  0.0 377.3 jit_solution(1757835600623744518)
XLA Ops:
  7.2 0.7 copy-done
  7.9 1.1 reduce-window.6
  9.6 2.9 copy.94
  12.5 3.0 copy.98
  15.5 2.8 fusion.14
  18.6 3.3 collective-permute-start
  21.9 0.6 copy.99
  22.7 23.3 %collective-permute-done = f32[16,136,128]{2,1,0:T(8,128)S(1)} collective-permute-done((f32[16,136,128]{2,1,0:T(8,128)S(1)}, f32[16,136,128]{2,1,0:T(8,128)S(1)}, u32[]{:S(2)}, u32[]{:S(2)}) %collective-permute-start) | collective-permute-done | bytes 1114144 | tf_op jit(solution)/shard_map/ppermute | solution.py:19
  46.6 3.5 collective-permute-start.1
  50.1 7.9 %multiply_convert_fusion = bf16[16,512,512]{2,1,0:T(8,128)(2,1)} fusion(bf16[512,16,128]{0,2,1:T(8,128)(2,1)S(1)} %bitcast.115, f32[16,512]{1,0:T(8,128)S(1)} %get-tuple-element.36, pred[512,512]{1,0:T(8,128)(4,1)S(1)} %iota_compare_fusion, bf16[512,16,128]{2,1,0:T(8,128)(2,1)S(1)} %bitcast.111), kind=kOutput, calls=%fused_computation | convolution fusion | flops 1098907648 | bytes 12877824 | tf_op jit(solution)/shard_map/thd,shd->hts/dot_general | solution.py:88
  58.0 15.3 %collective-permute-done.1 = f32[16,136,128]{2,1,0:T(8,128)S(1)} collective-permute-done((f32[16,136,128]{2,1,0:T(8,128)S(1)}, f32[16,136,128]{2,1,0:T(8,128)S(1)}, u32[]{:S(2)}, u32[]{:S(2)}) %collective-permute-start.1) | collective-permute-done | bytes 1114144 | tf_op jit(solution)/shard_map/ppermute | solution.py:19
  73.8 0.5 copy-done.20
  74.3 5.2 %collective-permute-start.2 = (f32[16,136,128]{2,1,0:T(8,128)S(1)}, f32[16,136,128]{2,1,0:T(8,128)}, u32[]{:S(2)}, u32[]{:S(2)}) collective-permute-start(f32[16,136,128]{2,1,0:T(8,128)S(1)} %pad_maximum_fusion.3), channel_id=1, source_target_pairs={{0,16},{4,20},{8,24},{12,28},{1,17},{5,21},{9,25},{13,29},{2,18},{... | collective-permute-start | bytes 3342344 | tf_op jit(solution)/shard_map/ppermute | solution.py:19
  79.5 5.8 %convolution_convert_fusion = bf16[512,2048]{1,0:T(8,128)(2,1)} fusion(bf16[2048,2048]{1,0:T(8,128)(2,1)S(1)} %bitcast.133, bf16[1,512,2048]{2,1,0:T(8,128)(2,1)S(1)} %copy-done.27, f32[512]{0:T(512)S(1)} %bitcast.130), kind=kOutput, calls=%fused_computation.26 | convolution fusion | flops 4299161600 | bytes 12584960 | tf_op jit(solution)/shard_map/dot_general | solution.py:77
  85.3 2.9 copy.82
  88.2 2.9 copy.95
  91.1 4.9 %fusion.11 = f32[16,128,128]{2,1,0:T(8,128)} fusion(bf16[512,16,128]{0,2,1:T(8,128)(2,1)S(1)} %bitcast.107, bf16[512,16,128]{0,2,1:T(8,128)(2,1)} %copy.82, f32[512,16]{0,1:T(8,128)S(1)} %get-tuple-element.32), kind=kOutput, calls=%fused_computation.20 | convolution fusion | flops 1612709888 | bytes 5275648 | tf_op jit(solution)/shard_map/thd,the->hde/dot_general | solution.py:82
  96.0 6.4 %fusion.28 = f32[16,512,128]{1,2,0:T(8,128)S(1)} fusion(bf16[16,512,512]{2,1,0:T(8,128)(2,1)} %multiply_convert_fusion, bf16[512,16,128]{2,1,0:T(8,128)(2,1)S(1)} %bitcast.119), kind=kOutput, calls=%fused_computation.38 | convolution fusion | flops 1073741824 | bytes 14680064 | tf_op jit(solution)/shard_map/hts,shd->thd/dot_general | solution.py:90
  102.4 24.1 %collective-permute-done.2 = f32[16,136,128]{2,1,0:T(8,128)} collective-permute-done((f32[16,136,128]{2,1,0:T(8,128)S(1)}, f32[16,136,128]{2,1,0:T(8,128)}, u32[]{:S(2)}, u32[]{:S(2)}) %collective-permute-start.2) | collective-permute-done | bytes 1114144 | tf_op jit(solution)/shard_map/ppermute | solution.py:19
  126.5 1.6 fusion.34
  128.2 0.3 copy-done.13
  128.5 2.1 fusion.8
  130.5 8.3 %fusion.18 = f32[2048,2048]{1,0:T(8,128)} fusion(bf16[512,2048]{0,1:T(8,128)(2,1)S(1)} %bitcast.127, bf16[1,512,2048]{2,1,0:T(8,128)(2,1)S(1)} %copy-done.28, f32[512]{0:T(512)S(1)} %bitcast.131), kind=kOutput, calls=%fused_computation.28 | convolution fusion | flops 4298113024 | bytes 20973568 | tf_op jit(solution)/shard_map/dot_general | solution.py:95
  138.8 1.4 pad_maximum_fusion
  140.2 3.1 collective-permute-start.3
  143.3 35.0 %collective-permute-done.3 = f32[16,136,128]{2,1,0:T(8,128)S(1)} collective-permute-done((f32[16,136,128]{2,1,0:T(8,128)S(1)}, f32[16,136,128]{2,1,0:T(8,128)S(1)}, u32[]{:S(2)}, u32[]{:S(2)}) %collective-permute-start.3) | collective-permute-done | bytes 1114144 | tf_op jit(solution)/shard_map/ppermute | solution.py:19
  178.8 1.0 copy-done.16
  179.8 1.1 pad_maximum_fusion.4
  180.9 2.6 collective-permute-start.4
  183.5 7.0 %multiply_convert_fusion.1 = bf16[16,512,512]{2,1,0:T(8,128)(2,1)S(1)} fusion(bf16[512,16,128]{0,2,1:T(8,128)(2,1)S(1)} %bitcast.108, f32[16,512]{1,0:T(8,128)S(1)} %get-tuple-element.36, pred[512,512]{1,0:T(8,128)(4,1)S(1)} %copy-done.24, bf16[512,16,128]{2,1,0:T(8,128)(2,1)S(1)} %bitcast.120), kind=kOutput, calls=%fused_computation.1 | convolution fusion | flops 1098907648 | bytes 12877824 | tf_op jit(solution)/shard_map/thd,shd->hts/dot_general | solution.py:102
  190.4 4.7 %fusion.39 = f32[16,512,128]{1,2,0:T(8,128)} fusion(bf16[16,512,512]{2,1,0:T(8,128)(2,1)S(1)} %multiply_convert_fusion.1, bf16[512,16,128]{0,2,1:T(8,128)(2,1)S(1)} %bitcast.116), kind=kOutput, calls=%fused_computation.78 | convolution fusion | flops 1073741824 | bytes 14680064 | tf_op jit(solution)/shard_map/hts,shd->thd/dot_general | solution.py:106
  195.2 14.2 %collective-permute-done.4 = f32[16,136,128]{2,1,0:T(8,128)} collective-permute-done((f32[16,136,128]{2,1,0:T(8,128)}, f32[16,136,128]{2,1,0:T(8,128)}, u32[]{:S(2)}, u32[]{:S(2)}) %collective-permute-start.4) | collective-permute-done | bytes 1114144 | tf_op jit(solution)/shard_map/ppermute | solution.py:19
  209.4 1.1 exponential_reduce_fusion.1
  210.5 1.9 multiply_add_fusion
  212.5 1.1 pad_maximum_fusion.5
  213.6 1.5 collective-permute-start.5
  215.2 3.6 fusion.25
  218.8 3.2 fusion.40
  222.0 3.5 fusion.10
  225.5 4.1 %copy.89 = bf16[1,512,2048]{2,1,0:T(8,128)(2,1)} copy(bf16[1,512,2048]{1,2,0:T(8,128)(2,1)} %bitcast.122) | data formatting | bytes 4194304
  229.5 11.4 %collective-permute-done.5 = f32[16,136,128]{2,1,0:T(8,128)} collective-permute-done((f32[16,136,128]{2,1,0:T(8,128)}, f32[16,136,128]{2,1,0:T(8,128)}, u32[]{:S(2)}, u32[]{:S(2)}) %collective-permute-start.5) | collective-permute-done | bytes 1114144 | tf_op jit(solution)/shard_map/ppermute | solution.py:19
  240.9 2.3 fusion.33
  243.2 0.9 copy-done.2
  244.1 3.9 %fusion.6 = bf16[512,16,128]{0,2,1:T(8,128)(2,1)} fusion(f32[16,128,512]{2,1,0:T(8,128)S(1)} %copy-done.2, f32[16,128,128]{2,1,0:T(8,128)S(1)} %fusion.33, f32[512,16]{0,1:T(8,128)S(1)} %get-tuple-element.30, bf16[512,16,128]{2,1,0:T(8,128)(2,1)S(1)} %bitcast.121), kind=kOutput, calls=%fused_computation.13 | convolution fusion | flops 1613758464 | bytes 9469952 | tf_op jit(solution)/shard_map/hde,she->shd/dot_general | solution.py:112
  248.1 4.1 %copy.90 = bf16[1,512,2048]{2,1,0:T(8,128)(2,1)} copy(bf16[1,512,2048]{1,2,0:T(8,128)(2,1)} %bitcast.124) | data formatting | bytes 4194304
  252.1 5.6 %fusion.4 = bf16[512,16,128]{0,2,1:T(8,128)(2,1)} fusion(f32[16,128,512]{2,1,0:T(8,128)} %fusion.40, f32[16,128,128]{2,1,0:T(8,128)S(1)} %fusion.33, bf16[512,16,128]{0,2,1:T(8,128)(2,1)S(1)} %bitcast.117, f32[512,16]{0,1:T(8,128)S(1)} %get-tuple-element.30), kind=kOutput, calls=%fused_computation.10 | convolution fusion | flops 1613758464 | bytes 9469952 | tf_op jit(solution)/shard_map/hde,shd->she/dot_general | solution.py:115
  257.7 3.9 %copy.91 = bf16[1,512,2048]{2,1,0:T(8,128)(2,1)} copy(bf16[1,512,2048]{1,2,0:T(8,128)(2,1)} %bitcast.123) | data formatting | bytes 4194304
  261.7 108.8 %reduce-scatter.2.cloned.1.call-done = f32[64,2048]{1,0:T(8,128)} async-done(((f32[2048,2048]{1,0:T(8,128)}), f32[64,2048]{1,0:T(8,128)}) %reduce-scatter.2.cloned.1.call-update) | async-done | bytes 524304 | tf_op jit(solution)/shard_map/reduce_scatter | solution.py:99
  (91 shorter events, 2.6 us)
Async XLA Ops:
  7.2 0.8 copy-start
  7.2 363.3 %reduce-scatter.2.cloned.1.call-start = ((), (), s32[]{:S(2)}) async-start(), calls=%async_computation.1 | async-start | bytes 17301504 | tf_op jit(solution)/shard_map/reduce_scatter | solution.py:99
  12.5 3.0 copy-start.5
  15.5 2.9 copy-start.9
  18.4 3.5 copy-start.22
  18.6 27.5 %collective-permute-start = (f32[16,136,128]{2,1,0:T(8,128)S(1)}, f32[16,136,128]{2,1,0:T(8,128)S(1)}, u32[]{:S(2)}, u32[]{:S(2)}) collective-permute-start(f32[16,136,128]{2,1,0:T(8,128)S(1)} %pad_maximum_fusion.1), channel_id=1, source_target_pairs={{0,4},{4,8},{8,12},{12,16},{16,20},{20,24},{24,28},{1,5},{5,9},{9,... | collective-permute-start | bytes 3342344 | tf_op jit(solution)/shard_map/ppermute | solution.py:19
  21.9 0.7 copy-start.25
  21.9 0.7 copy-start.26
  22.5 62.8 %copy-start.3 = (bf16[64,8,16,128]{3,2,1,0:T(8,128)(2,1)}, bf16[64,8,16,128]{3,2,1,0:T(8,128)(2,1)S(1)}, u32[]{:S(2)}) copy-start(bf16[64,8,16,128]{3,2,1,0:T(8,128)(2,1)S(1)} %copy.99) | copy-start | bytes 6291460
  22.7 27.4 %copy-start.23 = (pred[512,512]{1,0:T(8,128)(4,1)}, pred[512,512]{1,0:T(8,128)(4,1)S(1)}, u32[]{:S(2)}) copy-start(pred[512,512]{1,0:T(8,128)(4,1)S(1)} %iota_compare_fusion) | copy-start | bytes 786436
  22.7 27.4 %copy-start.6 = (bf16[1,512,2048]{1,2,0:T(8,128)(2,1)S(1)}, bf16[1,512,2048]{1,2,0:T(8,128)(2,1)}, u32[]{:S(2)}) copy-start(bf16[1,512,2048]{1,2,0:T(8,128)(2,1)} %copy-done.5) | copy-start | bytes 6291460
  46.0 27.2 %copy-start.18 = (f32[16,136,128]{2,1,0:T(8,128)}, f32[16,136,128]{2,1,0:T(8,128)S(1)}, u32[]{:S(2)}) copy-start(f32[16,136,128]{2,1,0:T(8,128)S(1)} %collective-permute-done) | copy-start | bytes 3342340
  46.5 33.0 %slice-start.2 = ((s8[8388608]{0:T(1024)(128)(4,1)}), s8[4194304]{0:T(1024)(128)(4,1)S(1)}, s32[]{:S(2)}) async-start(s8[8388608]{0:T(1024)(128)(4,1)} %bitcast.132), calls=%async_computation.4 | async-start | bytes 8388608
  46.6 26.7 %collective-permute-start.1 = (f32[16,136,128]{2,1,0:T(8,128)S(1)}, f32[16,136,128]{2,1,0:T(8,128)S(1)}, u32[]{:S(2)}, u32[]{:S(2)}) collective-permute-start(f32[16,136,128]{2,1,0:T(8,128)S(1)} %pad_maximum_fusion.2), channel_id=1, source_target_pairs={{0,8},{4,12},{8,16},{12,20},{16,24},{20,28},{1,9},{5,13},{9,17},{1... | collective-permute-start | bytes 3342344 | tf_op jit(solution)/shard_map/ppermute | solution.py:19
  50.1 29.5 %slice-start.3 = ((s8[8388608]{0:T(1024)(128)(4,1)}), s8[4194304]{0:T(1024)(128)(4,1)S(1)}, s32[]{:S(2)}) async-start(s8[8388608]{0:T(1024)(128)(4,1)} %bitcast.132), calls=%async_computation.5 | async-start | bytes 8388608
  73.2 1.1 copy-start.20
  73.5 6.1 %copy-start.27 = (bf16[1,512,2048]{2,1,0:T(8,128)(2,1)S(1)}, bf16[1,512,2048]{2,1,0:T(8,128)(2,1)}, u32[]{:S(2)}) copy-start(bf16[1,512,2048]{2,1,0:T(8,128)(2,1)} %param.11) | copy-start | bytes 6291460
  74.3 52.2 %collective-permute-start.2 = (f32[16,136,128]{2,1,0:T(8,128)S(1)}, f32[16,136,128]{2,1,0:T(8,128)}, u32[]{:S(2)}, u32[]{:S(2)}) collective-permute-start(f32[16,136,128]{2,1,0:T(8,128)S(1)} %pad_maximum_fusion.3), channel_id=1, source_target_pairs={{0,16},{4,20},{8,24},{12,28},{1,17},{5,21},{9,25},{13,29},{2,18},{... | collective-permute-start | bytes 3342344 | tf_op jit(solution)/shard_map/ppermute | solution.py:19
  91.1 4.9 %copy-start.10 = (bf16[64,8,16,128]{3,2,1,0:T(8,128)(2,1)S(1)}, bf16[64,8,16,128]{3,2,1,0:T(8,128)(2,1)}, u32[]{:S(2)}) copy-start(bf16[64,8,16,128]{3,2,1,0:T(8,128)(2,1)} %copy-done.9) | copy-start | bytes 6291460
  96.0 30.6 %copy-start.19 = (f32[16,136,128]{2,1,0:T(8,128)S(1)}, f32[16,136,128]{2,1,0:T(8,128)}, u32[]{:S(2)}) copy-start(f32[16,136,128]{2,1,0:T(8,128)} %copy-done.18) | copy-start | bytes 3342340
  96.0 30.6 %copy-start.21 = (f32[16,136,128]{2,1,0:T(8,128)S(1)}, f32[16,136,128]{2,1,0:T(8,128)}, u32[]{:S(2)}) copy-start(f32[16,136,128]{2,1,0:T(8,128)} %copy-done.20) | copy-start | bytes 3342340
  126.5 1.9 copy-start.13
  128.4 2.1 copy-start.28
  138.8 39.7 %copy-start.15 = (f32[16,128,128]{2,1,0:T(8,128)S(1)}, f32[16,128,128]{2,1,0:T(8,128)}, u32[]{:S(2)}) copy-start(f32[16,128,128]{2,1,0:T(8,128)} %fusion.11) | copy-start | bytes 3145732
  140.2 38.1 %collective-permute-start.3 = (f32[16,136,128]{2,1,0:T(8,128)S(1)}, f32[16,136,128]{2,1,0:T(8,128)S(1)}, u32[]{:S(2)}, u32[]{:S(2)}) collective-permute-start(f32[16,136,128]{2,1,0:T(8,128)S(1)} %pad_maximum_fusion), channel_id=1, source_target_pairs={{4,0},{8,4},{12,8},{16,12},{20,16},{24,20},{28,24},{5,1},{9,5},{13... | collective-permute-start | bytes 3342344 | tf_op jit(solution)/shard_map/ppermute | solution.py:19
  178.3 2.6 copy-start.17
  178.5 4.9 %copy-start.11 = (bf16[64,8,16,128]{3,2,1,0:T(8,128)(2,1)S(1)}, bf16[64,8,16,128]{3,2,1,0:T(8,128)(2,1)}, u32[]{:S(2)}) copy-start(bf16[64,8,16,128]{3,2,1,0:T(8,128)(2,1)} %copy-done.9) | copy-start | bytes 6291460
  178.5 4.9 %copy-start.24 = (pred[512,512]{1,0:T(8,128)(4,1)S(1)}, pred[512,512]{1,0:T(8,128)(4,1)}, u32[]{:S(2)}) copy-start(pred[512,512]{1,0:T(8,128)(4,1)} %copy-done.23) | copy-start | bytes 786436
  178.7 1.1 copy-start.16
  180.9 9.6 %copy-start.7 = (bf16[1,512,2048]{1,2,0:T(8,128)(2,1)S(1)}, bf16[1,512,2048]{1,2,0:T(8,128)(2,1)}, u32[]{:S(2)}) copy-start(bf16[1,512,2048]{1,2,0:T(8,128)(2,1)} %copy-done.5) | copy-start | bytes 6291460
  180.9 28.6 %collective-permute-start.4 = (f32[16,136,128]{2,1,0:T(8,128)}, f32[16,136,128]{2,1,0:T(8,128)}, u32[]{:S(2)}, u32[]{:S(2)}) collective-permute-start(f32[16,136,128]{2,1,0:T(8,128)} %pad_maximum_fusion.4), channel_id=1, source_target_pairs={{8,0},{12,4},{16,8},{20,12},{24,16},{28,20},{9,1},{13,5},{17,9},{2... | collective-permute-start | bytes 3342344 | tf_op jit(solution)/shard_map/ppermute | solution.py:19
  210.5 4.7 %copy-start.4 = (bf16[64,8,16,128]{3,2,1,0:T(8,128)(2,1)S(1)}, bf16[64,8,16,128]{3,2,1,0:T(8,128)(2,1)}, u32[]{:S(2)}) copy-start(bf16[64,8,16,128]{3,2,1,0:T(8,128)(2,1)} %copy-done.3) | copy-start | bytes 6291460
  212.5 6.2 %slice-start = ((s8[8388608]{0:T(1024)(128)(4,1)}), s8[4194304]{0:T(1024)(128)(4,1)S(1)}, s32[]{:S(2)}) async-start(s8[8388608]{0:T(1024)(128)(4,1)} %bitcast.105), calls=%async_computation.2 | async-start | bytes 8388608
  213.6 5.1 %slice-start.1 = ((s8[8388608]{0:T(1024)(128)(4,1)}), s8[4194304]{0:T(1024)(128)(4,1)S(1)}, s32[]{:S(2)}) async-start(s8[8388608]{0:T(1024)(128)(4,1)} %bitcast.105), calls=%async_computation.3 | async-start | bytes 8388608
  213.6 27.3 %collective-permute-start.5 = (f32[16,136,128]{2,1,0:T(8,128)}, f32[16,136,128]{2,1,0:T(8,128)}, u32[]{:S(2)}, u32[]{:S(2)}) collective-permute-start(f32[16,136,128]{2,1,0:T(8,128)} %pad_maximum_fusion.5), channel_id=1, source_target_pairs={{16,0},{20,4},{24,8},{28,12},{17,1},{21,5},{25,9},{29,13},{18,2},{... | collective-permute-start | bytes 3342344 | tf_op jit(solution)/shard_map/ppermute | solution.py:19
  218.8 3.2 copy-start.14
  225.5 17.8 %copy-start.12 = (bf16[64,8,16,128]{3,2,1,0:T(8,128)(2,1)S(1)}, bf16[64,8,16,128]{3,2,1,0:T(8,128)(2,1)}, u32[]{:S(2)}) copy-start(bf16[64,8,16,128]{3,2,1,0:T(8,128)(2,1)} %copy-done.9) | copy-start | bytes 6291460
  240.9 3.2 copy-start.2
  248.1 4.1 %copy-start.8 = (bf16[1,512,2048]{1,2,0:T(8,128)(2,1)S(1)}, bf16[1,512,2048]{1,2,0:T(8,128)(2,1)}, u32[]{:S(2)}) copy-start(bf16[1,512,2048]{1,2,0:T(8,128)(2,1)} %copy-done.5) | copy-start | bytes 6291460
  257.7 112.7 %copy-start.1 = (f32[1,512,16]{1,2,0:T(8,128)S(1)}, f32[1,512,16]{1,2,0:T(8,128)}, u32[]{:S(2)}) copy-start(f32[1,512,16]{1,2,0:T(8,128)} %param.13) | copy-start | bytes 98308
Sparse Core Ops, SparseCore 0:
  139.0 231.4 reduce-scatter.1

commit v3 on v2

--- a/solution.py
+++ b/solution.py
@@ -8,21 +8,29 @@
 BLOCK = 512
 
 
-def carried_in(value, axis, join, backward):
+def carried_in(value, axis, join, backward, radix):
     count = lax.axis_size(axis)
-    step = -1 if backward else 1
+    sign = -1 if backward else 1
     partial = value
     gathered = None
-    distance = 1
-    while distance < count:
-        pairs = [(i, i + step * distance) for i in range(count) if 0 <= i + step * distance < count]
-        arrived = jax.tree.map(lambda part: lax.ppermute(part, axis, pairs), partial)
+    unit = 1
+    while unit < count:
+        arrivals = []
+        for multiple in range(1, radix):
+            distance = sign * multiple * unit
+            if multiple * unit >= count:
+                break
+            pairs = [(i, i + distance) for i in range(count) if 0 <= i + distance < count]
+            arrivals.append(lax.ppermute(partial, axis, pairs))
+        arrived = arrivals[-1]
+        for nearer in reversed(arrivals[:-1]):
+            arrived = join(arrived, nearer)
         gathered = arrived if gathered is None else join(arrived, gathered)
-        if distance * 2 < count:
+        if unit * radix < count:
             partial = join(arrived, partial)
-        distance *= 2
+        unit *= radix
     if gathered is None:
-        gathered = jax.tree.map(jnp.zeros_like, value)
+        gathered = jnp.zeros_like(value)
     return gathered
 
 
@@ -69,7 +77,7 @@
     state_end = jnp.einsum(
         "shd,she->hde", key_f32 * remain, value_f32, precision=lax.Precision.HIGHEST
     )
-    state_in = carried_in(pack_state(total, state_end), "ctx", packed_join, False)[:, :HD]
+    state_in = carried_in(pack_state(total, state_end), "ctx", packed_join, False, 4)[:, :HD]
     state_end, upstream, query_heads = lax.optimization_barrier((state_end, upstream, query_heads))
 
     advantage = (2 * signs[0] - 1).astype(jnp.float32) * magnitude[0]
@@ -97,7 +105,7 @@
     )
     partial, back_end = lax.optimization_barrier((partial, back_end))
     grad_weight = lax.psum_scatter(partial, ("ctx", "dp"), scatter_dimension=0, tiled=True)
-    back_in = carried_in(pack_state(total, back_end), "ctx", packed_join, True)[:, :HD]
+    back_in = carried_in(pack_state(total, back_end), "ctx", packed_join, True, 2)[:, :HD]
 
     dscores = jnp.einsum(
         "thd,shd->hts", dout_heads, value_heads, preferred_element_type=jnp.float32

time: 378 us -> 417 us (1.10)
  waiting for transfers between devices: 232 us -> 259 us
  starting transfers between devices: 19.2 us -> 27.6 us
  matrix products: 69.7 us -> 76.4 us
    ppermute x6 -> x7, waiting for transfers between devices: 123 us -> 139 us  [carried_in(): arrivals.append(lax.ppermute(partial, axis, pairs))]
    reduce_scatter x1, waiting for transfers between devices: 109 us -> 120 us  [on_device(): lax.psum_scatter(partial, ('ctx', 'dp'), scatter_dimension=0, tiled=True)]
    ppermute x6 -> x7, starting transfers between devices: 19.2 us -> 27.6 us  [carried_in(): arrivals.append(lax.ppermute(partial, axis, pairs))]
    unnamed x71 -> x69, local copies, waits for them, and re-layouts: 19.1 us -> 19.5 us
  transfers between devices with their start and end apart: 7 -> 8, of which waited for: 7 -> 7; matrix products, arithmetic and copies ran while one was open for 22% -> 21% of each run, Pallas kernels for 0% -> 0%
where the time goes in v3:
time: 417 us
  waiting for transfers between devices  259 us (62%)
  matrix products  76.4 us (18%)
  local copies, waits for them, and re-layouts  28.7 us (7%)
  starting transfers between devices  27.6 us (7%)
  between operations  14.5 us (3%)
  other arithmetic  10.4 us (2%)
    ppermute x7, waiting for transfers between devices, carried_in(): arrivals.append(lax.ppermute(partial, axis, pairs))  139 us
    reduce_scatter x1, waiting for transfers between devices, on_device(): lax.psum_scatter(partial, ('ctx', 'dp'), scatter_dimension=0, tiled=True)  120 us
    ppermute x7, starting transfers between devices, carried_in(): arrivals.append(lax.ppermute(partial, axis, pairs))  27.6 us
    unnamed x69, local copies, waits for them, and re-layouts  19.5 us
  transfers between devices with their start and end apart: 8, of which 7 were waited for; matrix products, arithmetic and copies ran while one was open for 21% of the time, Pallas kernels for 0%

profile of v3, /device:TPU:11, one launch (start us, length us, event | category | flops | bytes accessed | tf_op | source)
XLA Modules:
  0.0 416.6 jit_solution(10479782607697616404)
XLA Ops:
  7.2 0.7 copy-done
  7.9 1.1 reduce-window.6
  9.6 2.9 copy.91
  12.5 3.0 copy.95
  15.5 2.8 fusion.14
  18.6 3.3 collective-permute-start.2
  21.9 3.2 collective-permute-start.1
  25.1 2.2 collective-permute-start
  27.5 0.6 copy.96
  28.2 1.1 copy-done.7
  29.3 7.8 %multiply_convert_fusion = bf16[16,512,512]{2,1,0:T(8,128)(2,1)} fusion(bf16[512,16,128]{0,2,1:T(8,128)(2,1)S(1)} %bitcast.112, f32[16,512]{1,0:T(8,128)S(1)} %get-tuple-element.38, pred[512,512]{1,0:T(8,128)(4,1)S(1)} %iota_compare_fusion, bf16[512,16,128]{2,1,0:T(8,128)(2,1)S(1)} %bitcast.108), kind=kOutput, calls=%fused_computation | convolution fusion | flops 1098907648 | bytes 12877824 | tf_op jit(solution)/shard_map/thd,shd->hts/dot_general | solution.py:96
  37.2 8.9 %collective-permute-done.2 = f32[16,136,128]{2,1,0:T(8,128)S(1)} collective-permute-done((f32[16,136,128]{2,1,0:T(8,128)S(1)}, f32[16,136,128]{2,1,0:T(8,128)S(1)}, u32[]{:S(2)}, u32[]{:S(2)}) %collective-permute-start.2) | collective-permute-done | bytes 1114144 | tf_op jit(solution)/shard_map/ppermute | solution.py:24
  46.0 23.8 %collective-permute-done.1 = f32[16,136,128]{2,1,0:T(8,128)S(1)} collective-permute-done((f32[16,136,128]{2,1,0:T(8,128)S(1)}, f32[16,136,128]{2,1,0:T(8,128)S(1)}, u32[]{:S(2)}, u32[]{:S(2)}) %collective-permute-start.1) | collective-permute-done | bytes 1114144 | tf_op jit(solution)/shard_map/ppermute | solution.py:24
  69.9 70.7 %collective-permute-done = f32[16,136,128]{2,1,0:T(8,128)S(1)} collective-permute-done((f32[16,136,128]{2,1,0:T(8,128)S(1)}, f32[16,136,128]{2,1,0:T(8,128)S(1)}, u32[]{:S(2)}, u32[]{:S(2)}) %collective-permute-start) | collective-permute-done | bytes 1114144 | tf_op jit(solution)/shard_map/ppermute | solution.py:24
  140.8 1.4 multiply_add_fusion.2
  142.3 1.1 pad_maximum_fusion.2
  143.4 2.3 collective-permute-start.3
  145.6 5.8 %convolution_convert_fusion = bf16[512,2048]{1,0:T(8,128)(2,1)} fusion(bf16[2048,2048]{1,0:T(8,128)(2,1)S(1)} %bitcast.129, bf16[1,512,2048]{2,1,0:T(8,128)(2,1)S(1)} %copy-done.26, f32[512]{0:T(512)S(1)} %bitcast.126), kind=kOutput, calls=%fused_computation.26 | convolution fusion | flops 4299161600 | bytes 12584960 | tf_op jit(solution)/shard_map/dot_general | solution.py:85
  151.4 2.8 copy.79
  154.2 2.9 copy.92
  157.1 3.9 fusion.11
  161.1 6.4 %fusion.28 = f32[16,512,128]{1,2,0:T(8,128)S(1)} fusion(bf16[16,512,512]{2,1,0:T(8,128)(2,1)} %multiply_convert_fusion, bf16[512,16,128]{2,1,0:T(8,128)(2,1)S(1)} %bitcast.116), kind=kOutput, calls=%fused_computation.38 | convolution fusion | flops 1073741824 | bytes 14680064 | tf_op jit(solution)/shard_map/hts,shd->thd/dot_general | solution.py:98
  167.5 3.7 fusion.8
  171.3 8.3 %fusion.18 = f32[2048,2048]{1,0:T(8,128)} fusion(bf16[512,2048]{0,1:T(8,128)(2,1)S(1)} %bitcast.124, bf16[1,512,2048]{2,1,0:T(8,128)(2,1)S(1)} %copy-done.27, f32[512]{0:T(512)S(1)} %bitcast.127), kind=kOutput, calls=%fused_computation.28 | convolution fusion | flops 4298113024 | bytes 20973568 | tf_op jit(solution)/shard_map/dot_general | solution.py:103
  179.7 7.2 %collective-permute-start.4 = (f32[16,136,128]{2,1,0:T(8,128)S(1)}, f32[16,136,128]{2,1,0:T(8,128)S(1)}, u32[]{:S(2)}, u32[]{:S(2)}) collective-permute-start(f32[16,136,128]{2,1,0:T(8,128)S(1)} %pad_maximum_fusion), channel_id=1, source_target_pairs={{4,0},{8,4},{12,8},{16,12},{20,16},{24,20},{28,24},{5,1},{9,5},{13... | collective-permute-start | bytes 3342344 | tf_op jit(solution)/shard_map/ppermute | solution.py:24
  186.9 7.9 %multiply_convert_fusion.1 = bf16[16,512,512]{2,1,0:T(8,128)(2,1)S(1)} fusion(bf16[512,16,128]{0,2,1:T(8,128)(2,1)S(1)} %bitcast.105, f32[16,512]{1,0:T(8,128)S(1)} %get-tuple-element.38, pred[512,512]{1,0:T(8,128)(4,1)} %copy-done.23, bf16[512,16,128]{2,1,0:T(8,128)(2,1)S(1)} %bitcast.117), kind=kOutput, calls=%fused_computation.1 | convolution fusion | flops 1098907648 | bytes 12877824 | tf_op jit(solution)/shard_map/thd,shd->hts/dot_general | solution.py:110
  194.8 17.3 %collective-permute-done.4 = f32[16,136,128]{2,1,0:T(8,128)S(1)} collective-permute-done((f32[16,136,128]{2,1,0:T(8,128)S(1)}, f32[16,136,128]{2,1,0:T(8,128)S(1)}, u32[]{:S(2)}, u32[]{:S(2)}) %collective-permute-start.4) | collective-permute-done | bytes 1114144 | tf_op jit(solution)/shard_map/ppermute | solution.py:24
  212.5 0.5 copy-done.20
  213.0 0.4 copy-done.16
  213.4 1.1 pad_maximum_fusion.3
  214.5 8.0 %collective-permute-start.5 = (f32[16,136,128]{2,1,0:T(8,128)}, f32[16,136,128]{2,1,0:T(8,128)S(1)}, u32[]{:S(2)}, u32[]{:S(2)}) collective-permute-start(f32[16,136,128]{2,1,0:T(8,128)} %pad_maximum_fusion.3), channel_id=1, source_target_pairs={{8,0},{12,4},{16,8},{20,12},{24,16},{28,20},{9,1},{13,5},{17,9},{2... | collective-permute-start | bytes 3342344 | tf_op jit(solution)/shard_map/ppermute | solution.py:24
  222.5 3.7 fusion.25
  226.2 8.3 %fusion.44 = f32[16,512,128]{1,2,0:T(8,128)} fusion(bf16[16,512,512]{2,1,0:T(8,128)(2,1)} %copy-done.2, bf16[512,16,128]{0,2,1:T(8,128)(2,1)S(1)} %bitcast.113), kind=kOutput, calls=%fused_computation.81 | convolution fusion | flops 1073741824 | bytes 14680064 | tf_op jit(solution)/shard_map/hts,shd->thd/dot_general | solution.py:114
  234.5 9.1 %collective-permute-done.5 = f32[16,136,128]{2,1,0:T(8,128)S(1)} collective-permute-done((f32[16,136,128]{2,1,0:T(8,128)}, f32[16,136,128]{2,1,0:T(8,128)S(1)}, u32[]{:S(2)}, u32[]{:S(2)}) %collective-permute-start.5) | collective-permute-done | bytes 1114144 | tf_op jit(solution)/shard_map/ppermute | solution.py:24
  243.6 1.1 exponential_reduce_fusion.1
  245.0 1.1 pad_maximum_fusion.4
  246.1 1.4 collective-permute-start.6
  247.6 3.3 fusion.45
  250.8 4.8 %fusion.10 = bf16[512,16,128]{0,2,1:T(8,128)(2,1)} fusion(f32[16,512,128]{1,2,0:T(8,128)S(1)} %copy-done.15, bf16[512,16,128]{0,2,1:T(8,128)(2,1)S(1)} %bitcast.107, f32[512,16]{0,1:T(8,128)S(1)} %get-tuple-element.37, f32[16,128,128]{2,1,0:T(8,128)S(1)} %copy-done.19, f32[16,136,128]{2,1,0:T(8,128)} %collective-permute-done.3, f32[16]{0:T(128)S(1)} %get-tuple-element.42), kind=kOutput, calls=%fused_computation.19 | convolution fusion | flops 1614282752 | bytes 10518592 | tf_op jit(solution)/shard_map/hde,the->thd/dot_general | solution.py:117
  255.6 4.1 copy.86
  259.7 9.5 %collective-permute-done.6 = f32[16,136,128]{2,1,0:T(8,128)} collective-permute-done((f32[16,136,128]{2,1,0:T(8,128)}, f32[16,136,128]{2,1,0:T(8,128)}, u32[]{:S(2)}, u32[]{:S(2)}) %collective-permute-start.6) | collective-permute-done | bytes 1114144 | tf_op jit(solution)/shard_map/ppermute | solution.py:24
  269.2 2.3 fusion.33
  271.6 0.9 copy-done.3
  272.5 3.9 fusion.6
  276.5 4.1 copy.87
  280.5 5.7 %fusion.4 = bf16[512,16,128]{0,2,1:T(8,128)(2,1)} fusion(f32[16,128,512]{2,1,0:T(8,128)} %fusion.45, f32[16,128,128]{2,1,0:T(8,128)S(1)} %fusion.33, bf16[512,16,128]{0,2,1:T(8,128)(2,1)S(1)} %bitcast.114, f32[512,16]{0,1:T(8,128)S(1)} %get-tuple-element.30), kind=kOutput, calls=%fused_computation.10 | convolution fusion | flops 1613758464 | bytes 9469952 | tf_op jit(solution)/shard_map/hde,shd->she/dot_general | solution.py:123
  286.2 3.9 copy.88
  290.1 119.6 %reduce-scatter.2.cloned.1.call-done = f32[64,2048]{1,0:T(8,128)} async-done(((f32[2048,2048]{1,0:T(8,128)}), f32[64,2048]{1,0:T(8,128)}) %reduce-scatter.2.cloned.1.call-update) | async-done | bytes 524304 | tf_op jit(solution)/shard_map/reduce_scatter | solution.py:107
  (85 shorter events, 2.2 us)
Async XLA Ops:
  7.2 0.8 copy-start
  7.2 402.6 %reduce-scatter.2.cloned.1.call-start = ((), (), s32[]{:S(2)}) async-start(), calls=%async_computation.1 | async-start | bytes 17301504 | tf_op jit(solution)/shard_map/reduce_scatter | solution.py:107
  12.5 3.0 copy-start.6
  15.5 2.9 copy-start.10
  18.4 9.0 %copy-start.22 = (bf16[1,512,2048]{2,1,0:T(8,128)(2,1)S(1)}, bf16[1,512,2048]{2,1,0:T(8,128)(2,1)}, u32[]{:S(2)}) copy-start(bf16[1,512,2048]{2,1,0:T(8,128)(2,1)} %param.8) | copy-start | bytes 6291460
  18.6 27.5 %collective-permute-start.2 = (f32[16,136,128]{2,1,0:T(8,128)S(1)}, f32[16,136,128]{2,1,0:T(8,128)S(1)}, u32[]{:S(2)}, u32[]{:S(2)}) collective-permute-start(f32[16,136,128]{2,1,0:T(8,128)S(1)} %pad_maximum_fusion.1), channel_id=1, source_target_pairs={{0,4},{4,8},{8,12},{12,16},{16,20},{20,24},{24,28},{1,5},{5,9},{9,... | collective-permute-start | bytes 3342344 | tf_op jit(solution)/shard_map/ppermute | solution.py:24
  21.9 48.0 %collective-permute-start.1 = (f32[16,136,128]{2,1,0:T(8,128)S(1)}, f32[16,136,128]{2,1,0:T(8,128)S(1)}, u32[]{:S(2)}, u32[]{:S(2)}) collective-permute-start(f32[16,136,128]{2,1,0:T(8,128)S(1)} %pad_maximum_fusion.1), channel_id=1, source_target_pairs={{0,8},{4,12},{8,16},{12,20},{16,24},{20,28},{1,9},{5,13},{9,17},{1... | collective-permute-start | bytes 3342344 | tf_op jit(solution)/shard_map/ppermute | solution.py:24
  25.1 115.5 %collective-permute-start = (f32[16,136,128]{2,1,0:T(8,128)S(1)}, f32[16,136,128]{2,1,0:T(8,128)S(1)}, u32[]{:S(2)}, u32[]{:S(2)}) collective-permute-start(f32[16,136,128]{2,1,0:T(8,128)S(1)} %pad_maximum_fusion.1), channel_id=1, source_target_pairs={{0,12},{4,16},{8,20},{12,24},{16,28},{1,13},{5,17},{9,21},{13,25},... | collective-permute-start | bytes 3342344 | tf_op jit(solution)/shard_map/ppermute | solution.py:24
  27.4 0.8 copy-start.23
  27.4 0.7 copy-start.24
  27.4 0.8 copy-start.25
  27.4 1.9 copy-start.7
  27.5 118.2 %slice-start.2 = ((s8[8388608]{0:T(1024)(128)(4,1)}), s8[4194304]{0:T(1024)(128)(4,1)S(1)}, s32[]{:S(2)}) async-start(s8[8388608]{0:T(1024)(128)(4,1)} %bitcast.128), calls=%async_computation.4 | async-start | bytes 8388608
  28.1 123.3 %copy-start.4 = (bf16[64,8,16,128]{3,2,1,0:T(8,128)(2,1)}, bf16[64,8,16,128]{3,2,1,0:T(8,128)(2,1)S(1)}, u32[]{:S(2)}) copy-start(bf16[64,8,16,128]{3,2,1,0:T(8,128)(2,1)S(1)} %copy.96) | copy-start | bytes 6291460
  29.3 116.3 %slice-start.3 = ((s8[8388608]{0:T(1024)(128)(4,1)}), s8[4194304]{0:T(1024)(128)(4,1)S(1)}, s32[]{:S(2)}) async-start(s8[8388608]{0:T(1024)(128)(4,1)} %bitcast.128), calls=%async_computation.5 | async-start | bytes 8388608
  142.2 3.4 copy-start.26
  143.4 24.2 %collective-permute-start.3 = (f32[16,136,128]{2,1,0:T(8,128)}, f32[16,136,128]{2,1,0:T(8,128)}, u32[]{:S(2)}, u32[]{:S(2)}) collective-permute-start(f32[16,136,128]{2,1,0:T(8,128)} %pad_maximum_fusion.2), channel_id=1, source_target_pairs={{0,16},{4,20},{8,24},{12,28},{1,17},{5,21},{9,25},{13,29},{2,18},{... | collective-permute-start | bytes 3342344 | tf_op jit(solution)/shard_map/ppermute | solution.py:24
  157.1 4.0 copy-start.11
  161.1 6.5 %copy-start.14 = (bf16[512,16,128]{0,2,1:T(8,128)(2,1)S(1)}, bf16[512,16,128]{0,2,1:T(8,128)(2,1)}, u32[]{:S(2)}) copy-start(bf16[512,16,128]{0,2,1:T(8,128)(2,1)} %copy.79) | copy-start | bytes 6291460
  161.1 6.5 %copy-start.18 = (f32[16,128,128]{2,1,0:T(8,128)S(1)}, f32[16,128,128]{2,1,0:T(8,128)}, u32[]{:S(2)}) copy-start(f32[16,128,128]{2,1,0:T(8,128)} %get-tuple-element.33) | copy-start | bytes 3145732
  167.5 3.8 copy-start.27
  179.6 7.3 %copy-start.12 = (bf16[64,8,16,128]{3,2,1,0:T(8,128)(2,1)S(1)}, bf16[64,8,16,128]{3,2,1,0:T(8,128)(2,1)}, u32[]{:S(2)}) copy-start(bf16[64,8,16,128]{3,2,1,0:T(8,128)(2,1)} %copy-done.10) | copy-start | bytes 6291460
  179.7 32.3 %collective-permute-start.4 = (f32[16,136,128]{2,1,0:T(8,128)S(1)}, f32[16,136,128]{2,1,0:T(8,128)S(1)}, u32[]{:S(2)}, u32[]{:S(2)}) collective-permute-start(f32[16,136,128]{2,1,0:T(8,128)S(1)} %pad_maximum_fusion), channel_id=1, source_target_pairs={{4,0},{8,4},{12,8},{16,12},{20,16},{24,20},{28,24},{5,1},{9,5},{13... | collective-permute-start | bytes 3342344 | tf_op jit(solution)/shard_map/ppermute | solution.py:24
  194.8 27.8 %copy-start.2 = (bf16[16,512,512]{2,1,0:T(8,128)(2,1)}, bf16[16,512,512]{2,1,0:T(8,128)(2,1)S(1)}, u32[]{:S(2)}) copy-start(bf16[16,512,512]{2,1,0:T(8,128)(2,1)S(1)} %multiply_convert_fusion.1) | copy-start | bytes 25165828
  212.0 1.0 copy-start.20
  212.2 10.3 %copy-start.5 = (bf16[64,8,16,128]{3,2,1,0:T(8,128)(2,1)S(1)}, bf16[64,8,16,128]{3,2,1,0:T(8,128)(2,1)}, u32[]{:S(2)}) copy-start(bf16[64,8,16,128]{3,2,1,0:T(8,128)(2,1)} %copy-done.4) | copy-start | bytes 6291460
  212.4 1.0 copy-start.16
  213.4 34.1 %slice-start = ((s8[8388608]{0:T(1024)(128)(4,1)}), s8[4194304]{0:T(1024)(128)(4,1)S(1)}, s32[]{:S(2)}) async-start(s8[8388608]{0:T(1024)(128)(4,1)} %bitcast.102), calls=%async_computation.2 | async-start | bytes 8388608
  214.5 11.7 %copy-start.8 = (bf16[1,512,2048]{1,2,0:T(8,128)(2,1)S(1)}, bf16[1,512,2048]{1,2,0:T(8,128)(2,1)}, u32[]{:S(2)}) copy-start(bf16[1,512,2048]{1,2,0:T(8,128)(2,1)} %copy-done.6) | copy-start | bytes 6291460
  214.5 33.1 %slice-start.1 = ((s8[8388608]{0:T(1024)(128)(4,1)}), s8[4194304]{0:T(1024)(128)(4,1)S(1)}, s32[]{:S(2)}) async-start(s8[8388608]{0:T(1024)(128)(4,1)} %bitcast.102), calls=%async_computation.3 | async-start | bytes 8388608
  214.5 29.2 %collective-permute-start.5 = (f32[16,136,128]{2,1,0:T(8,128)}, f32[16,136,128]{2,1,0:T(8,128)S(1)}, u32[]{:S(2)}, u32[]{:S(2)}) collective-permute-start(f32[16,136,128]{2,1,0:T(8,128)} %pad_maximum_fusion.3), channel_id=1, source_target_pairs={{8,0},{12,4},{16,8},{20,12},{24,16},{28,20},{9,1},{13,5},{17,9},{2... | collective-permute-start | bytes 3342344 | tf_op jit(solution)/shard_map/ppermute | solution.py:24
  226.2 18.5 %copy-start.17 = (f32[16,128,128]{2,1,0:T(8,128)S(1)}, f32[16,128,128]{2,1,0:T(8,128)}, u32[]{:S(2)}) copy-start(f32[16,128,128]{2,1,0:T(8,128)} %copy-done.16) | copy-start | bytes 3145732
  243.6 2.5 copy-start.21
  246.1 4.7 %copy-start.19 = (f32[16,128,128]{2,1,0:T(8,128)S(1)}, f32[16,128,128]{2,1,0:T(8,128)}, u32[]{:S(2)}) copy-start(f32[16,128,128]{2,1,0:T(8,128)} %get-tuple-element.33) | copy-start | bytes 3145732
  246.1 23.1 %collective-permute-start.6 = (f32[16,136,128]{2,1,0:T(8,128)}, f32[16,136,128]{2,1,0:T(8,128)}, u32[]{:S(2)}, u32[]{:S(2)}) collective-permute-start(f32[16,136,128]{2,1,0:T(8,128)} %pad_maximum_fusion.4), channel_id=1, source_target_pairs={{16,0},{20,4},{24,8},{28,12},{17,1},{21,5},{25,9},{29,13},{18,2},{... | collective-permute-start | bytes 3342344 | tf_op jit(solution)/shard_map/ppermute | solution.py:24
  247.6 3.3 copy-start.15
  255.6 15.9 %copy-start.13 = (bf16[64,8,16,128]{3,2,1,0:T(8,128)(2,1)S(1)}, bf16[64,8,16,128]{3,2,1,0:T(8,128)(2,1)}, u32[]{:S(2)}) copy-start(bf16[64,8,16,128]{3,2,1,0:T(8,128)(2,1)} %copy-done.10) | copy-start | bytes 6291460
  269.2 3.3 copy-start.3
  276.5 4.1 copy-start.9
  286.2 123.6 %copy-start.1 = (f32[1,512,16]{1,2,0:T(8,128)S(1)}, f32[1,512,16]{1,2,0:T(8,128)}, u32[]{:S(2)}) copy-start(f32[1,512,16]{1,2,0:T(8,128)} %param.13) | copy-start | bytes 98308
Sparse Core Ops, SparseCore 0:
  179.7 229.9 reduce-scatter.1

commit v4 on v2

--- a/solution.py
+++ b/solution.py
@@ -24,6 +24,18 @@
     if gathered is None:
         gathered = jax.tree.map(jnp.zeros_like, value)
     return gathered
+
+
+def gathered_in(total, state, axis):
+    count, mine = lax.axis_size(axis), lax.axis_index(axis)
+    packed = lax.all_gather(pack_state(total, state), axis)
+    rows = state.shape[1]
+    totals, states = packed[:, :, rows, 0], packed[:, :, :rows]
+    place = jnp.arange(count)
+    between = (place[None, :] > place[:, None]) & (place[None, :] < mine)
+    span = jnp.sum(jnp.where(between[:, :, None], totals[None, :, :], 0.0), axis=1)
+    factor = jnp.where((place < mine)[:, None], jnp.exp(span), 0.0)
+    return jnp.einsum("jh,jhde->hde", factor, states, precision=lax.Precision.HIGHEST)
 
 
 def decay_weights(cumulate, lower_mask):
@@ -69,7 +81,11 @@
     state_end = jnp.einsum(
         "shd,she->hde", key_f32 * remain, value_f32, precision=lax.Precision.HIGHEST
     )
-    state_in = carried_in(pack_state(total, state_end), "ctx", packed_join, False)[:, :HD]
+    split = LOCAL_HEADS // 2
+    state_in = jnp.concatenate([
+        carried_in(pack_state(total[:split], state_end[:split]), "ctx", packed_join, False)[:, :HD],
+        gathered_in(total[split:], state_end[split:], "ctx"),
+    ], axis=0)
     state_end, upstream, query_heads = lax.optimization_barrier((state_end, upstream, query_heads))
 
     advantage = (2 * signs[0] - 1).astype(jnp.float32) * magnitude[0]

time: 378 us -> 408 us (1.079)
  matrix products: 69.7 us -> 85.2 us
  local copies, waits for them, and re-layouts: 28.4 us -> 36 us
  starting transfers between devices: 19.2 us -> 25.3 us
    reduce_scatter x1, waiting for transfers between devices: 109 us -> 120 us  [on_device(): lax.psum_scatter(partial, ('ctx', 'dp'), scatter_dimension=0, tiled=True)]
    ppermute x6, waiting for transfers between devices: 123 us -> 112 us  [carried_in(): lax.ppermute(part, axis, pairs)]
    dot_general x0 -> x1, matrix products: none -> 8.36 us  [gathered_in(): jnp.einsum('jh,jhde->hde', factor, states, precision=lax.Precision.HIGHEST)]
    slice x1 -> x7, local copies, waits for them, and re-layouts: 0.15 us -> 6.55 us  [the longest x2 5.8 us: gathered_in(): totals, states = (packed[:, :, rows, 0], packed[:, :, :rows])]
    ppermute x6, starting transfers between devices: 19.2 us -> 25 us  [carried_in(): lax.ppermute(part, axis, pairs)]
    dot_general x1, matrix products: 5.8 us -> 9.89 us  [on_device(): lax.dot_general(weighted, out_weight, (((1,), (1,)), ((), ())), preferred...]
    unnamed x71 -> x69, local copies, waits for them, and re-layouts: 19.1 us -> 20 us
  transfers between devices with their start and end apart: 7 -> 8, of which waited for: 7 -> 7; matrix products, arithmetic and copies ran while one was open for 22% -> 22% of each run, Pallas kernels for 0% -> 0%
where the time goes in v4:
time: 408 us; the launch traced here: 403 us
  waiting for transfers between devices  232 us (57%)
  matrix products  85.2 us (21%)
  local copies, waits for them, and re-layouts  36 us (9%)
  starting transfers between devices  25.3 us (6%)
  between operations  14.8 us (4%)
  other arithmetic  9.76 us (2%)
    reduce_scatter x1, waiting for transfers between devices, on_device(): lax.psum_scatter(partial, ('ctx', 'dp'), scatter_dimension=0, tiled=True)  120 us
    ppermute x6, waiting for transfers between devices, carried_in(): lax.ppermute(part, axis, pairs)  112 us
    ppermute x6, starting transfers between devices, carried_in(): lax.ppermute(part, axis, pairs)  25 us
    unnamed x69, local copies, waits for them, and re-layouts  20 us
    dot_general x1, matrix products, on_device(): lax.dot_general(weighted, out_weight, (((1,), (1,)), ((), ())), preferred...  9.89 us
    dot_general x1, matrix products, on_device(): lax.dot_general(attn, weighted, (((0,), (0,)), ((), ())), preferred_eleme...  8.58 us
    dot_general x1, matrix products, gathered_in(): jnp.einsum('jh,jhde->hde', factor, states, precision=lax.Precision.HIGHEST)  8.36 us
  transfers between devices with their start and end apart: 8, of which 7 were waited for; matrix products, arithmetic and copies ran while one was open for 22% of the time, Pallas kernels for 0%

profile of v4, /device:TPU:11, one launch (start us, length us, event | category | flops | bytes accessed | tf_op | source)
XLA Modules:
  0.0 403.3 jit_solution(11786222392289000290)
XLA Ops:
  7.2 0.7 copy-done
  7.9 1.1 reduce-window.6
  9.9 2.9 copy.187
  12.7 3.0 copy.191
  15.7 2.8 fusion.16
  18.8 3.2 collective-permute-start
  21.9 12.2 %collective-permute-done = f32[8,136,128]{2,1,0:T(8,128)S(1)} collective-permute-done((f32[8,136,128]{2,1,0:T(8,128)S(1)}, f32[8,136,128]{2,1,0:T(8,128)S(1)}, u32[]{:S(2)}, u32[]{:S(2)}) %collective-permute-start) | collective-permute-done | bytes 557088 | tf_op jit(solution)/shard_map/ppermute | solution.py:19
  34.4 0.5 copy-done.22
  35.0 0.9 pad_maximum_fusion.9
  36.2 2.2 copy.192
  38.4 3.0 copy.173
  41.4 9.9 %convolution_convert_fusion = bf16[512,2048]{1,0:T(8,128)(2,1)} fusion(bf16[2048,2048]{1,0:T(8,128)(2,1)} %param.12, bf16[1,512,2048]{2,1,0:T(8,128)(2,1)} %param.11, f32[512]{0:T(512)S(1)} %bitcast.134), kind=kOutput, calls=%fused_computation.28 | convolution fusion | flops 4299161600 | bytes 12584960 | tf_op jit(solution)/shard_map/dot_general | solution.py:93
  51.3 2.9 copy.188
  54.3 7.7 %multiply_convert_fusion = bf16[16,512,512]{2,1,0:T(8,128)(2,1)S(1)} fusion(bf16[512,16,128]{0,2,1:T(8,128)(2,1)} %bitcast.117, f32[16,512]{1,0:T(8,128)S(1)} %get-tuple-element.58, pred[512,512]{1,0:T(8,128)(4,1)S(1)} %iota_compare_fusion, bf16[512,16,128]{2,1,0:T(8,128)(2,1)} %bitcast.114), kind=kOutput, calls=%fused_computation | convolution fusion | flops 1098907648 | bytes 12877824 | tf_op jit(solution)/shard_map/thd,shd->hts/dot_general | solution.py:104
  62.1 3.2 collective-permute-start.1
  65.4 2.3 fusion.13
  67.7 11.4 %collective-permute-done.1 = f32[8,136,128]{2,1,0:T(8,128)S(1)} collective-permute-done((f32[8,136,128]{2,1,0:T(8,128)S(1)}, f32[8,136,128]{2,1,0:T(8,128)S(1)}, u32[]{:S(2)}, u32[]{:S(2)}) %collective-permute-start.1) | collective-permute-done | bytes 557088 | tf_op jit(solution)/shard_map/ppermute | solution.py:19
  79.0 0.9 exponential_reduce_fusion.3
  80.2 0.8 pad_maximum_fusion.8
  81.0 7.1 %collective-permute-start.2 = (f32[8,136,128]{2,1,0:T(8,128)}, f32[8,136,128]{2,1,0:T(8,128)}, u32[]{:S(2)}, u32[]{:S(2)}) collective-permute-start(f32[8,136,128]{2,1,0:T(8,128)} %pad_maximum_fusion.8), channel_id=1, source_target_pairs={{0,16},{4,20},{8,24},{12,28},{1,17},{5,21},{9,25},{13,29},{2,18},{... | collective-permute-start | bytes 1671176 | tf_op jit(solution)/shard_map/ppermute | solution.py:19
  88.2 6.5 %fusion.30 = f32[16,512,128]{1,2,0:T(8,128)} fusion(bf16[16,512,512]{2,1,0:T(8,128)(2,1)S(1)} %multiply_convert_fusion, bf16[512,16,128]{2,1,0:T(8,128)(2,1)} %bitcast.121), kind=kOutput, calls=%fused_computation.38 | convolution fusion | flops 1073741824 | bytes 14680064 | tf_op jit(solution)/shard_map/hts,shd->thd/dot_general | solution.py:106
  94.7 40.8 %collective-permute-done.2 = f32[8,136,128]{2,1,0:T(8,128)} collective-permute-done((f32[8,136,128]{2,1,0:T(8,128)}, f32[8,136,128]{2,1,0:T(8,128)}, u32[]{:S(2)}, u32[]{:S(2)}) %collective-permute-start.2) | collective-permute-done | bytes 557088 | tf_op jit(solution)/shard_map/ppermute | solution.py:19
  135.6 2.0 fusion.36
  137.6 1.1 slice_reduce_fusion
  138.7 4.7 %slice.106 = f32[8,8,128,128]{3,2,1,0:T(8,128)} slice(f32[8,8,136,128]{3,2,1,0:T(8,128)} %bitcast.130), slice={[0:8], [0:8], [0:128], [0:128]} | slice | bytes 8388608 | tf_op jit(solution)/shard_map/slice | solution.py:33
  143.6 8.4 %fusion.11 = f32[8,1,128,128]{3,1,2,0:T(1,128)S(1)} fusion(f32[8,8,1,1]{0,2,3,1:T(1,128)S(1)} %copy.182, f32[8,8,128,128]{3,2,1,0:T(8,128)} %slice.106), kind=kOutput, calls=%fused_computation.20 | convolution fusion | flops 12582912 | bytes 4718848 | tf_op jit(solution)/shard_map/jh,jhde->hde/dot_general | solution.py:38
  152.0 4.4 %fusion.8 = bf16[512,16,128]{0,2,1:T(8,128)(2,1)S(1)} fusion(f32[16,512,128]{1,2,0:T(8,128)} %fusion.30, bf16[512,16,128]{0,2,1:T(8,128)(2,1)S(1)} %copy-done.13, f32[512,16]{0,1:T(8,128)S(1)} %get-tuple-element.57, f32[8,128,128]{2,1,0:T(8,128)S(1)} %bitcast.127, f32[8,128,128]{2,1,0:T(8,128)S(1)} %copy-done.14), kind=kOutput, calls=%fused_computation.16 | convolution fusion | flops 1614020608 | bytes 9469952 | tf_op jit(solution)/shard_map/thd,hde->the/dot_general | solution.py:107
  156.5 8.6 %fusion.20 = f32[2048,2048]{1,0:T(8,128)} fusion(bf16[512,2048]{0,1:T(8,128)(2,1)S(1)} %bitcast.133, bf16[1,512,2048]{2,1,0:T(8,128)(2,1)S(1)} %copy-done.29, f32[512]{0:T(512)S(1)} %bitcast.135), kind=kOutput, calls=%fused_computation.30 | convolution fusion | flops 4298113024 | bytes 20973568 | tf_op jit(solution)/shard_map/dot_general | solution.py:111
  165.3 4.5 %collective-permute-start.3 = (f32[16,136,128]{2,1,0:T(8,128)S(1)}, f32[16,136,128]{2,1,0:T(8,128)S(1)}, u32[]{:S(2)}, u32[]{:S(2)}) collective-permute-start(f32[16,136,128]{2,1,0:T(8,128)S(1)} %pad_maximum_fusion), channel_id=1, source_target_pairs={{4,0},{8,4},{12,8},{16,12},{20,16},{24,20},{28,24},{5,1},{9,5},{13... | collective-permute-start | bytes 3342344 | tf_op jit(solution)/shard_map/ppermute | solution.py:19
  169.8 7.9 %multiply_convert_fusion.1 = bf16[16,512,512]{2,1,0:T(8,128)(2,1)S(1)} fusion(bf16[512,16,128]{0,2,1:T(8,128)(2,1)S(1)} %bitcast.110, f32[16,512]{1,0:T(8,128)S(1)} %get-tuple-element.58, pred[512,512]{1,0:T(8,128)(4,1)} %copy-done.26, bf16[512,16,128]{2,1,0:T(8,128)(2,1)S(1)} %bitcast.122), kind=kOutput, calls=%fused_computation.1 | convolution fusion | flops 1098907648 | bytes 12877824 | tf_op jit(solution)/shard_map/thd,shd->hts/dot_general | solution.py:118
  177.7 21.5 %collective-permute-done.3 = f32[16,136,128]{2,1,0:T(8,128)S(1)} collective-permute-done((f32[16,136,128]{2,1,0:T(8,128)S(1)}, f32[16,136,128]{2,1,0:T(8,128)S(1)}, u32[]{:S(2)}, u32[]{:S(2)}) %collective-permute-start.3) | collective-permute-done | bytes 1114144 | tf_op jit(solution)/shard_map/ppermute | solution.py:19
  199.8 5.6 %collective-permute-start.4 = (f32[16,136,128]{2,1,0:T(8,128)S(1)}, f32[16,136,128]{2,1,0:T(8,128)S(1)}, u32[]{:S(2)}, u32[]{:S(2)}) collective-permute-start(f32[16,136,128]{2,1,0:T(8,128)S(1)} %pad_maximum_fusion.1), channel_id=1, source_target_pairs={{8,0},{12,4},{16,8},{20,12},{24,16},{28,20},{9,1},{13,5},{17,9},{2... | collective-permute-start | bytes 3342344 | tf_op jit(solution)/shard_map/ppermute | solution.py:19
  205.4 3.2 fusion.44
  208.7 3.6 fusion.27
  212.3 16.8 %collective-permute-done.4 = f32[16,136,128]{2,1,0:T(8,128)S(1)} collective-permute-done((f32[16,136,128]{2,1,0:T(8,128)S(1)}, f32[16,136,128]{2,1,0:T(8,128)S(1)}, u32[]{:S(2)}, u32[]{:S(2)}) %collective-permute-start.4) | collective-permute-done | bytes 1114144 | tf_op jit(solution)/shard_map/ppermute | solution.py:19
  229.7 0.4 copy-done.21
  230.1 1.4 collective-permute-start.5
  231.6 4.8 %fusion.43 = f32[16,512,128]{1,2,0:T(8,128)} fusion(bf16[16,512,512]{2,1,0:T(8,128)(2,1)S(1)} %multiply_convert_fusion.1, bf16[512,16,128]{0,2,1:T(8,128)(2,1)S(1)} %bitcast.118), kind=kOutput, calls=%fused_computation.91 | convolution fusion | flops 1073741824 | bytes 14680064 | tf_op jit(solution)/shard_map/hts,shd->thd/dot_general | solution.py:122
  236.3 5.6 %fusion.10 = bf16[512,16,128]{0,2,1:T(8,128)(2,1)} fusion(f32[16,512,128]{1,2,0:T(8,128)} %fusion.43, bf16[512,16,128]{0,2,1:T(8,128)(2,1)S(1)} %bitcast.112, f32[512,16]{0,1:T(8,128)S(1)} %get-tuple-element.57, f32[8,128,128]{2,1,0:T(8,128)S(1)} %bitcast.128, f32[8,128,128]{2,1,0:T(8,128)S(1)} %copy-done.15), kind=kOutput, calls=%fused_computation.19 | convolution fusion | flops 1614020608 | bytes 9469952 | tf_op jit(solution)/shard_map/hde,the->thd/dot_general | solution.py:125
  241.9 4.2 %copy.179 = bf16[1,512,2048]{2,1,0:T(8,128)(2,1)} copy(bf16[1,512,2048]{1,2,0:T(8,128)(2,1)} %bitcast.124) | data formatting | bytes 4194304
  246.1 9.0 %collective-permute-done.5 = f32[16,136,128]{2,1,0:T(8,128)} collective-permute-done((f32[16,136,128]{2,1,0:T(8,128)S(1)}, f32[16,136,128]{2,1,0:T(8,128)}, u32[]{:S(2)}, u32[]{:S(2)}) %collective-permute-start.5) | collective-permute-done | bytes 1114144 | tf_op jit(solution)/shard_map/ppermute | solution.py:19
  255.1 2.3 fusion.35
  257.4 0.9 copy-done.3
  258.3 3.9 fusion.6
  262.2 4.1 %copy.180 = bf16[1,512,2048]{2,1,0:T(8,128)(2,1)} copy(bf16[1,512,2048]{1,2,0:T(8,128)(2,1)} %bitcast.126) | data formatting | bytes 4194304
  266.3 5.6 %fusion.4 = bf16[512,16,128]{0,2,1:T(8,128)(2,1)} fusion(f32[16,128,512]{2,1,0:T(8,128)} %fusion.44, f32[16,128,128]{2,1,0:T(8,128)S(1)} %fusion.35, bf16[512,16,128]{0,2,1:T(8,128)(2,1)S(1)} %bitcast.119, f32[512,16]{0,1:T(8,128)S(1)} %get-tuple-element.48), kind=kOutput, calls=%fused_computation.10 | convolution fusion | flops 1613758464 | bytes 9469952 | tf_op jit(solution)/shard_map/hde,shd->she/dot_general | solution.py:131
  271.9 3.9 copy.181
  275.8 120.4 %reduce-scatter.2.cloned.1.call-done = f32[64,2048]{1,0:T(8,128)} async-done(((f32[2048,2048]{1,0:T(8,128)}), f32[64,2048]{1,0:T(8,128)}) %reduce-scatter.2.cloned.1.call-update) | async-done | bytes 524304 | tf_op jit(solution)/shard_map/reduce_scatter | solution.py:115
  (105 shorter events, 3.6 us)
Async XLA Ops:
  7.2 0.8 copy-start
  7.2 130.4 %all-gather.3.cloned.1.call-start = ((), (), s32[]{:S(2)}) async-start(), calls=%async_computation.2 | async-start | bytes 5013504 | tf_op jit(solution)/shard_map/all_gather | solution.py:31
  12.7 3.0 copy-start.6
  15.7 2.9 copy-start.9
  18.8 15.4 %collective-permute-start = (f32[8,136,128]{2,1,0:T(8,128)S(1)}, f32[8,136,128]{2,1,0:T(8,128)S(1)}, u32[]{:S(2)}, u32[]{:S(2)}) collective-permute-start(f32[8,136,128]{2,1,0:T(8,128)S(1)} %pad_maximum_fusion.6), channel_id=1, source_target_pairs={{0,4},{4,8},{8,12},{12,16},{16,20},{20,24},{24,28},{1,5},{5,9},{9,... | collective-permute-start | bytes 1671176 | tf_op jit(solution)/shard_map/ppermute | solution.py:19
  34.1 0.8 copy-start.22
  35.0 27.1 %copy-start.18 = (f32[8,128,128]{2,1,0:T(8,128)}, f32[8,128,128]{2,1,0:T(8,128)S(1)}, u32[]{:S(2)}) copy-start(f32[8,128,128]{2,1,0:T(8,128)S(1)} %get-tuple-element.54) | copy-start | bytes 1572868
  36.0 360.2 %reduce-scatter.2.cloned.1.call-start = ((), (), s32[]{:S(2)}) async-start(), calls=%async_computation.1 | async-start | bytes 17301504 | tf_op jit(solution)/shard_map/reduce_scatter | solution.py:115
  38.4 3.0 copy-start.4
  38.4 3.0 copy-start.27
  38.4 3.0 copy-start.28
  54.3 7.7 %copy-start.26 = (pred[512,512]{1,0:T(8,128)(4,1)}, pred[512,512]{1,0:T(8,128)(4,1)S(1)}, u32[]{:S(2)}) copy-start(pred[512,512]{1,0:T(8,128)(4,1)S(1)} %iota_compare_fusion) | copy-start | bytes 786436
  54.3 11.0 %copy-start.12 = (bf16[512,16,128]{0,2,1:T(8,128)(2,1)S(1)}, bf16[512,16,128]{0,2,1:T(8,128)(2,1)}, u32[]{:S(2)}) copy-start(bf16[512,16,128]{0,2,1:T(8,128)(2,1)} %copy.173) | copy-start | bytes 6291460
  62.0 26.1 %copy-start.2 = (bf16[16,512,512]{2,1,0:T(8,128)(2,1)}, bf16[16,512,512]{2,1,0:T(8,128)(2,1)S(1)}, u32[]{:S(2)}) copy-start(bf16[16,512,512]{2,1,0:T(8,128)(2,1)S(1)} %multiply_convert_fusion) | copy-start | bytes 25165828
  62.1 16.9 %collective-permute-start.1 = (f32[8,136,128]{2,1,0:T(8,128)S(1)}, f32[8,136,128]{2,1,0:T(8,128)S(1)}, u32[]{:S(2)}, u32[]{:S(2)}) collective-permute-start(f32[8,136,128]{2,1,0:T(8,128)S(1)} %pad_maximum_fusion.7), channel_id=1, source_target_pairs={{0,8},{4,12},{8,16},{12,20},{16,24},{20,28},{1,9},{5,13},{9,17},{1... | collective-permute-start | bytes 1671176 | tf_op jit(solution)/shard_map/ppermute | solution.py:19
  65.4 14.6 %copy-start.19 = (f32[8,128,128]{2,1,0:T(8,128)S(1)}, f32[8,128,128]{2,1,0:T(8,128)}, u32[]{:S(2)}) copy-start(f32[8,128,128]{2,1,0:T(8,128)} %copy-done.18) | copy-start | bytes 1572868
  79.0 2.0 copy-start.24
  81.0 54.5 %copy-start.23 = (f32[8,136,128]{2,1,0:T(8,128)S(1)}, f32[8,136,128]{2,1,0:T(8,128)}, u32[]{:S(2)}) copy-start(f32[8,136,128]{2,1,0:T(8,128)} %copy-done.22) | copy-start | bytes 1671172
  81.0 54.5 %collective-permute-start.2 = (f32[8,136,128]{2,1,0:T(8,128)}, f32[8,136,128]{2,1,0:T(8,128)}, u32[]{:S(2)}, u32[]{:S(2)}) collective-permute-start(f32[8,136,128]{2,1,0:T(8,128)} %pad_maximum_fusion.8), channel_id=1, source_target_pairs={{0,16},{4,20},{8,24},{12,28},{1,17},{5,21},{9,25},{13,29},{2,18},{... | collective-permute-start | bytes 1671176 | tf_op jit(solution)/shard_map/ppermute | solution.py:19
  88.2 47.4 %copy-start.25 = (f32[8,136,128]{2,1,0:T(8,128)S(1)}, f32[8,136,128]{2,1,0:T(8,128)}, u32[]{:S(2)}) copy-start(f32[8,136,128]{2,1,0:T(8,128)} %copy-done.24) | copy-start | bytes 1671172
  143.6 8.4 %copy-start.13 = (bf16[512,16,128]{0,2,1:T(8,128)(2,1)S(1)}, bf16[512,16,128]{0,2,1:T(8,128)(2,1)}, u32[]{:S(2)}) copy-start(bf16[512,16,128]{0,2,1:T(8,128)(2,1)} %copy.173) | copy-start | bytes 6291460
  143.6 8.4 %copy-start.14 = (f32[8,128,128]{2,1,0:T(8,128)S(1)}, f32[8,128,128]{2,1,0:T(8,128)}, u32[]{:S(2)}) copy-start(f32[8,128,128]{2,1,0:T(8,128)} %fusion.36) | copy-start | bytes 1572868
  152.0 4.5 %copy-start.16 = (f32[8,1,128,128]{3,1,2,0:T(1,128)}, f32[8,1,128,128]{3,1,2,0:T(1,128)S(1)}, u32[]{:S(2)}) copy-start(f32[8,1,128,128]{3,1,2,0:T(1,128)S(1)} %fusion.11) | copy-start | bytes 1572868
  152.0 4.5 %copy-start.29 = (bf16[1,512,2048]{2,1,0:T(8,128)(2,1)S(1)}, bf16[1,512,2048]{2,1,0:T(8,128)(2,1)}, u32[]{:S(2)}) copy-start(bf16[1,512,2048]{2,1,0:T(8,128)(2,1)} %param.11) | copy-start | bytes 6291460
  165.1 4.7 %copy-start.10 = (bf16[64,8,16,128]{3,2,1,0:T(8,128)(2,1)S(1)}, bf16[64,8,16,128]{3,2,1,0:T(8,128)(2,1)}, u32[]{:S(2)}) copy-start(bf16[64,8,16,128]{3,2,1,0:T(8,128)(2,1)} %copy-done.9) | copy-start | bytes 6291460
  165.2 40.2 %slice-start = ((s8[8388608]{0:T(1024)(128)(4,1)}), s8[4194304]{0:T(1024)(128)(4,1)S(1)}, s32[]{:S(2)}) async-start(s8[8388608]{0:T(1024)(128)(4,1)} %bitcast.107), calls=%async_computation.3 | async-start | bytes 8388608
  165.3 40.1 %slice-start.1 = ((s8[8388608]{0:T(1024)(128)(4,1)}), s8[4194304]{0:T(1024)(128)(4,1)S(1)}, s32[]{:S(2)}) async-start(s8[8388608]{0:T(1024)(128)(4,1)} %bitcast.107), calls=%async_computation.4 | async-start | bytes 8388608
  165.3 33.9 %collective-permute-start.3 = (f32[16,136,128]{2,1,0:T(8,128)S(1)}, f32[16,136,128]{2,1,0:T(8,128)S(1)}, u32[]{:S(2)}, u32[]{:S(2)}) collective-permute-start(f32[16,136,128]{2,1,0:T(8,128)S(1)} %pad_maximum_fusion), channel_id=1, source_target_pairs={{4,0},{8,4},{12,8},{16,12},{20,16},{24,20},{28,24},{5,1},{9,5},{13... | collective-permute-start | bytes 3342344 | tf_op jit(solution)/shard_map/ppermute | solution.py:19
  199.2 29.9 %copy-start.20 = (f32[16,136,128]{2,1,0:T(8,128)}, f32[16,136,128]{2,1,0:T(8,128)S(1)}, u32[]{:S(2)}) copy-start(f32[16,136,128]{2,1,0:T(8,128)S(1)} %collective-permute-done.3) | copy-start | bytes 3342340
  199.8 29.3 %collective-permute-start.4 = (f32[16,136,128]{2,1,0:T(8,128)S(1)}, f32[16,136,128]{2,1,0:T(8,128)S(1)}, u32[]{:S(2)}, u32[]{:S(2)}) collective-permute-start(f32[16,136,128]{2,1,0:T(8,128)S(1)} %pad_maximum_fusion.1), channel_id=1, source_target_pairs={{8,0},{12,4},{16,8},{20,12},{24,16},{28,20},{9,1},{13,5},{17,9},{2... | collective-permute-start | bytes 3342344 | tf_op jit(solution)/shard_map/ppermute | solution.py:19
  205.4 3.2 copy-start.5
  229.1 1.0 copy-start.21
  229.3 2.2 copy-start.7
  230.1 6.2 %copy-start.15 = (f32[8,128,128]{2,1,0:T(8,128)S(1)}, f32[8,128,128]{2,1,0:T(8,128)}, u32[]{:S(2)}) copy-start(f32[8,128,128]{2,1,0:T(8,128)} %fusion.36) | copy-start | bytes 1572868
  230.1 6.2 %copy-start.17 = (f32[8,1,128,128]{3,1,2,0:T(1,128)S(1)}, f32[8,1,128,128]{3,1,2,0:T(1,128)}, u32[]{:S(2)}) copy-start(f32[8,1,128,128]{3,1,2,0:T(1,128)} %copy-done.16) | copy-start | bytes 1572868
  230.1 25.0 %collective-permute-start.5 = (f32[16,136,128]{2,1,0:T(8,128)S(1)}, f32[16,136,128]{2,1,0:T(8,128)}, u32[]{:S(2)}, u32[]{:S(2)}) collective-permute-start(f32[16,136,128]{2,1,0:T(8,128)S(1)} %pad_maximum_fusion.2), channel_id=1, source_target_pairs={{16,0},{20,4},{24,8},{28,12},{17,1},{21,5},{25,9},{29,13},{18,2},{... | collective-permute-start | bytes 3342344 | tf_op jit(solution)/shard_map/ppermute | solution.py:19
  241.9 15.5 %copy-start.11 = (bf16[64,8,16,128]{3,2,1,0:T(8,128)(2,1)S(1)}, bf16[64,8,16,128]{3,2,1,0:T(8,128)(2,1)}, u32[]{:S(2)}) copy-start(bf16[64,8,16,128]{3,2,1,0:T(8,128)(2,1)} %copy-done.9) | copy-start | bytes 6291460
  255.1 3.2 copy-start.3
  262.2 4.1 %copy-start.8 = (bf16[1,512,2048]{1,2,0:T(8,128)(2,1)S(1)}, bf16[1,512,2048]{1,2,0:T(8,128)(2,1)}, u32[]{:S(2)}) copy-start(bf16[1,512,2048]{1,2,0:T(8,128)(2,1)} %copy-done.6) | copy-start | bytes 6291460
  271.9 124.3 %copy-start.1 = (f32[1,512,16]{1,2,0:T(8,128)S(1)}, f32[1,512,16]{1,2,0:T(8,128)}, u32[]{:S(2)}) copy-start(f32[1,512,16]{1,2,0:T(8,128)} %param.13) | copy-start | bytes 98308
Sparse Core Ops, SparseCore 0:
  36.1 100.6 all-gather.2
  165.2 230.9 reduce-scatter.1

commit v5 on v2

--- a/solution.py
+++ b/solution.py
@@ -24,6 +24,20 @@
     if gathered is None:
         gathered = jax.tree.map(jnp.zeros_like, value)
     return gathered
+
+
+def split_einsum(spec, first, second):
+    def passes(wide, place):
+        high = wide.astype(jnp.bfloat16)
+        low = (wide - high.astype(jnp.float32)).astype(jnp.bfloat16)
+        out = []
+        for part in (high, low):
+            args = (first, part) if place == 1 else (part, second)
+            out.append(jnp.einsum(spec, *args, preferred_element_type=jnp.float32))
+        return out[0] + out[1]
+    if first.dtype == jnp.float32:
+        return passes(first, 0)
+    return passes(second, 1)
 
 
 def decay_weights(cumulate, lower_mask):
@@ -66,9 +80,7 @@
     key_f32 = key_heads.astype(jnp.float32)
     value_f32 = value_heads.astype(jnp.float32)
 
-    state_end = jnp.einsum(
-        "shd,she->hde", key_f32 * remain, value_f32, precision=lax.Precision.HIGHEST
-    )
+    state_end = split_einsum("shd,she->hde", key_f32 * remain, value_heads)
     state_in = carried_in(pack_state(total, state_end), "ctx", packed_join, False)[:, :HD]
     state_end, upstream, query_heads = lax.optimization_barrier((state_end, upstream, query_heads))
 
@@ -78,19 +90,14 @@
         weighted, out_weight, (((1,), (1,)), ((), ())), preferred_element_type=jnp.float32
     ).astype(jnp.bfloat16)
     dout_heads = to_heads(dout)
-    dout_f32 = dout_heads.astype(jnp.float32)
-    back_end = jnp.einsum(
-        "thd,the->hde", query_f32 * growth, dout_f32, precision=lax.Precision.HIGHEST
-    )
+    back_end = split_einsum("thd,the->hde", query_f32 * growth, dout_heads)
 
     lower_mask = (jnp.arange(BLOCK)[:, None] >= jnp.arange(BLOCK)[None, :])[None]
     weight = decay_weights(running, lower_mask)
     scores = jnp.einsum("thd,shd->hts", query_heads, key_heads, preferred_element_type=jnp.float32)
     probs = (scale * scores * weight).astype(jnp.bfloat16)
     attend = jnp.einsum("hts,shd->thd", probs, value_heads, preferred_element_type=jnp.float32)
-    attend = attend + scale * growth * jnp.einsum(
-        "thd,hde->the", query_f32, state_in, precision=lax.Precision.HIGHEST
-    )
+    attend = attend + scale * growth * split_einsum("thd,hde->the", query_heads, state_in)
     attn = attend.reshape(tokens, width).astype(jnp.bfloat16)
     partial = lax.dot_general(
         attn, weighted, (((0,), (0,)), ((), ())), preferred_element_type=jnp.float32
@@ -106,15 +113,9 @@
     grad_q = jnp.einsum("hts,shd->thd", dprobs, key_heads, preferred_element_type=jnp.float32)
     grad_k = jnp.einsum("hts,thd->shd", dprobs, query_heads, preferred_element_type=jnp.float32)
     grad_v = jnp.einsum("hts,thd->shd", probs, dout_heads, preferred_element_type=jnp.float32)
-    grad_q = grad_q + scale * growth * jnp.einsum(
-        "hde,the->thd", state_in, dout_f32, precision=lax.Precision.HIGHEST
-    )
-    grad_k = grad_k + scale * remain * jnp.einsum(
-        "hde,she->shd", back_in, value_f32, precision=lax.Precision.HIGHEST
-    )
-    grad_v = grad_v + scale * remain * jnp.einsum(
-        "hde,shd->she", back_in, key_f32, precision=lax.Precision.HIGHEST
-    )
+    grad_q = grad_q + scale * growth * split_einsum("hde,the->thd", state_in, dout_heads)
+    grad_k = grad_k + scale * remain * split_einsum("hde,she->shd", back_in, value_heads)
+    grad_v = grad_v + scale * remain * split_einsum("hde,shd->she", back_in, key_heads)
     shape_out = (1, tokens, width)
     return (
         grad_q.reshape(shape_out).astype(jnp.bfloat16),

time: 378 us -> 383 us (1.013)
  waiting for transfers between devices: 232 us -> 227 us
  matrix products: 69.7 us -> 73.6 us
    ppermute x6, waiting for transfers between devices: 123 us -> 117 us  [carried_in(): lax.ppermute(part, axis, pairs)]
    dot_general x6 -> x12, matrix products: 22.8 us -> 18.5 us  [passes(): out.append(jnp.einsum(spec, *args, preferred_element_type=jnp.float32))]
    dot_general x1, matrix products: 5.8 us -> 9.88 us  [on_device(): lax.dot_general(weighted, out_weight, (((1,), (1,)), ((), ())), preferred...]
    unnamed x71 -> x65, local copies, waits for them, and re-layouts: 19.1 us -> 21.6 us
  transfers between devices with their start and end apart: 7 -> 7, of which waited for: 7 -> 7; matrix products, arithmetic and copies ran while one was open for 22% -> 23% of each run, Pallas kernels for 0% -> 0%
where the time goes in v5:
time: 383 us; the launch traced here: 382 us
  waiting for transfers between devices  227 us (59%)
  matrix products  73.6 us (19%)
  local copies, waits for them, and re-layouts  31 us (8%)
  starting transfers between devices  19.1 us (5%)
  other arithmetic  16.6 us (4%)
  between operations  14.6 us (4%)
    ppermute x6, waiting for transfers between devices, carried_in(): lax.ppermute(part, axis, pairs)  117 us
    reduce_scatter x1, waiting for transfers between devices, on_device(): lax.psum_scatter(partial, ('ctx', 'dp'), scatter_dimension=0, tiled=True)  110 us
    unnamed x65, local copies, waits for them, and re-layouts  21.6 us
    ppermute x6, starting transfers between devices, carried_in(): lax.ppermute(part, axis, pairs)  19.1 us
    dot_general x12, matrix products, passes(): out.append(jnp.einsum(spec, *args, preferred_element_type=jnp.float32))  18.5 us
    dot_general x1, matrix products, on_device(): lax.dot_general(weighted, out_weight, (((1,), (1,)), ((), ())), preferred...  9.88 us
    dot_general x1, matrix products, on_device(): jnp.einsum('hts,shd->thd', dprobs, key_heads, preferred_element_type=jnp....  8.25 us
    dot_general x1, matrix products, on_device(): lax.dot_general(attn, weighted, (((0,), (0,)), ((), ())), preferred_eleme...  8.16 us
  transfers between devices with their start and end apart: 7, of which 7 were waited for; matrix products, arithmetic and copies ran while one was open for 23% of the time, Pallas kernels for 0%

profile of v5, /device:TPU:11, one launch (start us, length us, event | category | flops | bytes accessed | tf_op | source)
XLA Modules:
  0.0 381.6 jit_solution(3244245219101252627)
XLA Ops:
  7.9 1.1 reduce-window.6
  9.6 2.9 copy.120
  12.5 3.0 copy.124
  15.5 1.4 fusion.13
  16.9 1.5 fusion.30
  18.5 1.1 pad_maximum_fusion.1
  19.6 3.2 collective-permute-start
  23.5 3.0 copy.102
  26.5 9.9 %convolution_convert_fusion = bf16[512,2048]{1,0:T(8,128)(2,1)} fusion(bf16[2048,2048]{1,0:T(8,128)(2,1)} %param.12, bf16[1,512,2048]{2,1,0:T(8,128)(2,1)} %param.11, f32[512]{0:T(512)S(1)} %bitcast.136), kind=kOutput, calls=%fused_computation.26 | convolution fusion | flops 4299161600 | bytes 12584960 | tf_op jit(solution)/shard_map/dot_general | solution.py:89
  36.4 2.9 copy.121
  39.3 7.9 %collective-permute-done = f32[16,136,128]{2,1,0:T(8,128)} collective-permute-done((f32[16,136,128]{2,1,0:T(8,128)}, f32[16,136,128]{2,1,0:T(8,128)}, u32[]{:S(2)}, u32[]{:S(2)}) %collective-permute-start) | collective-permute-done | bytes 1114144 | tf_op jit(solution)/shard_map/ppermute | solution.py:19
  47.3 1.4 multiply_add_fusion.3
  49.9 3.2 collective-permute-start.1
  53.1 7.7 %multiply_convert_fusion = bf16[16,512,512]{2,1,0:T(8,128)(2,1)} fusion(bf16[512,16,128]{0,2,1:T(8,128)(2,1)S(1)} %bitcast.124, f32[16,512]{1,0:T(8,128)S(1)} %get-tuple-element.36, pred[512,512]{1,0:T(8,128)(4,1)S(1)} %iota_compare_fusion, bf16[512,16,128]{2,1,0:T(8,128)(2,1)S(1)} %bitcast.110), kind=kOutput, calls=%fused_computation | convolution fusion | flops 1098907648 | bytes 12877824 | tf_op jit(solution)/shard_map/thd,shd->hts/dot_general | solution.py:97
  60.8 15.5 %collective-permute-done.1 = f32[16,136,128]{2,1,0:T(8,128)S(1)} collective-permute-done((f32[16,136,128]{2,1,0:T(8,128)S(1)}, f32[16,136,128]{2,1,0:T(8,128)S(1)}, u32[]{:S(2)}, u32[]{:S(2)}) %collective-permute-start.1) | collective-permute-done | bytes 1114144 | tf_op jit(solution)/shard_map/ppermute | solution.py:19
  77.7 5.4 %collective-permute-start.2 = (f32[16,136,128]{2,1,0:T(8,128)S(1)}, f32[16,136,128]{2,1,0:T(8,128)}, u32[]{:S(2)}, u32[]{:S(2)}) collective-permute-start(f32[16,136,128]{2,1,0:T(8,128)S(1)} %pad_maximum_fusion.3), channel_id=1, source_target_pairs={{0,16},{4,20},{8,24},{12,28},{1,17},{5,21},{9,25},{13,29},{2,18},{... | collective-permute-start | bytes 3342344 | tf_op jit(solution)/shard_map/ppermute | solution.py:19
  83.8 1.7 fusion.29
  85.5 6.3 %fusion.39 = f32[16,512,128]{1,2,0:T(8,128)S(1)} fusion(bf16[16,512,512]{2,1,0:T(8,128)(2,1)} %multiply_convert_fusion, bf16[512,16,128]{2,1,0:T(8,128)(2,1)S(1)} %bitcast.118), kind=kOutput, calls=%fused_computation.64 | convolution fusion | flops 1073741824 | bytes 14680064 | tf_op jit(solution)/shard_map/hts,shd->thd/dot_general | solution.py:99
  91.8 38.3 %collective-permute-done.2 = f32[16,136,128]{2,1,0:T(8,128)} collective-permute-done((f32[16,136,128]{2,1,0:T(8,128)S(1)}, f32[16,136,128]{2,1,0:T(8,128)}, u32[]{:S(2)}, u32[]{:S(2)}) %collective-permute-start.2) | collective-permute-done | bytes 1114144 | tf_op jit(solution)/shard_map/ppermute | solution.py:19
  130.1 1.8 fusion.38
  131.9 1.3 fusion.33
  133.2 1.7 fusion.8
  134.9 8.2 %fusion.20 = f32[2048,2048]{1,0:T(8,128)} fusion(bf16[512,2048]{0,1:T(8,128)(2,1)S(1)} %bitcast.133, bf16[1,512,2048]{2,1,0:T(8,128)(2,1)S(1)} %copy-done.27, f32[512]{0:T(512)S(1)} %bitcast.137), kind=kOutput, calls=%fused_computation.32 | convolution fusion | flops 4298113024 | bytes 20973568 | tf_op jit(solution)/shard_map/dot_general | solution.py:102
  143.1 1.5 pad_maximum_fusion
  144.6 3.2 collective-permute-start.3
  147.8 7.9 %multiply_convert_fusion.1 = bf16[16,512,512]{2,1,0:T(8,128)(2,1)S(1)} fusion(bf16[512,16,128]{0,2,1:T(8,128)(2,1)S(1)} %bitcast.105, f32[16,512]{1,0:T(8,128)S(1)} %get-tuple-element.36, pred[512,512]{1,0:T(8,128)(4,1)} %copy-done.24, bf16[512,16,128]{2,1,0:T(8,128)(2,1)S(1)} %bitcast.119), kind=kOutput, calls=%fused_computation.1 | convolution fusion | flops 1098907648 | bytes 12877824 | tf_op jit(solution)/shard_map/thd,shd->hts/dot_general | solution.py:109
  155.7 27.1 %collective-permute-done.3 = f32[16,136,128]{2,1,0:T(8,128)S(1)} collective-permute-done((f32[16,136,128]{2,1,0:T(8,128)S(1)}, f32[16,136,128]{2,1,0:T(8,128)S(1)}, u32[]{:S(2)}, u32[]{:S(2)}) %collective-permute-start.3) | collective-permute-done | bytes 1114144 | tf_op jit(solution)/shard_map/ppermute | solution.py:19
  185.3 2.9 collective-permute-start.4
  188.2 3.7 fusion.31
  191.9 8.2 %fusion.57 = f32[16,512,128]{1,2,0:T(8,128)} fusion(bf16[16,512,512]{2,1,0:T(8,128)(2,1)} %copy-done.5, bf16[512,16,128]{0,2,1:T(8,128)(2,1)S(1)} %bitcast.125), kind=kOutput, calls=%fused_computation.100 | convolution fusion | flops 1073741824 | bytes 14680064 | tf_op jit(solution)/shard_map/hts,shd->thd/dot_general | solution.py:113
  200.1 14.0 %collective-permute-done.4 = f32[16,136,128]{2,1,0:T(8,128)} collective-permute-done((f32[16,136,128]{2,1,0:T(8,128)}, f32[16,136,128]{2,1,0:T(8,128)}, u32[]{:S(2)}, u32[]{:S(2)}) %collective-permute-start.4) | collective-permute-done | bytes 1114144 | tf_op jit(solution)/shard_map/ppermute | solution.py:19
  214.2 1.1 exponential_reduce_fusion.1
  215.3 1.4 multiply_add_fusion
  216.8 1.1 pad_maximum_fusion.5
  217.9 1.3 collective-permute-start.5
  219.2 3.2 fusion.58
  223.1 1.5 copy-done.16
  224.7 2.2 fusion.10
  226.9 4.0 %copy.113 = bf16[1,512,2048]{2,1,0:T(8,128)(2,1)} copy(bf16[1,512,2048]{1,2,0:T(8,128)(2,1)} %bitcast.128) | data formatting | bytes 4194304
  230.9 14.0 %collective-permute-done.5 = f32[16,136,128]{2,1,0:T(8,128)} collective-permute-done((f32[16,136,128]{2,1,0:T(8,128)}, f32[16,136,128]{2,1,0:T(8,128)}, u32[]{:S(2)}, u32[]{:S(2)}) %collective-permute-start.5) | collective-permute-done | bytes 1114144 | tf_op jit(solution)/shard_map/ppermute | solution.py:19
  244.9 2.0 fusion.37
  247.9 1.5 copy-done.15
  249.4 2.2 fusion.4
  251.7 4.1 %copy.115 = bf16[1,512,2048]{2,1,0:T(8,128)(2,1)} copy(bf16[1,512,2048]{1,2,0:T(8,128)(2,1)} %bitcast.130) | data formatting | bytes 4194304
  255.7 1.3 fusion.41
  257.9 3.0 fusion.6
  260.9 3.9 %copy.114 = bf16[1,512,2048]{2,1,0:T(8,128)(2,1)} copy(bf16[1,512,2048]{1,2,0:T(8,128)(2,1)} %bitcast.129) | data formatting | bytes 4194304
  264.9 109.9 %reduce-scatter.2.cloned.1.call-done = f32[64,2048]{1,0:T(8,128)} async-done(((f32[2048,2048]{1,0:T(8,128)}), f32[64,2048]{1,0:T(8,128)}) %reduce-scatter.2.cloned.1.call-update) | async-done | bytes 524304 | tf_op jit(solution)/shard_map/reduce_scatter | solution.py:106
  (90 shorter events, 10.7 us)
Async XLA Ops:
  7.2 0.8 copy-start
  7.2 367.6 %reduce-scatter.2.cloned.1.call-start = ((), (), s32[]{:S(2)}) async-start(), calls=%async_computation.1 | async-start | bytes 17301504 | tf_op jit(solution)/shard_map/reduce_scatter | solution.py:106
  12.5 4.4 %copy-start.10 = (bf16[1,512,2048]{1,2,0:T(8,128)(2,1)}, bf16[1,512,2048]{1,2,0:T(8,128)(2,1)S(1)}, u32[]{:S(2)}) copy-start(bf16[1,512,2048]{1,2,0:T(8,128)(2,1)S(1)} %copy.120) | copy-start | bytes 6291460
  15.5 1.4 copy-start.6
  18.4 4.4 %copy-start.23 = (bf16[1,512,2048]{2,1,0:T(8,128)(2,1)S(1)}, bf16[1,512,2048]{2,1,0:T(8,128)(2,1)}, u32[]{:S(2)}) copy-start(bf16[1,512,2048]{2,1,0:T(8,128)(2,1)} %param.8) | copy-start | bytes 6291460
  19.6 27.6 %collective-permute-start = (f32[16,136,128]{2,1,0:T(8,128)}, f32[16,136,128]{2,1,0:T(8,128)}, u32[]{:S(2)}, u32[]{:S(2)}) collective-permute-start(f32[16,136,128]{2,1,0:T(8,128)} %pad_maximum_fusion.1), channel_id=1, source_target_pairs={{0,4},{4,8},{8,12},{12,16},{16,20},{20,24},{24,28},{1,5},{5,9},{9,... | collective-permute-start | bytes 3342344 | tf_op jit(solution)/shard_map/ppermute | solution.py:19
  23.5 3.0 copy-start.2
  23.5 3.0 copy-start.25
  23.5 3.0 copy-start.26
  39.3 13.8 %copy-start.24 = (pred[512,512]{1,0:T(8,128)(4,1)}, pred[512,512]{1,0:T(8,128)(4,1)S(1)}, u32[]{:S(2)}) copy-start(pred[512,512]{1,0:T(8,128)(4,1)S(1)} %iota_compare_fusion) | copy-start | bytes 786436
  39.3 13.8 %copy-start.3 = (bf16[64,8,16,128]{3,2,1,0:T(8,128)(2,1)S(1)}, bf16[64,8,16,128]{3,2,1,0:T(8,128)(2,1)}, u32[]{:S(2)}) copy-start(bf16[64,8,16,128]{3,2,1,0:T(8,128)(2,1)} %copy-done.2) | copy-start | bytes 6291460
  39.3 13.8 %copy-start.11 = (bf16[1,512,2048]{1,2,0:T(8,128)(2,1)S(1)}, bf16[1,512,2048]{1,2,0:T(8,128)(2,1)}, u32[]{:S(2)}) copy-start(bf16[1,512,2048]{1,2,0:T(8,128)(2,1)} %copy-done.10) | copy-start | bytes 6291460
  49.9 26.4 %collective-permute-start.1 = (f32[16,136,128]{2,1,0:T(8,128)S(1)}, f32[16,136,128]{2,1,0:T(8,128)S(1)}, u32[]{:S(2)}, u32[]{:S(2)}) collective-permute-start(f32[16,136,128]{2,1,0:T(8,128)S(1)} %pad_maximum_fusion.2), channel_id=1, source_target_pairs={{0,8},{4,12},{8,16},{12,20},{16,24},{20,28},{1,9},{5,13},{9,17},{1... | collective-permute-start | bytes 3342344 | tf_op jit(solution)/shard_map/ppermute | solution.py:19
  77.3 5.7 %copy-start.19 = (bf16[512,16,128]{0,2,1:T(8,128)(2,1)S(1)}, bf16[512,16,128]{0,2,1:T(8,128)(2,1)}, u32[]{:S(2)}) copy-start(bf16[512,16,128]{0,2,1:T(8,128)(2,1)} %copy.102) | copy-start | bytes 6291460
  77.7 52.4 %collective-permute-start.2 = (f32[16,136,128]{2,1,0:T(8,128)S(1)}, f32[16,136,128]{2,1,0:T(8,128)}, u32[]{:S(2)}, u32[]{:S(2)}) collective-permute-start(f32[16,136,128]{2,1,0:T(8,128)S(1)} %pad_maximum_fusion.3), channel_id=1, source_target_pairs={{0,16},{4,20},{8,24},{12,28},{1,17},{5,21},{9,25},{13,29},{2,18},{... | collective-permute-start | bytes 3342344 | tf_op jit(solution)/shard_map/ppermute | solution.py:19
  83.8 1.7 copy-start.7
  133.2 1.7 copy-start.27
  143.1 4.7 %copy-start.8 = (bf16[64,8,16,128]{3,2,1,0:T(8,128)(2,1)S(1)}, bf16[64,8,16,128]{3,2,1,0:T(8,128)(2,1)}, u32[]{:S(2)}) copy-start(bf16[64,8,16,128]{3,2,1,0:T(8,128)(2,1)} %copy-done.6) | copy-start | bytes 6291460
  144.6 38.5 %copy-start.20 = (f32[16,128,128]{2,1,0:T(8,128)S(1)}, f32[16,128,128]{2,1,0:T(8,128)}, u32[]{:S(2)}) copy-start(f32[16,128,128]{2,1,0:T(8,128)} %fusion.29) | copy-start | bytes 3145732
  144.6 38.3 %collective-permute-start.3 = (f32[16,136,128]{2,1,0:T(8,128)S(1)}, f32[16,136,128]{2,1,0:T(8,128)S(1)}, u32[]{:S(2)}, u32[]{:S(2)}) collective-permute-start(f32[16,136,128]{2,1,0:T(8,128)S(1)} %pad_maximum_fusion), channel_id=1, source_target_pairs={{4,0},{8,4},{12,8},{16,12},{20,16},{24,20},{28,24},{5,1},{9,5},{13... | collective-permute-start | bytes 3342344 | tf_op jit(solution)/shard_map/ppermute | solution.py:19
  155.7 32.5 %copy-start.5 = (bf16[16,512,512]{2,1,0:T(8,128)(2,1)}, bf16[16,512,512]{2,1,0:T(8,128)(2,1)S(1)}, u32[]{:S(2)}) copy-start(bf16[16,512,512]{2,1,0:T(8,128)(2,1)S(1)} %multiply_convert_fusion.1) | copy-start | bytes 25165828
  182.8 1.0 copy-start.21
  183.1 5.1 %copy-start.4 = (bf16[64,8,16,128]{3,2,1,0:T(8,128)(2,1)S(1)}, bf16[64,8,16,128]{3,2,1,0:T(8,128)(2,1)}, u32[]{:S(2)}) copy-start(bf16[64,8,16,128]{3,2,1,0:T(8,128)(2,1)} %copy-done.2) | copy-start | bytes 6291460
  183.2 1.0 copy-start.17
  184.2 34.9 %slice-start = ((s8[8388608]{0:T(1024)(128)(4,1)}), s8[4194304]{0:T(1024)(128)(4,1)S(1)}, s32[]{:S(2)}) async-start(s8[8388608]{0:T(1024)(128)(4,1)} %bitcast.114), calls=%async_computation.2 | async-start | bytes 8388608
  185.3 6.6 %copy-start.12 = (bf16[1,512,2048]{1,2,0:T(8,128)(2,1)S(1)}, bf16[1,512,2048]{1,2,0:T(8,128)(2,1)}, u32[]{:S(2)}) copy-start(bf16[1,512,2048]{1,2,0:T(8,128)(2,1)} %copy-done.10) | copy-start | bytes 6291460
  185.3 33.9 %slice-start.1 = ((s8[8388608]{0:T(1024)(128)(4,1)}), s8[4194304]{0:T(1024)(128)(4,1)S(1)}, s32[]{:S(2)}) async-start(s8[8388608]{0:T(1024)(128)(4,1)} %bitcast.114), calls=%async_computation.3 | async-start | bytes 8388608
  185.3 28.9 %collective-permute-start.4 = (f32[16,136,128]{2,1,0:T(8,128)}, f32[16,136,128]{2,1,0:T(8,128)}, u32[]{:S(2)}, u32[]{:S(2)}) collective-permute-start(f32[16,136,128]{2,1,0:T(8,128)} %pad_maximum_fusion.4), channel_id=1, source_target_pairs={{8,0},{12,4},{16,8},{20,12},{24,16},{28,20},{9,1},{13,5},{17,9},{2... | collective-permute-start | bytes 3342344 | tf_op jit(solution)/shard_map/ppermute | solution.py:19
  191.9 23.4 %copy-start.18 = (f32[16,128,128]{2,1,0:T(8,128)S(1)}, f32[16,128,128]{2,1,0:T(8,128)}, u32[]{:S(2)}) copy-start(f32[16,128,128]{2,1,0:T(8,128)} %copy-done.17) | copy-start | bytes 3145732
  217.9 27.0 %collective-permute-start.5 = (f32[16,136,128]{2,1,0:T(8,128)}, f32[16,136,128]{2,1,0:T(8,128)}, u32[]{:S(2)}, u32[]{:S(2)}) collective-permute-start(f32[16,136,128]{2,1,0:T(8,128)} %pad_maximum_fusion.5), channel_id=1, source_target_pairs={{16,0},{20,4},{24,8},{28,12},{17,1},{21,5},{25,9},{29,13},{18,2},{... | collective-permute-start | bytes 3342344 | tf_op jit(solution)/shard_map/ppermute | solution.py:19
  222.4 2.2 copy-start.16
  226.9 18.0 %copy-start.22 = (f32[16,136,128]{2,1,0:T(8,128)S(1)}, f32[16,136,128]{2,1,0:T(8,128)}, u32[]{:S(2)}) copy-start(f32[16,136,128]{2,1,0:T(8,128)} %copy-done.21) | copy-start | bytes 3342340
  244.9 2.3 copy-start.13
  247.2 2.3 copy-start.15
  251.7 4.1 %copy-start.9 = (bf16[64,8,16,128]{3,2,1,0:T(8,128)(2,1)S(1)}, bf16[64,8,16,128]{3,2,1,0:T(8,128)(2,1)}, u32[]{:S(2)}) copy-start(bf16[64,8,16,128]{3,2,1,0:T(8,128)(2,1)} %copy-done.6) | copy-start | bytes 6291460
  255.7 2.2 copy-start.14
  260.9 113.8 %copy-start.1 = (f32[1,512,16]{1,2,0:T(8,128)S(1)}, f32[1,512,16]{1,2,0:T(8,128)}, u32[]{:S(2)}) copy-start(f32[1,512,16]{1,2,0:T(8,128)} %param.13) | copy-start | bytes 98308
Sparse Core Ops, SparseCore 0:
  143.2 231.4 reduce-scatter.1

commit v6 on v2

--- a/solution.py
+++ b/solution.py
@@ -8,21 +8,25 @@
 BLOCK = 512
 
 
-def carried_in(value, axis, join, backward):
-    count = lax.axis_size(axis)
-    step = -1 if backward else 1
+def carried_in(value, join, heading):
+    count, groups = lax.axis_size("ctx"), lax.axis_size("dp")
     partial = value
     gathered = None
     distance = 1
     while distance < count:
-        pairs = [(i, i + step * distance) for i in range(count) if 0 <= i + step * distance < count]
-        arrived = jax.tree.map(lambda part: lax.ppermute(part, axis, pairs), partial)
+        pairs = []
+        for place in range(count):
+            for group in range(groups):
+                step = heading[group % 2] * distance
+                if step != 0 and 0 <= place + step < count:
+                    pairs.append((place * groups + group, (place + step) * groups + group))
+        arrived = lax.ppermute(partial, ("ctx", "dp"), pairs)
         gathered = arrived if gathered is None else join(arrived, gathered)
         if distance * 2 < count:
             partial = join(arrived, partial)
         distance *= 2
     if gathered is None:
-        gathered = jax.tree.map(jnp.zeros_like, value)
+        gathered = jnp.zeros_like(value)
     return gathered
 
 
@@ -69,7 +73,6 @@
     state_end = jnp.einsum(
         "shd,she->hde", key_f32 * remain, value_f32, precision=lax.Precision.HIGHEST
     )
-    state_in = carried_in(pack_state(total, state_end), "ctx", packed_join, False)[:, :HD]
     state_end, upstream, query_heads = lax.optimization_barrier((state_end, upstream, query_heads))
 
     advantage = (2 * signs[0] - 1).astype(jnp.float32) * magnitude[0]
@@ -82,6 +85,13 @@
     back_end = jnp.einsum(
         "thd,the->hde", query_f32 * growth, dout_f32, precision=lax.Precision.HIGHEST
     )
+    even = lax.axis_index("dp") % 2 == 0
+    first = carried_in(
+        pack_state(total, jnp.where(even, state_end, back_end)), packed_join, (1, -1)
+    )[:, :HD]
+    state_end, first = lax.optimization_barrier((state_end, first))
+    second = carried_in(pack_state(total, state_end), packed_join, (0, 1))[:, :HD]
+    state_in = jnp.where(even, first, second)
 
     lower_mask = (jnp.arange(BLOCK)[:, None] >= jnp.arange(BLOCK)[None, :])[None]
     weight = decay_weights(running, lower_mask)
@@ -97,7 +107,8 @@
     )
     partial, back_end = lax.optimization_barrier((partial, back_end))
     grad_weight = lax.psum_scatter(partial, ("ctx", "dp"), scatter_dimension=0, tiled=True)
-    back_in = carried_in(pack_state(total, back_end), "ctx", packed_join, True)[:, :HD]
+    back_late = carried_in(pack_state(total, back_end), packed_join, (-1, 0))[:, :HD]
+    back_in = jnp.where(even, back_late, first)
 
     dscores = jnp.einsum(
         "thd,shd->hts", dout_heads, value_heads, preferred_element_type=jnp.float32

time: 378 us -> 392 us (1.037)
  starting transfers between devices: 19.2 us -> 30.4 us
  waiting for transfers between devices: 232 us -> 226 us
  matrix products: 69.7 us -> 75 us
    ppermute x6 -> x9, waiting for transfers between devices: 123 us -> 89.5 us  [carried_in(): arrived = lax.ppermute(partial, ('ctx', 'dp'), pairs)]
    reduce_scatter x1, waiting for transfers between devices: 109 us -> 136 us  [on_device(): lax.psum_scatter(partial, ('ctx', 'dp'), scatter_dimension=0, tiled=True)]
    ppermute x6 -> x9, starting transfers between devices: 19.2 us -> 30.4 us  [carried_in(): arrived = lax.ppermute(partial, ('ctx', 'dp'), pairs)]
    select_n x0 -> x2, other arithmetic: none -> 4.94 us  [the longest x1 2.63 us: on_device(): back_in = jnp.where(even, back_late, first)]
    unnamed x71 -> x65, local copies, waits for them, and re-layouts: 19.1 us -> 19.8 us
  transfers between devices with their start and end apart: 7 -> 10, of which waited for: 7 -> 7; matrix products, arithmetic and copies ran while one was open for 22% -> 17% of each run, Pallas kernels for 0% -> 0%
where the time goes in v6:
time: 392 us
  waiting for transfers between devices  226 us (58%)
  matrix products  75 us (19%)
  local copies, waits for them, and re-layouts  30.4 us (8%)
  starting transfers between devices  30.4 us (8%)
  other arithmetic  15.6 us (4%)
  between operations  14.6 us (4%)
    reduce_scatter x1, waiting for transfers between devices, on_device(): lax.psum_scatter(partial, ('ctx', 'dp'), scatter_dimension=0, tiled=True)  136 us
    ppermute x9, waiting for transfers between devices, carried_in(): arrived = lax.ppermute(partial, ('ctx', 'dp'), pairs)  89.5 us
    ppermute x9, starting transfers between devices, carried_in(): arrived = lax.ppermute(partial, ('ctx', 'dp'), pairs)  30.4 us
    unnamed x65, local copies, waits for them, and re-layouts  19.8 us
    dot_general x1, matrix products, on_device(): lax.dot_general(weighted, out_weight, (((1,), (1,)), ((), ())), preferred...  9.2 us
    dot_general x1, matrix products, on_device(): lax.dot_general(attn, weighted, (((0,), (0,)), ((), ())), preferred_eleme...  8.17 us
    dot_general x1, matrix products, on_device(): jnp.einsum('hts,shd->thd', probs, value_heads, preferred_element_type=jnp...  7.99 us
  transfers between devices with their start and end apart: 10, of which 7 were waited for; matrix products, arithmetic and copies ran while one was open for 17% of the time, Pallas kernels for 0%

profile of v6, /device:TPU:11, one launch (start us, length us, event | category | flops | bytes accessed | tf_op | source)
XLA Modules:
  0.0 391.6 jit_solution(12416328367085531515)
XLA Ops:
  7.9 1.1 reduce-window.6
  9.6 2.2 copy.102
  11.9 2.9 copy.76
  14.8 3.9 %copy.97 = bf16[1,512,2048]{1,2,0:T(8,128)(2,1)} copy(bf16[1,512,2048]{2,1,0:T(8,128)(2,1)} %param.9) | data formatting | bytes 4194304 | tf_op jit(solution)/shard_map/reshape;squeeze | solution.py:59
  18.7 2.4 copy.101
  21.1 2.8 fusion.14
  24.0 9.2 %convolution_convert_fusion = bf16[512,2048]{1,0:T(8,128)(2,1)} fusion(bf16[2048,2048]{1,0:T(8,128)(2,1)} %param.12, bf16[1,512,2048]{2,1,0:T(8,128)(2,1)S(1)} %copy-done.26, f32[512]{0:T(512)S(1)} %bitcast.132), kind=kOutput, calls=%fused_computation.26 | convolution fusion | flops 4299161600 | bytes 12584960 | tf_op jit(solution)/shard_map/dot_general | solution.py:80
  33.2 2.9 copy.98
  36.0 4.8 %broadcast_select_fusion = (f32[16,128,128]{2,1,0:T(8,128)S(1)}, f32[16,128,128]{2,1,0:T(8,128)}) fusion(f32[16,128,128]{2,1,0:T(8,128)S(1)} %fusion.14, pred[]{:T(512)S(6)} %eq.5, bf16[512,16,128]{0,2,1:T(8,128)(2,1)S(1)} %bitcast.108, bf16[512,16,128]{0,2,1:T(8,128)(2,1)} %copy.76, f32[512,16]{0,1:T(8,128)S(1)} %get-tuple-element.42), kind=kOutput, calls=%fused_computation.65 | convolution fusion | flops 1612972032 | bytes 7372801 | tf_op jit(solution)/shard_map/thd,the->hde/dot_general | solution.py:85
  41.0 2.2 collective-permute-start
  43.2 24.3 %collective-permute-done = f32[16,136,128]{2,1,0:T(8,128)S(1)} collective-permute-done((f32[16,136,128]{2,1,0:T(8,128)S(1)}, f32[16,136,128]{2,1,0:T(8,128)S(1)}, u32[]{:S(2)}, u32[]{:S(2)}) %collective-permute-start) | collective-permute-done | bytes 1114144 | tf_op jit(solution)/shard_map/ppermute | solution.py:23
  68.1 1.9 collective-permute-start.1
  70.1 14.6 %collective-permute-done.1 = f32[16,136,128]{2,1,0:T(8,128)S(1)} collective-permute-done((f32[16,136,128]{2,1,0:T(8,128)S(1)}, f32[16,136,128]{2,1,0:T(8,128)S(1)}, u32[]{:S(2)}, u32[]{:S(2)}) %collective-permute-start.1) | collective-permute-done | bytes 1114144 | tf_op jit(solution)/shard_map/ppermute | solution.py:23
  85.2 1.3 collective-permute-start.2
  86.5 15.9 %collective-permute-done.2 = f32[16,136,128]{2,1,0:T(8,128)S(1)} collective-permute-done((f32[16,136,128]{2,1,0:T(8,128)S(1)}, f32[16,136,128]{2,1,0:T(8,128)S(1)}, u32[]{:S(2)}, u32[]{:S(2)}) %collective-permute-start.2) | collective-permute-done | bytes 1114144 | tf_op jit(solution)/shard_map/ppermute | solution.py:23
  102.8 13.5 %collective-permute-start.3 = (f32[16,136,128]{2,1,0:T(8,128)S(1)}, f32[16,136,128]{2,1,0:T(8,128)S(1)}, u32[]{:S(2)}, u32[]{:S(2)}) collective-permute-start(f32[16,136,128]{2,1,0:T(8,128)S(1)} %pad_maximum_fusion.1), channel_id=1, source_target_pairs={{1,5},{3,7},{5,9},{7,11},{9,13},{11,15},{13,17},{15,19},{17,21},{1... | collective-permute-start | bytes 3342344 | tf_op jit(solution)/shard_map/ppermute | solution.py:23
  116.3 12.5 %collective-permute-done.3 = f32[16,136,128]{2,1,0:T(8,128)S(1)} collective-permute-done((f32[16,136,128]{2,1,0:T(8,128)S(1)}, f32[16,136,128]{2,1,0:T(8,128)S(1)}, u32[]{:S(2)}, u32[]{:S(2)}) %collective-permute-start.3) | collective-permute-done | bytes 1114144 | tf_op jit(solution)/shard_map/ppermute | solution.py:23
  129.4 3.2 collective-permute-start.4
  132.7 12.9 %collective-permute-done.4 = f32[16,136,128]{2,1,0:T(8,128)S(1)} collective-permute-done((f32[16,136,128]{2,1,0:T(8,128)S(1)}, f32[16,136,128]{2,1,0:T(8,128)S(1)}, u32[]{:S(2)}, u32[]{:S(2)}) %collective-permute-start.4) | collective-permute-done | bytes 1114144 | tf_op jit(solution)/shard_map/ppermute | solution.py:23
  146.6 3.9 %collective-permute-start.5 = (f32[16,136,128]{2,1,0:T(8,128)S(1)}, f32[16,136,128]{2,1,0:T(8,128)}, u32[]{:S(2)}, u32[]{:S(2)}) collective-permute-start(f32[16,136,128]{2,1,0:T(8,128)S(1)} %pad_maximum_fusion.6), channel_id=1, source_target_pairs={{1,17},{3,19},{5,21},{7,23},{9,25},{11,27},{13,29},{15,31}} | collective-permute-start | bytes 3342344 | tf_op jit(solution)/shard_map/ppermute | solution.py:23
  150.5 6.2 %multiply_convert_fusion = bf16[16,512,512]{2,1,0:T(8,128)(2,1)S(1)} fusion(bf16[512,16,128]{0,2,1:T(8,128)(2,1)S(1)} %bitcast.116, f32[16,512]{1,0:T(8,128)S(1)} %get-tuple-element.47, pred[512,512]{1,0:T(8,128)(4,1)S(1)} %iota_compare_fusion, bf16[512,16,128]{2,1,0:T(8,128)(2,1)S(1)} %bitcast.113), kind=kOutput, calls=%fused_computation | convolution fusion | flops 1098907648 | bytes 12877824 | tf_op jit(solution)/shard_map/thd,shd->hts/dot_general | solution.py:98
  156.7 8.0 %fusion.28 = f32[16,512,128]{1,2,0:T(8,128)} fusion(bf16[16,512,512]{2,1,0:T(8,128)(2,1)S(1)} %multiply_convert_fusion, bf16[512,16,128]{2,1,0:T(8,128)(2,1)} %bitcast.120), kind=kOutput, calls=%fused_computation.39 | convolution fusion | flops 1073741824 | bytes 14680064 | tf_op jit(solution)/shard_map/hts,shd->thd/dot_general | solution.py:100
  164.7 9.2 %collective-permute-done.5 = f32[16,136,128]{2,1,0:T(8,128)} collective-permute-done((f32[16,136,128]{2,1,0:T(8,128)S(1)}, f32[16,136,128]{2,1,0:T(8,128)}, u32[]{:S(2)}, u32[]{:S(2)}) %collective-permute-start.5) | collective-permute-done | bytes 1114144 | tf_op jit(solution)/shard_map/ppermute | solution.py:23
  173.9 2.3 fusion.36
  176.4 4.4 %fusion.8 = bf16[512,16,128]{0,2,1:T(8,128)(2,1)S(1)} fusion(f32[16,512,128]{1,2,0:T(8,128)} %fusion.28, f32[16,128,128]{2,1,0:T(8,128)S(1)} %fusion.36, bf16[512,16,128]{0,2,1:T(8,128)(2,1)S(1)} %copy-done.14, f32[512,16]{0,1:T(8,128)S(1)} %get-tuple-element.41), kind=kOutput, calls=%fused_computation.16 | convolution fusion | flops 1613758464 | bytes 9469952 | tf_op jit(solution)/shard_map/thd,hde->the/dot_general | solution.py:101
  180.8 8.2 %fusion.18 = f32[2048,2048]{1,0:T(8,128)} fusion(bf16[512,2048]{0,1:T(8,128)(2,1)S(1)} %bitcast.128, bf16[1,512,2048]{2,1,0:T(8,128)(2,1)S(1)} %copy-done.27, f32[512]{0:T(512)S(1)} %bitcast.133), kind=kOutput, calls=%fused_computation.28 | convolution fusion | flops 4298113024 | bytes 20973568 | tf_op jit(solution)/shard_map/dot_general | solution.py:105
  189.0 1.4 pad_maximum_fusion
  190.4 0.7 collective-permute-start.6
  191.7 0.9 copy-done.16
  192.6 1.1 pad_maximum_fusion.7
  193.6 1.8 collective-permute-start.7
  195.5 6.9 %multiply_convert_fusion.1 = bf16[16,512,512]{2,1,0:T(8,128)(2,1)S(1)} fusion(bf16[512,16,128]{0,2,1:T(8,128)(2,1)S(1)} %bitcast.109, f32[16,512]{1,0:T(8,128)S(1)} %get-tuple-element.47, pred[512,512]{1,0:T(8,128)(4,1)S(1)} %copy-done.23, bf16[512,16,128]{2,1,0:T(8,128)(2,1)S(1)} %bitcast.121), kind=kOutput, calls=%fused_computation.1 | convolution fusion | flops 1098907648 | bytes 12877824 | tf_op jit(solution)/shard_map/thd,shd->hts/dot_general | solution.py:113
  202.5 4.8 %fusion.43 = f32[16,512,128]{1,2,0:T(8,128)} fusion(bf16[16,512,512]{2,1,0:T(8,128)(2,1)S(1)} %multiply_convert_fusion.1, bf16[512,16,128]{0,2,1:T(8,128)(2,1)S(1)} %bitcast.117), kind=kOutput, calls=%fused_computation.93 | convolution fusion | flops 1073741824 | bytes 14680064 | tf_op jit(solution)/shard_map/hts,shd->thd/dot_general | solution.py:117
  207.2 1.1 exponential_reduce_fusion.1
  208.3 1.9 multiply_add_fusion
  210.3 1.1 pad_maximum_fusion.8
  211.4 1.8 collective-permute-start.8
  213.2 3.5 fusion.25
  216.7 3.2 fusion.44
  219.9 3.5 fusion.10
  223.4 4.1 %copy.92 = bf16[1,512,2048]{2,1,0:T(8,128)(2,1)} copy(bf16[1,512,2048]{1,2,0:T(8,128)(2,1)} %bitcast.123) | data formatting | bytes 4194304
  227.5 2.6 fusion.34
  230.1 0.9 copy-done.3
  231.0 3.9 %fusion.6 = bf16[512,16,128]{0,2,1:T(8,128)(2,1)} fusion(f32[16,128,512]{2,1,0:T(8,128)S(1)} %copy-done.3, f32[16,128,128]{2,1,0:T(8,128)S(1)} %fusion.34, f32[512,16]{0,1:T(8,128)S(1)} %get-tuple-element.43, bf16[512,16,128]{2,1,0:T(8,128)(2,1)S(1)} %bitcast.122), kind=kOutput, calls=%fused_computation.13 | convolution fusion | flops 1613758464 | bytes 9469952 | tf_op jit(solution)/shard_map/hde,she->shd/dot_general | solution.py:123
  234.9 4.1 %copy.93 = bf16[1,512,2048]{2,1,0:T(8,128)(2,1)} copy(bf16[1,512,2048]{1,2,0:T(8,128)(2,1)} %bitcast.125) | data formatting | bytes 4194304
  239.0 5.6 %fusion.4 = bf16[512,16,128]{0,2,1:T(8,128)(2,1)} fusion(f32[16,128,512]{2,1,0:T(8,128)} %fusion.44, f32[16,128,128]{2,1,0:T(8,128)S(1)} %fusion.34, bf16[512,16,128]{0,2,1:T(8,128)(2,1)S(1)} %bitcast.118, f32[512,16]{0,1:T(8,128)S(1)} %get-tuple-element.43), kind=kOutput, calls=%fused_computation.10 | convolution fusion | flops 1613758464 | bytes 9469952 | tf_op jit(solution)/shard_map/hde,shd->she/dot_general | solution.py:126
  244.6 3.9 %copy.94 = bf16[1,512,2048]{2,1,0:T(8,128)(2,1)} copy(bf16[1,512,2048]{1,2,0:T(8,128)(2,1)} %bitcast.124) | data formatting | bytes 4194304
  248.6 136.2 %reduce-scatter.2.cloned.1.call-done = f32[64,2048]{1,0:T(8,128)} async-done(((f32[2048,2048]{1,0:T(8,128)}), f32[64,2048]{1,0:T(8,128)}) %reduce-scatter.2.cloned.1.call-update) | async-done | bytes 524304 | tf_op jit(solution)/shard_map/reduce_scatter | solution.py:109
  (101 shorter events, 5.4 us)
Async XLA Ops:
  7.2 0.8 copy-start
  7.2 377.6 %reduce-scatter.2.cloned.1.call-start = ((), (), s32[]{:S(2)}) async-start(), calls=%async_computation.1 | async-start | bytes 17301504 | tf_op jit(solution)/shard_map/reduce_scatter | solution.py:109
  11.8 2.9 copy-start.4
  18.7 2.4 copy-start.7
  21.1 2.8 copy-start.11
  21.1 2.8 copy-start.24
  21.1 2.8 copy-start.25
  21.1 2.8 copy-start.26
  41.0 26.5 %collective-permute-start = (f32[16,136,128]{2,1,0:T(8,128)S(1)}, f32[16,136,128]{2,1,0:T(8,128)S(1)}, u32[]{:S(2)}, u32[]{:S(2)}) collective-permute-start(f32[16,136,128]{2,1,0:T(8,128)S(1)} %pad_maximum_fusion.2), channel_id=1, source_target_pairs={{0,4},{2,6},{4,8},{5,1},{6,10},{7,3},{8,12},{9,5},{10,14},{11,7},{... | collective-permute-start | bytes 3342344 | tf_op jit(solution)/shard_map/ppermute | solution.py:23
  68.1 16.5 %collective-permute-start.1 = (f32[16,136,128]{2,1,0:T(8,128)S(1)}, f32[16,136,128]{2,1,0:T(8,128)S(1)}, u32[]{:S(2)}, u32[]{:S(2)}) collective-permute-start(f32[16,136,128]{2,1,0:T(8,128)S(1)} %pad_maximum_fusion.3), channel_id=1, source_target_pairs={{0,8},{2,10},{4,12},{6,14},{8,16},{9,1},{10,18},{11,3},{12,20},{13... | collective-permute-start | bytes 3342344 | tf_op jit(solution)/shard_map/ppermute | solution.py:23
  85.2 17.2 %collective-permute-start.2 = (f32[16,136,128]{2,1,0:T(8,128)S(1)}, f32[16,136,128]{2,1,0:T(8,128)S(1)}, u32[]{:S(2)}, u32[]{:S(2)}) collective-permute-start(f32[16,136,128]{2,1,0:T(8,128)S(1)} %pad_maximum_fusion.4), channel_id=1, source_target_pairs={{0,16},{2,18},{4,20},{6,22},{8,24},{10,26},{12,28},{14,30},{17,1},... | collective-permute-start | bytes 3342344 | tf_op jit(solution)/shard_map/ppermute | solution.py:23
  102.7 71.1 %copy-start.17 = (f32[16,128,128]{2,1,0:T(8,128)}, f32[16,128,128]{2,1,0:T(8,128)S(1)}, u32[]{:S(2)}) copy-start(f32[16,128,128]{2,1,0:T(8,128)S(1)} %fusion.37) | copy-start | bytes 3145732
  102.8 25.9 %collective-permute-start.3 = (f32[16,136,128]{2,1,0:T(8,128)S(1)}, f32[16,136,128]{2,1,0:T(8,128)S(1)}, u32[]{:S(2)}, u32[]{:S(2)}) collective-permute-start(f32[16,136,128]{2,1,0:T(8,128)S(1)} %pad_maximum_fusion.1), channel_id=1, source_target_pairs={{1,5},{3,7},{5,9},{7,11},{9,13},{11,15},{13,17},{15,19},{17,21},{1... | collective-permute-start | bytes 3342344 | tf_op jit(solution)/shard_map/ppermute | solution.py:23
  128.8 16.8 %copy-start.20 = (f32[16,136,128]{2,1,0:T(8,128)}, f32[16,136,128]{2,1,0:T(8,128)S(1)}, u32[]{:S(2)}) copy-start(f32[16,136,128]{2,1,0:T(8,128)S(1)} %collective-permute-done.3) | copy-start | bytes 3342340
  129.4 16.2 %collective-permute-start.4 = (f32[16,136,128]{2,1,0:T(8,128)S(1)}, f32[16,136,128]{2,1,0:T(8,128)S(1)}, u32[]{:S(2)}, u32[]{:S(2)}) collective-permute-start(f32[16,136,128]{2,1,0:T(8,128)S(1)} %pad_maximum_fusion.5), channel_id=1, source_target_pairs={{1,9},{3,11},{5,13},{7,15},{9,17},{11,19},{13,21},{15,23},{17,25},... | collective-permute-start | bytes 3342344 | tf_op jit(solution)/shard_map/ppermute | solution.py:23
  132.7 17.8 %copy-start.22 = (pred[512,512]{1,0:T(8,128)(4,1)}, pred[512,512]{1,0:T(8,128)(4,1)S(1)}, u32[]{:S(2)}) copy-start(pred[512,512]{1,0:T(8,128)(4,1)S(1)} %iota_compare_fusion) | copy-start | bytes 786436
  145.6 1.0 copy-start.21
  145.8 4.7 %copy-start.5 = (bf16[64,8,16,128]{3,2,1,0:T(8,128)(2,1)S(1)}, bf16[64,8,16,128]{3,2,1,0:T(8,128)(2,1)}, u32[]{:S(2)}) copy-start(bf16[64,8,16,128]{3,2,1,0:T(8,128)(2,1)} %copy-done.4) | copy-start | bytes 6291460
  145.8 4.7 %copy-start.8 = (bf16[1,512,2048]{1,2,0:T(8,128)(2,1)S(1)}, bf16[1,512,2048]{1,2,0:T(8,128)(2,1)}, u32[]{:S(2)}) copy-start(bf16[1,512,2048]{1,2,0:T(8,128)(2,1)} %copy.97) | copy-start | bytes 6291460
  146.6 27.3 %collective-permute-start.5 = (f32[16,136,128]{2,1,0:T(8,128)S(1)}, f32[16,136,128]{2,1,0:T(8,128)}, u32[]{:S(2)}, u32[]{:S(2)}) collective-permute-start(f32[16,136,128]{2,1,0:T(8,128)S(1)} %pad_maximum_fusion.6), channel_id=1, source_target_pairs={{1,17},{3,19},{5,21},{7,23},{9,25},{11,27},{13,29},{15,31}} | collective-permute-start | bytes 3342344 | tf_op jit(solution)/shard_map/ppermute | solution.py:23
  156.7 8.0 %copy-start.2 = (bf16[16,512,512]{2,1,0:T(8,128)(2,1)}, bf16[16,512,512]{2,1,0:T(8,128)(2,1)S(1)}, u32[]{:S(2)}) copy-start(bf16[16,512,512]{2,1,0:T(8,128)(2,1)S(1)} %multiply_convert_fusion) | copy-start | bytes 25165828
  173.9 2.5 copy-start.14
  176.4 4.4 %copy-start.27 = (bf16[1,512,2048]{2,1,0:T(8,128)(2,1)S(1)}, bf16[1,512,2048]{2,1,0:T(8,128)(2,1)}, u32[]{:S(2)}) copy-start(bf16[1,512,2048]{2,1,0:T(8,128)(2,1)} %param.11) | copy-start | bytes 6291460
  189.0 2.4 copy-start.18
  190.4 0.7 collective-permute-start.6
  191.2 2.5 copy-start.19
  191.4 4.1 %copy-start.12 = (bf16[64,8,16,128]{3,2,1,0:T(8,128)(2,1)S(1)}, bf16[64,8,16,128]{3,2,1,0:T(8,128)(2,1)}, u32[]{:S(2)}) copy-start(bf16[64,8,16,128]{3,2,1,0:T(8,128)(2,1)} %copy-done.11) | copy-start | bytes 6291460
  191.4 4.1 %copy-start.23 = (pred[512,512]{1,0:T(8,128)(4,1)S(1)}, pred[512,512]{1,0:T(8,128)(4,1)}, u32[]{:S(2)}) copy-start(pred[512,512]{1,0:T(8,128)(4,1)} %copy-done.22) | copy-start | bytes 786436
  191.6 1.0 copy-start.16
  193.6 8.8 %copy-start.9 = (bf16[1,512,2048]{1,2,0:T(8,128)(2,1)S(1)}, bf16[1,512,2048]{1,2,0:T(8,128)(2,1)}, u32[]{:S(2)}) copy-start(bf16[1,512,2048]{1,2,0:T(8,128)(2,1)} %copy.97) | copy-start | bytes 6291460
  193.6 13.6 %collective-permute-start.7 = (f32[16,136,128]{2,1,0:T(8,128)}, f32[16,136,128]{2,1,0:T(8,128)}, u32[]{:S(2)}, u32[]{:S(2)}) collective-permute-start(f32[16,136,128]{2,1,0:T(8,128)} %pad_maximum_fusion.7), channel_id=1, source_target_pairs={{8,0},{10,2},{12,4},{14,6},{16,8},{18,10},{20,12},{22,14},{24,16},... | collective-permute-start | bytes 3342344 | tf_op jit(solution)/shard_map/ppermute | solution.py:23
  208.3 4.9 %copy-start.6 = (bf16[64,8,16,128]{3,2,1,0:T(8,128)(2,1)S(1)}, bf16[64,8,16,128]{3,2,1,0:T(8,128)(2,1)}, u32[]{:S(2)}) copy-start(bf16[64,8,16,128]{3,2,1,0:T(8,128)(2,1)} %copy-done.4) | copy-start | bytes 6291460
  210.3 6.4 %slice-start = ((s8[8388608]{0:T(1024)(128)(4,1)}), s8[4194304]{0:T(1024)(128)(4,1)S(1)}, s32[]{:S(2)}) async-start(s8[8388608]{0:T(1024)(128)(4,1)} %bitcast.106), calls=%async_computation.2 | async-start | bytes 8388608
  211.4 5.4 %slice-start.1 = ((s8[8388608]{0:T(1024)(128)(4,1)}), s8[4194304]{0:T(1024)(128)(4,1)S(1)}, s32[]{:S(2)}) async-start(s8[8388608]{0:T(1024)(128)(4,1)} %bitcast.106), calls=%async_computation.3 | async-start | bytes 8388608
  211.4 16.1 %collective-permute-start.8 = (f32[16,136,128]{2,1,0:T(8,128)}, f32[16,136,128]{2,1,0:T(8,128)}, u32[]{:S(2)}, u32[]{:S(2)}) collective-permute-start(f32[16,136,128]{2,1,0:T(8,128)} %pad_maximum_fusion.8), channel_id=1, source_target_pairs={{16,0},{18,2},{20,4},{22,6},{24,8},{26,10},{28,12},{30,14}} | collective-permute-start | bytes 3342344 | tf_op jit(solution)/shard_map/ppermute | solution.py:23
  216.7 3.2 copy-start.15
  223.4 6.7 %copy-start.13 = (bf16[64,8,16,128]{3,2,1,0:T(8,128)(2,1)S(1)}, bf16[64,8,16,128]{3,2,1,0:T(8,128)(2,1)}, u32[]{:S(2)}) copy-start(bf16[64,8,16,128]{3,2,1,0:T(8,128)(2,1)} %copy-done.11) | copy-start | bytes 6291460
  227.5 3.5 copy-start.3
  234.9 4.1 %copy-start.10 = (bf16[1,512,2048]{1,2,0:T(8,128)(2,1)S(1)}, bf16[1,512,2048]{1,2,0:T(8,128)(2,1)}, u32[]{:S(2)}) copy-start(bf16[1,512,2048]{1,2,0:T(8,128)(2,1)} %copy.97) | copy-start | bytes 6291460
  244.6 140.1 %copy-start.1 = (f32[1,512,16]{1,2,0:T(8,128)S(1)}, f32[1,512,16]{1,2,0:T(8,128)}, u32[]{:S(2)}) copy-start(f32[1,512,16]{1,2,0:T(8,128)} %param.13) | copy-start | bytes 98308
Sparse Core Ops, SparseCore 0:
  189.1 195.5 reduce-scatter.1

commit v7 on v2

--- a/solution.py
+++ b/solution.py
@@ -67,7 +67,7 @@
     value_f32 = value_heads.astype(jnp.float32)
 
     state_end = jnp.einsum(
-        "shd,she->hde", key_f32 * remain, value_f32, precision=lax.Precision.HIGHEST
+        "shd,she->hde", key_f32 * remain, value_f32, precision=lax.Precision.HIGH
     )
     state_in = carried_in(pack_state(total, state_end), "ctx", packed_join, False)[:, :HD]
     state_end, upstream, query_heads = lax.optimization_barrier((state_end, upstream, query_heads))
@@ -80,7 +80,7 @@
     dout_heads = to_heads(dout)
     dout_f32 = dout_heads.astype(jnp.float32)
     back_end = jnp.einsum(
-        "thd,the->hde", query_f32 * growth, dout_f32, precision=lax.Precision.HIGHEST
+        "thd,the->hde", query_f32 * growth, dout_f32, precision=lax.Precision.HIGH
     )
 
     lower_mask = (jnp.arange(BLOCK)[:, None] >= jnp.arange(BLOCK)[None, :])[None]
@@ -89,7 +89,7 @@
     probs = (scale * scores * weight).astype(jnp.bfloat16)
     attend = jnp.einsum("hts,shd->thd", probs, value_heads, preferred_element_type=jnp.float32)
     attend = attend + scale * growth * jnp.einsum(
-        "thd,hde->the", query_f32, state_in, precision=lax.Precision.HIGHEST
+        "thd,hde->the", query_f32, state_in, precision=lax.Precision.HIGH
     )
     attn = attend.reshape(tokens, width).astype(jnp.bfloat16)
     partial = lax.dot_general(
@@ -107,13 +107,13 @@
     grad_k = jnp.einsum("hts,thd->shd", dprobs, query_heads, preferred_element_type=jnp.float32)
     grad_v = jnp.einsum("hts,thd->shd", probs, dout_heads, preferred_element_type=jnp.float32)
     grad_q = grad_q + scale * growth * jnp.einsum(
-        "hde,the->thd", state_in, dout_f32, precision=lax.Precision.HIGHEST
+        "hde,the->thd", state_in, dout_f32, precision=lax.Precision.HIGH
     )
     grad_k = grad_k + scale * remain * jnp.einsum(
-        "hde,she->shd", back_in, value_f32, precision=lax.Precision.HIGHEST
+        "hde,she->shd", back_in, value_f32, precision=lax.Precision.HIGH
     )
     grad_v = grad_v + scale * remain * jnp.einsum(
-        "hde,shd->she", back_in, key_f32, precision=lax.Precision.HIGHEST
+        "hde,shd->she", back_in, key_f32, precision=lax.Precision.HIGH
     )
     shape_out = (1, tokens, width)
     return (

time: 378 us -> 377 us (level)
  matrix products: 69.7 us -> 65.6 us
where the time goes in v7:
time: 377 us; the launch traced here: 376 us
  waiting for transfers between devices  235 us (62%)
  matrix products  65.6 us (17%)
  local copies, waits for them, and re-layouts  28.5 us (8%)
  starting transfers between devices  19.2 us (5%)
  between operations  14.5 us (4%)
  other arithmetic  13.3 us (4%)
    ppermute x6, waiting for transfers between devices, carried_in(): lax.ppermute(part, axis, pairs)  125 us
    reduce_scatter x1, waiting for transfers between devices, on_device(): lax.psum_scatter(partial, ('ctx', 'dp'), scatter_dimension=0, tiled=True)  110 us
    unnamed x71, local copies, waits for them, and re-layouts  19.2 us
    ppermute x6, starting transfers between devices, carried_in(): lax.ppermute(part, axis, pairs)  19.2 us
    dot_general x1, matrix products, on_device(): lax.dot_general(attn, weighted, (((0,), (0,)), ((), ())), preferred_eleme...  8.26 us
    dot_general x1, matrix products, on_device(): jnp.einsum('thd,shd->hts', query_heads, key_heads, preferred_element_type...  7.89 us
  transfers between devices with their start and end apart: 7, of which 7 were waited for; matrix products, arithmetic and copies ran while one was open for 22% of the time, Pallas kernels for 0%

profile of v7, /device:TPU:11, one launch (start us, length us, event | category | flops | bytes accessed | tf_op | source)
XLA Modules:
  0.0 375.9 jit_solution(6125641999175208331)
XLA Ops:
  7.2 0.7 copy-done
  7.9 1.1 reduce-window.6
  9.6 2.9 copy.94
  12.5 3.0 copy.98
  15.5 2.0 fusion.14
  17.8 3.3 collective-permute-start
  21.1 0.6 copy.99
  21.9 23.3 %collective-permute-done = f32[16,136,128]{2,1,0:T(8,128)S(1)} collective-permute-done((f32[16,136,128]{2,1,0:T(8,128)S(1)}, f32[16,136,128]{2,1,0:T(8,128)S(1)}, u32[]{:S(2)}, u32[]{:S(2)}) %collective-permute-start) | collective-permute-done | bytes 1114144 | tf_op jit(solution)/shard_map/ppermute | solution.py:19
  45.8 3.5 collective-permute-start.1
  49.3 7.9 %multiply_convert_fusion = bf16[16,512,512]{2,1,0:T(8,128)(2,1)} fusion(bf16[512,16,128]{0,2,1:T(8,128)(2,1)S(1)} %bitcast.115, f32[16,512]{1,0:T(8,128)S(1)} %get-tuple-element.36, pred[512,512]{1,0:T(8,128)(4,1)S(1)} %iota_compare_fusion, bf16[512,16,128]{2,1,0:T(8,128)(2,1)S(1)} %bitcast.111), kind=kOutput, calls=%fused_computation | convolution fusion | flops 1098907648 | bytes 12877824 | tf_op jit(solution)/shard_map/thd,shd->hts/dot_general | solution.py:88
  57.2 15.3 %collective-permute-done.1 = f32[16,136,128]{2,1,0:T(8,128)S(1)} collective-permute-done((f32[16,136,128]{2,1,0:T(8,128)S(1)}, f32[16,136,128]{2,1,0:T(8,128)S(1)}, u32[]{:S(2)}, u32[]{:S(2)}) %collective-permute-start.1) | collective-permute-done | bytes 1114144 | tf_op jit(solution)/shard_map/ppermute | solution.py:19
  73.0 0.5 copy-done.20
  73.5 5.2 %collective-permute-start.2 = (f32[16,136,128]{2,1,0:T(8,128)S(1)}, f32[16,136,128]{2,1,0:T(8,128)}, u32[]{:S(2)}, u32[]{:S(2)}) collective-permute-start(f32[16,136,128]{2,1,0:T(8,128)S(1)} %pad_maximum_fusion.3), channel_id=1, source_target_pairs={{0,16},{4,20},{8,24},{12,28},{1,17},{5,21},{9,25},{13,29},{2,18},{... | collective-permute-start | bytes 3342344 | tf_op jit(solution)/shard_map/ppermute | solution.py:19
  78.7 5.8 %convolution_convert_fusion = bf16[512,2048]{1,0:T(8,128)(2,1)} fusion(bf16[2048,2048]{1,0:T(8,128)(2,1)S(1)} %bitcast.133, bf16[1,512,2048]{2,1,0:T(8,128)(2,1)S(1)} %copy-done.27, f32[512]{0:T(512)S(1)} %bitcast.130), kind=kOutput, calls=%fused_computation.26 | convolution fusion | flops 4299161600 | bytes 12584960 | tf_op jit(solution)/shard_map/dot_general | solution.py:77
  84.5 2.9 copy.82
  87.4 2.9 copy.95
  90.3 4.0 %fusion.11 = f32[16,128,128]{2,1,0:T(8,128)} fusion(bf16[512,16,128]{0,2,1:T(8,128)(2,1)S(1)} %bitcast.107, bf16[512,16,128]{0,2,1:T(8,128)(2,1)} %copy.82, f32[512,16]{0,1:T(8,128)S(1)} %get-tuple-element.32), kind=kOutput, calls=%fused_computation.20 | convolution fusion | flops 807403520 | bytes 5275648 | tf_op jit(solution)/shard_map/thd,the->hde/dot_general | solution.py:82
  94.3 6.4 %fusion.28 = f32[16,512,128]{1,2,0:T(8,128)S(1)} fusion(bf16[16,512,512]{2,1,0:T(8,128)(2,1)} %multiply_convert_fusion, bf16[512,16,128]{2,1,0:T(8,128)(2,1)S(1)} %bitcast.119), kind=kOutput, calls=%fused_computation.38 | convolution fusion | flops 1073741824 | bytes 14680064 | tf_op jit(solution)/shard_map/hts,shd->thd/dot_general | solution.py:90
  100.7 25.0 %collective-permute-done.2 = f32[16,136,128]{2,1,0:T(8,128)} collective-permute-done((f32[16,136,128]{2,1,0:T(8,128)S(1)}, f32[16,136,128]{2,1,0:T(8,128)}, u32[]{:S(2)}, u32[]{:S(2)}) %collective-permute-start.2) | collective-permute-done | bytes 1114144 | tf_op jit(solution)/shard_map/ppermute | solution.py:19
  125.7 1.6 fusion.34
  127.4 0.3 copy-done.13
  127.6 1.5 fusion.8
  129.2 8.3 %fusion.18 = f32[2048,2048]{1,0:T(8,128)} fusion(bf16[512,2048]{0,1:T(8,128)(2,1)S(1)} %bitcast.127, bf16[1,512,2048]{2,1,0:T(8,128)(2,1)S(1)} %copy-done.28, f32[512]{0:T(512)S(1)} %bitcast.131), kind=kOutput, calls=%fused_computation.28 | convolution fusion | flops 4298113024 | bytes 20973568 | tf_op jit(solution)/shard_map/dot_general | solution.py:95
  137.5 1.4 pad_maximum_fusion
  138.9 3.1 collective-permute-start.3
  142.0 35.0 %collective-permute-done.3 = f32[16,136,128]{2,1,0:T(8,128)S(1)} collective-permute-done((f32[16,136,128]{2,1,0:T(8,128)S(1)}, f32[16,136,128]{2,1,0:T(8,128)S(1)}, u32[]{:S(2)}, u32[]{:S(2)}) %collective-permute-start.3) | collective-permute-done | bytes 1114144 | tf_op jit(solution)/shard_map/ppermute | solution.py:19
  177.5 1.0 copy-done.16
  178.5 1.1 pad_maximum_fusion.4
  179.5 2.6 collective-permute-start.4
  182.1 7.0 %multiply_convert_fusion.1 = bf16[16,512,512]{2,1,0:T(8,128)(2,1)S(1)} fusion(bf16[512,16,128]{0,2,1:T(8,128)(2,1)S(1)} %bitcast.108, f32[16,512]{1,0:T(8,128)S(1)} %get-tuple-element.36, pred[512,512]{1,0:T(8,128)(4,1)S(1)} %copy-done.24, bf16[512,16,128]{2,1,0:T(8,128)(2,1)S(1)} %bitcast.120), kind=kOutput, calls=%fused_computation.1 | convolution fusion | flops 1098907648 | bytes 12877824 | tf_op jit(solution)/shard_map/thd,shd->hts/dot_general | solution.py:102
  189.1 4.7 %fusion.39 = f32[16,512,128]{1,2,0:T(8,128)} fusion(bf16[16,512,512]{2,1,0:T(8,128)(2,1)S(1)} %multiply_convert_fusion.1, bf16[512,16,128]{0,2,1:T(8,128)(2,1)S(1)} %bitcast.116), kind=kOutput, calls=%fused_computation.78 | convolution fusion | flops 1073741824 | bytes 14680064 | tf_op jit(solution)/shard_map/hts,shd->thd/dot_general | solution.py:106
  193.9 14.2 %collective-permute-done.4 = f32[16,136,128]{2,1,0:T(8,128)} collective-permute-done((f32[16,136,128]{2,1,0:T(8,128)}, f32[16,136,128]{2,1,0:T(8,128)}, u32[]{:S(2)}, u32[]{:S(2)}) %collective-permute-start.4) | collective-permute-done | bytes 1114144 | tf_op jit(solution)/shard_map/ppermute | solution.py:19
  208.1 1.1 exponential_reduce_fusion.1
  209.2 1.9 multiply_add_fusion
  211.2 1.1 pad_maximum_fusion.5
  212.3 1.5 collective-permute-start.5
  213.8 3.6 fusion.25
  217.4 3.2 fusion.40
  220.6 2.9 fusion.10
  223.5 4.1 %copy.89 = bf16[1,512,2048]{2,1,0:T(8,128)(2,1)} copy(bf16[1,512,2048]{1,2,0:T(8,128)(2,1)} %bitcast.122) | data formatting | bytes 4194304
  227.6 11.9 %collective-permute-done.5 = f32[16,136,128]{2,1,0:T(8,128)} collective-permute-done((f32[16,136,128]{2,1,0:T(8,128)}, f32[16,136,128]{2,1,0:T(8,128)}, u32[]{:S(2)}, u32[]{:S(2)}) %collective-permute-start.5) | collective-permute-done | bytes 1114144 | tf_op jit(solution)/shard_map/ppermute | solution.py:19
  239.5 2.3 fusion.33
  241.9 0.9 copy-done.2
  242.8 3.3 fusion.6
  246.0 4.1 %copy.90 = bf16[1,512,2048]{2,1,0:T(8,128)(2,1)} copy(bf16[1,512,2048]{1,2,0:T(8,128)(2,1)} %bitcast.124) | data formatting | bytes 4194304
  250.1 5.0 %fusion.4 = bf16[512,16,128]{0,2,1:T(8,128)(2,1)} fusion(f32[16,128,512]{2,1,0:T(8,128)} %fusion.40, f32[16,128,128]{2,1,0:T(8,128)S(1)} %fusion.33, bf16[512,16,128]{0,2,1:T(8,128)(2,1)S(1)} %bitcast.117, f32[512,16]{0,1:T(8,128)S(1)} %get-tuple-element.30), kind=kOutput, calls=%fused_computation.10 | convolution fusion | flops 808452096 | bytes 9469952 | tf_op jit(solution)/shard_map/hde,shd->she/dot_general | solution.py:115
  255.1 3.9 %copy.91 = bf16[1,512,2048]{2,1,0:T(8,128)(2,1)} copy(bf16[1,512,2048]{1,2,0:T(8,128)(2,1)} %bitcast.123) | data formatting | bytes 4194304
  259.0 110.0 %reduce-scatter.2.cloned.1.call-done = f32[64,2048]{1,0:T(8,128)} async-done(((f32[2048,2048]{1,0:T(8,128)}), f32[64,2048]{1,0:T(8,128)}) %reduce-scatter.2.cloned.1.call-update) | async-done | bytes 524304 | tf_op jit(solution)/shard_map/reduce_scatter | solution.py:99
  (91 shorter events, 2.7 us)
Async XLA Ops:
  7.2 0.8 copy-start
  7.2 361.9 %reduce-scatter.2.cloned.1.call-start = ((), (), s32[]{:S(2)}) async-start(), calls=%async_computation.1 | async-start | bytes 17301504 | tf_op jit(solution)/shard_map/reduce_scatter | solution.py:99
  12.5 3.0 copy-start.5
  15.5 2.1 copy-start.9
  17.6 3.5 copy-start.22
  17.8 27.5 %collective-permute-start = (f32[16,136,128]{2,1,0:T(8,128)S(1)}, f32[16,136,128]{2,1,0:T(8,128)S(1)}, u32[]{:S(2)}, u32[]{:S(2)}) collective-permute-start(f32[16,136,128]{2,1,0:T(8,128)S(1)} %pad_maximum_fusion.1), channel_id=1, source_target_pairs={{0,4},{4,8},{8,12},{12,16},{16,20},{20,24},{24,28},{1,5},{5,9},{9,... | collective-permute-start | bytes 3342344 | tf_op jit(solution)/shard_map/ppermute | solution.py:19
  21.1 0.7 copy-start.25
  21.1 0.7 copy-start.26
  21.7 62.8 %copy-start.3 = (bf16[64,8,16,128]{3,2,1,0:T(8,128)(2,1)}, bf16[64,8,16,128]{3,2,1,0:T(8,128)(2,1)S(1)}, u32[]{:S(2)}) copy-start(bf16[64,8,16,128]{3,2,1,0:T(8,128)(2,1)S(1)} %copy.99) | copy-start | bytes 6291460
  21.9 27.4 %copy-start.23 = (pred[512,512]{1,0:T(8,128)(4,1)}, pred[512,512]{1,0:T(8,128)(4,1)S(1)}, u32[]{:S(2)}) copy-start(pred[512,512]{1,0:T(8,128)(4,1)S(1)} %iota_compare_fusion) | copy-start | bytes 786436
  21.9 27.4 %copy-start.6 = (bf16[1,512,2048]{1,2,0:T(8,128)(2,1)S(1)}, bf16[1,512,2048]{1,2,0:T(8,128)(2,1)}, u32[]{:S(2)}) copy-start(bf16[1,512,2048]{1,2,0:T(8,128)(2,1)} %copy-done.5) | copy-start | bytes 6291460
  45.2 27.2 %copy-start.18 = (f32[16,136,128]{2,1,0:T(8,128)}, f32[16,136,128]{2,1,0:T(8,128)S(1)}, u32[]{:S(2)}) copy-start(f32[16,136,128]{2,1,0:T(8,128)S(1)} %collective-permute-done) | copy-start | bytes 3342340
  45.7 33.1 %slice-start.2 = ((s8[8388608]{0:T(1024)(128)(4,1)}), s8[4194304]{0:T(1024)(128)(4,1)S(1)}, s32[]{:S(2)}) async-start(s8[8388608]{0:T(1024)(128)(4,1)} %bitcast.132), calls=%async_computation.4 | async-start | bytes 8388608
  45.8 26.7 %collective-permute-start.1 = (f32[16,136,128]{2,1,0:T(8,128)S(1)}, f32[16,136,128]{2,1,0:T(8,128)S(1)}, u32[]{:S(2)}, u32[]{:S(2)}) collective-permute-start(f32[16,136,128]{2,1,0:T(8,128)S(1)} %pad_maximum_fusion.2), channel_id=1, source_target_pairs={{0,8},{4,12},{8,16},{12,20},{16,24},{20,28},{1,9},{5,13},{9,17},{1... | collective-permute-start | bytes 3342344 | tf_op jit(solution)/shard_map/ppermute | solution.py:19
  49.3 29.5 %slice-start.3 = ((s8[8388608]{0:T(1024)(128)(4,1)}), s8[4194304]{0:T(1024)(128)(4,1)S(1)}, s32[]{:S(2)}) async-start(s8[8388608]{0:T(1024)(128)(4,1)} %bitcast.132), calls=%async_computation.5 | async-start | bytes 8388608
  72.4 1.1 copy-start.20
  72.7 6.1 %copy-start.27 = (bf16[1,512,2048]{2,1,0:T(8,128)(2,1)S(1)}, bf16[1,512,2048]{2,1,0:T(8,128)(2,1)}, u32[]{:S(2)}) copy-start(bf16[1,512,2048]{2,1,0:T(8,128)(2,1)} %param.11) | copy-start | bytes 6291460
  73.5 52.2 %collective-permute-start.2 = (f32[16,136,128]{2,1,0:T(8,128)S(1)}, f32[16,136,128]{2,1,0:T(8,128)}, u32[]{:S(2)}, u32[]{:S(2)}) collective-permute-start(f32[16,136,128]{2,1,0:T(8,128)S(1)} %pad_maximum_fusion.3), channel_id=1, source_target_pairs={{0,16},{4,20},{8,24},{12,28},{1,17},{5,21},{9,25},{13,29},{2,18},{... | collective-permute-start | bytes 3342344 | tf_op jit(solution)/shard_map/ppermute | solution.py:19
  90.3 4.0 %copy-start.10 = (bf16[64,8,16,128]{3,2,1,0:T(8,128)(2,1)S(1)}, bf16[64,8,16,128]{3,2,1,0:T(8,128)(2,1)}, u32[]{:S(2)}) copy-start(bf16[64,8,16,128]{3,2,1,0:T(8,128)(2,1)} %copy-done.9) | copy-start | bytes 6291460
  94.3 31.5 %copy-start.19 = (f32[16,136,128]{2,1,0:T(8,128)S(1)}, f32[16,136,128]{2,1,0:T(8,128)}, u32[]{:S(2)}) copy-start(f32[16,136,128]{2,1,0:T(8,128)} %copy-done.18) | copy-start | bytes 3342340
  94.3 31.5 %copy-start.21 = (f32[16,136,128]{2,1,0:T(8,128)S(1)}, f32[16,136,128]{2,1,0:T(8,128)}, u32[]{:S(2)}) copy-start(f32[16,136,128]{2,1,0:T(8,128)} %copy-done.20) | copy-start | bytes 3342340
  125.7 1.9 copy-start.13
  127.6 1.6 copy-start.28
  137.5 39.7 %copy-start.15 = (f32[16,128,128]{2,1,0:T(8,128)S(1)}, f32[16,128,128]{2,1,0:T(8,128)}, u32[]{:S(2)}) copy-start(f32[16,128,128]{2,1,0:T(8,128)} %fusion.11) | copy-start | bytes 3145732
  138.9 38.1 %collective-permute-start.3 = (f32[16,136,128]{2,1,0:T(8,128)S(1)}, f32[16,136,128]{2,1,0:T(8,128)S(1)}, u32[]{:S(2)}, u32[]{:S(2)}) collective-permute-start(f32[16,136,128]{2,1,0:T(8,128)S(1)} %pad_maximum_fusion), channel_id=1, source_target_pairs={{4,0},{8,4},{12,8},{16,12},{20,16},{24,20},{28,24},{5,1},{9,5},{13... | collective-permute-start | bytes 3342344 | tf_op jit(solution)/shard_map/ppermute | solution.py:19
  177.0 2.6 copy-start.17
  177.2 4.9 %copy-start.11 = (bf16[64,8,16,128]{3,2,1,0:T(8,128)(2,1)S(1)}, bf16[64,8,16,128]{3,2,1,0:T(8,128)(2,1)}, u32[]{:S(2)}) copy-start(bf16[64,8,16,128]{3,2,1,0:T(8,128)(2,1)} %copy-done.9) | copy-start | bytes 6291460
  177.2 4.9 %copy-start.24 = (pred[512,512]{1,0:T(8,128)(4,1)S(1)}, pred[512,512]{1,0:T(8,128)(4,1)}, u32[]{:S(2)}) copy-start(pred[512,512]{1,0:T(8,128)(4,1)} %copy-done.23) | copy-start | bytes 786436
  177.4 1.1 copy-start.16
  179.5 9.6 %copy-start.7 = (bf16[1,512,2048]{1,2,0:T(8,128)(2,1)S(1)}, bf16[1,512,2048]{1,2,0:T(8,128)(2,1)}, u32[]{:S(2)}) copy-start(bf16[1,512,2048]{1,2,0:T(8,128)(2,1)} %copy-done.5) | copy-start | bytes 6291460
  179.5 28.6 %collective-permute-start.4 = (f32[16,136,128]{2,1,0:T(8,128)}, f32[16,136,128]{2,1,0:T(8,128)}, u32[]{:S(2)}, u32[]{:S(2)}) collective-permute-start(f32[16,136,128]{2,1,0:T(8,128)} %pad_maximum_fusion.4), channel_id=1, source_target_pairs={{8,0},{12,4},{16,8},{20,12},{24,16},{28,20},{9,1},{13,5},{17,9},{2... | collective-permute-start | bytes 3342344 | tf_op jit(solution)/shard_map/ppermute | solution.py:19
  209.2 4.6 %copy-start.4 = (bf16[64,8,16,128]{3,2,1,0:T(8,128)(2,1)S(1)}, bf16[64,8,16,128]{3,2,1,0:T(8,128)(2,1)}, u32[]{:S(2)}) copy-start(bf16[64,8,16,128]{3,2,1,0:T(8,128)(2,1)} %copy-done.3) | copy-start | bytes 6291460
  211.2 6.2 %slice-start = ((s8[8388608]{0:T(1024)(128)(4,1)}), s8[4194304]{0:T(1024)(128)(4,1)S(1)}, s32[]{:S(2)}) async-start(s8[8388608]{0:T(1024)(128)(4,1)} %bitcast.105), calls=%async_computation.2 | async-start | bytes 8388608
  212.3 5.1 %slice-start.1 = ((s8[8388608]{0:T(1024)(128)(4,1)}), s8[4194304]{0:T(1024)(128)(4,1)S(1)}, s32[]{:S(2)}) async-start(s8[8388608]{0:T(1024)(128)(4,1)} %bitcast.105), calls=%async_computation.3 | async-start | bytes 8388608
  212.3 27.3 %collective-permute-start.5 = (f32[16,136,128]{2,1,0:T(8,128)}, f32[16,136,128]{2,1,0:T(8,128)}, u32[]{:S(2)}, u32[]{:S(2)}) collective-permute-start(f32[16,136,128]{2,1,0:T(8,128)} %pad_maximum_fusion.5), channel_id=1, source_target_pairs={{16,0},{20,4},{24,8},{28,12},{17,1},{21,5},{25,9},{29,13},{18,2},{... | collective-permute-start | bytes 3342344 | tf_op jit(solution)/shard_map/ppermute | solution.py:19
  217.4 3.2 copy-start.14
  223.5 18.3 %copy-start.12 = (bf16[64,8,16,128]{3,2,1,0:T(8,128)(2,1)S(1)}, bf16[64,8,16,128]{3,2,1,0:T(8,128)(2,1)}, u32[]{:S(2)}) copy-start(bf16[64,8,16,128]{3,2,1,0:T(8,128)(2,1)} %copy-done.9) | copy-start | bytes 6291460
  239.5 3.2 copy-start.2
  246.0 4.1 %copy-start.8 = (bf16[1,512,2048]{1,2,0:T(8,128)(2,1)S(1)}, bf16[1,512,2048]{1,2,0:T(8,128)(2,1)}, u32[]{:S(2)}) copy-start(bf16[1,512,2048]{1,2,0:T(8,128)(2,1)} %copy-done.5) | copy-start | bytes 6291460
  255.1 114.0 %copy-start.1 = (f32[1,512,16]{1,2,0:T(8,128)S(1)}, f32[1,512,16]{1,2,0:T(8,128)}, u32[]{:S(2)}) copy-start(f32[1,512,16]{1,2,0:T(8,128)} %param.13) | copy-start | bytes 98308
Sparse Core Ops, SparseCore 0:
  137.6 231.4 reduce-scatter.1

commit v8 on v7

--- a/solution.py
+++ b/solution.py
@@ -23,6 +23,28 @@
         distance *= 2
     if gathered is None:
         gathered = jax.tree.map(jnp.zeros_like, value)
+    return gathered
+
+
+def carried_groups(value, join, heading):
+    count, groups = lax.axis_size("ctx"), lax.axis_size("dp")
+    partial = value
+    gathered = None
+    distance = 1
+    while distance < count:
+        pairs = []
+        for place in range(count):
+            for group in range(groups):
+                step = heading[group % 2] * distance
+                if step != 0 and 0 <= place + step < count:
+                    pairs.append((place * groups + group, (place + step) * groups + group))
+        arrived = lax.ppermute(partial, ("ctx", "dp"), pairs)
+        gathered = arrived if gathered is None else join(arrived, gathered)
+        if distance * 2 < count:
+            partial = join(arrived, partial)
+        distance *= 2
+    if gathered is None:
+        gathered = jnp.zeros_like(value)
     return gathered
 
 
@@ -97,7 +119,11 @@
     )
     partial, back_end = lax.optimization_barrier((partial, back_end))
     grad_weight = lax.psum_scatter(partial, ("ctx", "dp"), scatter_dimension=0, tiled=True)
-    back_in = carried_in(pack_state(total, back_end), "ctx", packed_join, True)[:, :HD]
+    even = lax.axis_index("dp") % 2 == 0
+    back_even = carried_groups(pack_state(total, back_end), packed_join, (-1, 0))[:, :HD]
+    back_end, back_even = lax.optimization_barrier((back_end, back_even))
+    back_odd = carried_groups(pack_state(total, back_end), packed_join, (0, -1))[:, :HD]
+    back_in = jnp.where(even, back_even, back_odd)
 
     dscores = jnp.einsum(
         "thd,shd->hts", dout_heads, value_heads, preferred_element_type=jnp.float32

time: 377 us -> 381 us (1.011)
    ppermute x6 -> x3, waiting for transfers between devices: 125 us -> 65 us  [carried_in(): lax.ppermute(part, axis, pairs)]
    ppermute x0 -> x6, waiting for transfers between devices: none -> 56.3 us  [carried_groups(): arrived = lax.ppermute(partial, ('ctx', 'dp'), pairs)]
    ppermute x0 -> x6, starting transfers between devices: none -> 8.8 us  [carried_groups(): arrived = lax.ppermute(partial, ('ctx', 'dp'), pairs)]
    ppermute x6 -> x3, starting transfers between devices: 19.2 us -> 12 us  [carried_in(): lax.ppermute(part, axis, pairs)]
    unnamed x71 -> x77, local copies, waits for them, and re-layouts: 19.2 us -> 18.6 us
  transfers between devices with their start and end apart: 7 -> 10, of which waited for: 7 -> 6; matrix products, arithmetic and copies ran while one was open for 22% -> 22% of each run, Pallas kernels for 0% -> 0%
where the time goes in v8:
time: 381 us; the launch traced here: 380 us
  waiting for transfers between devices  233 us (61%)
  matrix products  68.3 us (18%)
  local copies, waits for them, and re-layouts  28.1 us (7%)
  starting transfers between devices  20.9 us (5%)
  other arithmetic  15.2 us (4%)
  between operations  14.6 us (4%)
    reduce_scatter x1, waiting for transfers between devices, on_device(): lax.psum_scatter(partial, ('ctx', 'dp'), scatter_dimension=0, tiled=True)  112 us
    ppermute x3, waiting for transfers between devices, carried_in(): lax.ppermute(part, axis, pairs)  65 us
    ppermute x6, waiting for transfers between devices, carried_groups(): arrived = lax.ppermute(partial, ('ctx', 'dp'), pairs)  56.3 us
    unnamed x77, local copies, waits for them, and re-layouts  18.6 us
    ppermute x3, starting transfers between devices, carried_in(): lax.ppermute(part, axis, pairs)  12 us
    ppermute x6, starting transfers between devices, carried_groups(): arrived = lax.ppermute(partial, ('ctx', 'dp'), pairs)  8.8 us
    dot_general x1, matrix products, on_device(): lax.dot_general(attn, weighted, (((0,), (0,)), ((), ())), preferred_eleme...  8.25 us
    dot_general x1, matrix products, on_device(): jnp.einsum('thd,shd->hts', query_heads, key_heads, preferred_element_type...  7.84 us
  transfers between devices with their start and end apart: 10, of which 6 were waited for; matrix products, arithmetic and copies ran while one was open for 22% of the time, Pallas kernels for 0%

profile of v8, /device:TPU:11, one launch (start us, length us, event | category | flops | bytes accessed | tf_op | source)
XLA Modules:
  0.0 380.1 jit_solution(6861507139513193229)
XLA Ops:
  7.2 0.7 copy-done
  7.9 1.1 reduce-window.6
  9.5 0.7 broadcast_multiply_fusion
  10.2 2.9 copy.97
  13.1 3.0 copy.101
  16.1 2.0 fusion.14
  18.3 3.3 collective-permute-start
  22.5 23.3 %collective-permute-done = f32[16,136,128]{2,1,0:T(8,128)S(1)} collective-permute-done((f32[16,136,128]{2,1,0:T(8,128)S(1)}, f32[16,136,128]{2,1,0:T(8,128)S(1)}, u32[]{:S(2)}, u32[]{:S(2)}) %collective-permute-start) | collective-permute-done | bytes 1114144 | tf_op jit(solution)/shard_map/ppermute | solution.py:19
  46.4 3.5 collective-permute-start.1
  49.9 7.8 %multiply_convert_fusion = bf16[16,512,512]{2,1,0:T(8,128)(2,1)} fusion(bf16[512,16,128]{0,2,1:T(8,128)(2,1)S(1)} %bitcast.114, f32[16,512]{1,0:T(8,128)S(1)} %get-tuple-element.43, pred[512,512]{1,0:T(8,128)(4,1)S(1)} %iota_compare_fusion, bf16[512,16,128]{2,1,0:T(8,128)(2,1)S(1)} %bitcast.110), kind=kOutput, calls=%fused_computation | convolution fusion | flops 1098907648 | bytes 12877824 | tf_op jit(solution)/shard_map/thd,shd->hts/dot_general | solution.py:110
  57.7 15.3 %collective-permute-done.1 = f32[16,136,128]{2,1,0:T(8,128)S(1)} collective-permute-done((f32[16,136,128]{2,1,0:T(8,128)S(1)}, f32[16,136,128]{2,1,0:T(8,128)S(1)}, u32[]{:S(2)}, u32[]{:S(2)}) %collective-permute-start.1) | collective-permute-done | bytes 1114144 | tf_op jit(solution)/shard_map/ppermute | solution.py:19
  73.0 0.8 exponential_reduce_fusion.5
  74.1 1.1 pad_maximum_fusion.4
  75.2 5.2 %collective-permute-start.2 = (f32[16,136,128]{2,1,0:T(8,128)}, f32[16,136,128]{2,1,0:T(8,128)}, u32[]{:S(2)}, u32[]{:S(2)}) collective-permute-start(f32[16,136,128]{2,1,0:T(8,128)} %pad_maximum_fusion.4), channel_id=1, source_target_pairs={{0,16},{4,20},{8,24},{12,28},{1,17},{5,21},{9,25},{13,29},{2,18},{... | collective-permute-start | bytes 3342344 | tf_op jit(solution)/shard_map/ppermute | solution.py:19
  80.5 5.8 %convolution_convert_fusion = bf16[512,2048]{1,0:T(8,128)(2,1)} fusion(bf16[2048,2048]{1,0:T(8,128)(2,1)S(1)} %bitcast.133, bf16[1,512,2048]{2,1,0:T(8,128)(2,1)S(1)} %copy-done.32, f32[512]{0:T(512)S(1)} %bitcast.130), kind=kOutput, calls=%fused_computation.26 | convolution fusion | flops 4299161600 | bytes 12584960 | tf_op jit(solution)/shard_map/dot_general | solution.py:99
  86.3 2.9 copy.84
  89.2 2.9 copy.98
  92.1 3.0 fusion.11
  95.1 6.4 %fusion.28 = f32[16,512,128]{1,2,0:T(8,128)S(1)} fusion(bf16[16,512,512]{2,1,0:T(8,128)(2,1)} %multiply_convert_fusion, bf16[512,16,128]{2,1,0:T(8,128)(2,1)S(1)} %bitcast.118), kind=kOutput, calls=%fused_computation.39 | convolution fusion | flops 1073741824 | bytes 14680064 | tf_op jit(solution)/shard_map/hts,shd->thd/dot_general | solution.py:112
  101.5 26.3 %collective-permute-done.2 = f32[16,136,128]{2,1,0:T(8,128)} collective-permute-done((f32[16,136,128]{2,1,0:T(8,128)}, f32[16,136,128]{2,1,0:T(8,128)}, u32[]{:S(2)}, u32[]{:S(2)}) %collective-permute-start.2) | collective-permute-done | bytes 1114144 | tf_op jit(solution)/shard_map/ppermute | solution.py:19
  127.8 2.0 fusion.36
  130.0 1.5 fusion.8
  131.7 8.3 %fusion.18 = f32[2048,2048]{1,0:T(8,128)} fusion(bf16[512,2048]{0,1:T(8,128)(2,1)S(1)} %bitcast.126, bf16[1,512,2048]{2,1,0:T(8,128)(2,1)S(1)} %copy-done.33, f32[512]{0:T(512)S(1)} %bitcast.131), kind=kOutput, calls=%fused_computation.28 | convolution fusion | flops 4298113024 | bytes 20973568 | tf_op jit(solution)/shard_map/dot_general | solution.py:117
  140.1 0.7 collective-permute-start.3
  141.4 0.7 collective-permute-start.4
  142.7 0.7 collective-permute-start.5
  143.5 1.2 fusion.35
  144.8 3.3 collective-permute-start.6
  148.1 36.1 %collective-permute-done.6 = f32[16,136,128]{2,1,0:T(8,128)S(1)} collective-permute-done((f32[16,136,128]{2,1,0:T(8,128)S(1)}, f32[16,136,128]{2,1,0:T(8,128)S(1)}, u32[]{:S(2)}, u32[]{:S(2)}) %collective-permute-start.6) | collective-permute-done | bytes 1114144 | tf_op jit(solution)/shard_map/ppermute | solution.py:41
  185.6 1.1 pad_maximum_fusion.7
  186.6 2.0 collective-permute-start.7
  188.7 6.9 %multiply_convert_fusion.1 = bf16[16,512,512]{2,1,0:T(8,128)(2,1)S(1)} fusion(bf16[512,16,128]{0,2,1:T(8,128)(2,1)S(1)} %bitcast.107, f32[16,512]{1,0:T(8,128)S(1)} %copy-done.26, pred[512,512]{1,0:T(8,128)(4,1)S(1)} %iota_compare_fusion, bf16[512,16,128]{2,1,0:T(8,128)(2,1)S(1)} %bitcast.119), kind=kOutput, calls=%fused_computation.1 | convolution fusion | flops 1098907648 | bytes 12877824 | tf_op jit(solution)/shard_map/thd,shd->hts/dot_general | solution.py:128
  195.7 4.9 %fusion.42 = f32[16,512,128]{1,2,0:T(8,128)} fusion(bf16[16,512,512]{2,1,0:T(8,128)(2,1)S(1)} %multiply_convert_fusion.1, bf16[512,16,128]{0,2,1:T(8,128)(2,1)S(1)} %bitcast.115), kind=kOutput, calls=%fused_computation.91 | convolution fusion | flops 1073741824 | bytes 14680064 | tf_op jit(solution)/shard_map/hts,shd->thd/dot_general | solution.py:132
  200.5 20.2 %collective-permute-done.7 = f32[16,136,128]{2,1,0:T(8,128)S(1)} collective-permute-done((f32[16,136,128]{2,1,0:T(8,128)}, f32[16,136,128]{2,1,0:T(8,128)S(1)}, u32[]{:S(2)}, u32[]{:S(2)}) %collective-permute-start.7) | collective-permute-done | bytes 1114144 | tf_op jit(solution)/shard_map/ppermute | solution.py:41
  220.7 1.1 exponential_reduce_fusion.1
  222.1 1.1 pad_maximum_fusion.8
  223.2 1.3 collective-permute-start.8
  224.5 3.5 fusion.25
  228.1 6.9 %fusion.43 = f32[16,128,512]{2,1,0:T(8,128)} fusion(bf16[512,16,128]{0,2,1:T(8,128)(2,1)S(1)} %bitcast.108, bf16[16,512,512]{2,1,0:T(8,128)(2,1)} %multiply_convert_fusion), kind=kOutput, calls=%fused_computation.92 | convolution fusion | flops 1073741824 | bytes 14680064 | tf_op jit(solution)/shard_map/hts,thd->shd/dot_general | solution.py:134
  235.0 3.0 fusion.10
  238.0 4.1 %copy.92 = bf16[1,512,2048]{2,1,0:T(8,128)(2,1)} copy(bf16[1,512,2048]{1,2,0:T(8,128)(2,1)} %bitcast.121) | data formatting | bytes 4194304
  242.0 2.3 fusion.34
  244.4 0.8 copy-done.2
  245.2 3.3 fusion.6
  248.5 4.1 %copy.93 = bf16[1,512,2048]{2,1,0:T(8,128)(2,1)} copy(bf16[1,512,2048]{1,2,0:T(8,128)(2,1)} %bitcast.123) | data formatting | bytes 4194304
  252.5 5.0 %fusion.4 = bf16[512,16,128]{0,2,1:T(8,128)(2,1)} fusion(f32[16,128,512]{2,1,0:T(8,128)} %fusion.43, f32[16,128,128]{2,1,0:T(8,128)S(1)} %fusion.34, bf16[512,16,128]{0,2,1:T(8,128)(2,1)S(1)} %bitcast.116, f32[512,16]{0,1:T(8,128)S(1)} %get-tuple-element.37), kind=kOutput, calls=%fused_computation.10 | convolution fusion | flops 808452096 | bytes 9469952 | tf_op jit(solution)/shard_map/hde,shd->she/dot_general | solution.py:141
  257.5 3.9 %copy.94 = bf16[1,512,2048]{2,1,0:T(8,128)(2,1)} copy(bf16[1,512,2048]{1,2,0:T(8,128)(2,1)} %bitcast.122) | data formatting | bytes 4194304
  261.5 111.7 %reduce-scatter.2.cloned.1.call-done = f32[64,2048]{1,0:T(8,128)} async-done(((f32[2048,2048]{1,0:T(8,128)}), f32[64,2048]{1,0:T(8,128)}) %reduce-scatter.2.cloned.1.call-update) | async-done | bytes 524304 | tf_op jit(solution)/shard_map/reduce_scatter | solution.py:121
  (113 shorter events, 5.6 us)
Async XLA Ops:
  7.2 0.8 copy-start
  7.2 366.0 %reduce-scatter.2.cloned.1.call-start = ((), (), s32[]{:S(2)}) async-start(), calls=%async_computation.1 | async-start | bytes 17301504 | tf_op jit(solution)/shard_map/reduce_scatter | solution.py:121
  9.3 40.5 %copy-start.25 = (f32[16,512]{1,0:T(8,128)}, f32[16,512]{1,0:T(8,128)S(1)}, u32[]{:S(2)}) copy-start(f32[16,512]{1,0:T(8,128)S(1)} %get-tuple-element.43) | copy-start | bytes 98308
  13.1 3.0 copy-start.5
  16.1 2.1 copy-start.9
  18.2 3.5 copy-start.24
  18.3 27.5 %collective-permute-start = (f32[16,136,128]{2,1,0:T(8,128)S(1)}, f32[16,136,128]{2,1,0:T(8,128)S(1)}, u32[]{:S(2)}, u32[]{:S(2)}) collective-permute-start(f32[16,136,128]{2,1,0:T(8,128)S(1)} %pad_maximum_fusion.2), channel_id=1, source_target_pairs={{0,4},{4,8},{8,12},{12,16},{16,20},{20,24},{24,28},{1,5},{5,9},{9,... | collective-permute-start | bytes 3342344 | tf_op jit(solution)/shard_map/ppermute | solution.py:19
  21.7 0.7 copy-start.28
  21.7 0.7 copy-start.29
  22.3 64.0 %copy-start.3 = (bf16[64,8,16,128]{3,2,1,0:T(8,128)(2,1)}, bf16[64,8,16,128]{3,2,1,0:T(8,128)(2,1)S(1)}, u32[]{:S(2)}) copy-start(bf16[64,8,16,128]{3,2,1,0:T(8,128)(2,1)S(1)} %copy.102) | copy-start | bytes 6291460
  22.5 58.0 %copy-start.30 = (f32[1,512]{1,0:T(1,128)}, f32[1,512]{1,0:T(1,128)S(1)}, u32[]{:S(2)}) copy-start(f32[1,512]{1,0:T(1,128)S(1)} %convert_multiply_fusion.1) | copy-start | bytes 6148
  22.5 27.4 %copy-start.6 = (bf16[1,512,2048]{1,2,0:T(8,128)(2,1)S(1)}, bf16[1,512,2048]{1,2,0:T(8,128)(2,1)}, u32[]{:S(2)}) copy-start(bf16[1,512,2048]{1,2,0:T(8,128)(2,1)} %copy-done.5) | copy-start | bytes 6291460
  45.8 27.2 %copy-start.19 = (f32[16,136,128]{2,1,0:T(8,128)}, f32[16,136,128]{2,1,0:T(8,128)S(1)}, u32[]{:S(2)}) copy-start(f32[16,136,128]{2,1,0:T(8,128)S(1)} %collective-permute-done) | copy-start | bytes 3342340
  46.3 34.2 %slice-start = ((s8[8388608]{0:T(1024)(128)(4,1)}), s8[4194304]{0:T(1024)(128)(4,1)S(1)}, s32[]{:S(2)}) async-start(s8[8388608]{0:T(1024)(128)(4,1)} %bitcast.132), calls=%async_computation.2 | async-start | bytes 8388608
  46.4 26.7 %collective-permute-start.1 = (f32[16,136,128]{2,1,0:T(8,128)S(1)}, f32[16,136,128]{2,1,0:T(8,128)S(1)}, u32[]{:S(2)}, u32[]{:S(2)}) collective-permute-start(f32[16,136,128]{2,1,0:T(8,128)S(1)} %pad_maximum_fusion.3), channel_id=1, source_target_pairs={{0,8},{4,12},{8,16},{12,20},{16,24},{20,28},{1,9},{5,13},{9,17},{1... | collective-permute-start | bytes 3342344 | tf_op jit(solution)/shard_map/ppermute | solution.py:19
  49.9 30.6 %slice-start.1 = ((s8[8388608]{0:T(1024)(128)(4,1)}), s8[4194304]{0:T(1024)(128)(4,1)S(1)}, s32[]{:S(2)}) async-start(s8[8388608]{0:T(1024)(128)(4,1)} %bitcast.132), calls=%async_computation.3 | async-start | bytes 8388608
  73.0 2.2 copy-start.22
  73.9 6.6 %copy-start.32 = (bf16[1,512,2048]{2,1,0:T(8,128)(2,1)S(1)}, bf16[1,512,2048]{2,1,0:T(8,128)(2,1)}, u32[]{:S(2)}) copy-start(bf16[1,512,2048]{2,1,0:T(8,128)(2,1)} %param.11) | copy-start | bytes 6291460
  75.2 52.6 %collective-permute-start.2 = (f32[16,136,128]{2,1,0:T(8,128)}, f32[16,136,128]{2,1,0:T(8,128)}, u32[]{:S(2)}, u32[]{:S(2)}) collective-permute-start(f32[16,136,128]{2,1,0:T(8,128)} %pad_maximum_fusion.4), channel_id=1, source_target_pairs={{0,16},{4,20},{8,24},{12,28},{1,17},{5,21},{9,25},{13,29},{2,18},{... | collective-permute-start | bytes 3342344 | tf_op jit(solution)/shard_map/ppermute | solution.py:19
  92.0 3.0 copy-start.10
  95.1 32.7 %copy-start.20 = (f32[16,136,128]{2,1,0:T(8,128)S(1)}, f32[16,136,128]{2,1,0:T(8,128)}, u32[]{:S(2)}) copy-start(f32[16,136,128]{2,1,0:T(8,128)} %copy-done.19) | copy-start | bytes 3342340
  95.1 32.7 %copy-start.27 = (f32[16]{0:T(128)S(1)}, f32[16]{0:T(128)}, u32[]{:S(2)}) copy-start(f32[16]{0:T(128)} %get-tuple-element.35) | copy-start | bytes 196
  127.8 2.2 copy-start.13
  129.8 1.8 copy-start.15
  130.0 1.5 copy-start.31
  130.0 1.7 copy-start.33
  140.1 0.7 collective-permute-start.3
  141.4 0.7 collective-permute-start.4
  142.7 0.7 collective-permute-start.5
  144.8 39.4 %collective-permute-start.6 = (f32[16,136,128]{2,1,0:T(8,128)S(1)}, f32[16,136,128]{2,1,0:T(8,128)S(1)}, u32[]{:S(2)}, u32[]{:S(2)}) collective-permute-start(f32[16,136,128]{2,1,0:T(8,128)S(1)} %pad_maximum_fusion), channel_id=1, source_target_pairs={{5,1},{7,3},{9,5},{11,7},{13,9},{15,11},{17,13},{19,15},{21,17},{2... | collective-permute-start | bytes 3342344 | tf_op jit(solution)/shard_map/ppermute | solution.py:41
  184.2 1.0 copy-start.21
  184.4 4.3 %copy-start.11 = (bf16[64,8,16,128]{3,2,1,0:T(8,128)(2,1)S(1)}, bf16[64,8,16,128]{3,2,1,0:T(8,128)(2,1)}, u32[]{:S(2)}) copy-start(bf16[64,8,16,128]{3,2,1,0:T(8,128)(2,1)} %copy-done.9) | copy-start | bytes 6291460
  184.4 4.3 %copy-start.26 = (f32[16,512]{1,0:T(8,128)S(1)}, f32[16,512]{1,0:T(8,128)}, u32[]{:S(2)}) copy-start(f32[16,512]{1,0:T(8,128)} %copy-done.25) | copy-start | bytes 98308
  184.6 1.0 copy-start.17
  186.6 9.0 %copy-start.7 = (bf16[1,512,2048]{1,2,0:T(8,128)(2,1)S(1)}, bf16[1,512,2048]{1,2,0:T(8,128)(2,1)}, u32[]{:S(2)}) copy-start(bf16[1,512,2048]{1,2,0:T(8,128)(2,1)} %copy-done.5) | copy-start | bytes 6291460
  186.6 34.1 %collective-permute-start.7 = (f32[16,136,128]{2,1,0:T(8,128)}, f32[16,136,128]{2,1,0:T(8,128)S(1)}, u32[]{:S(2)}, u32[]{:S(2)}) collective-permute-start(f32[16,136,128]{2,1,0:T(8,128)} %pad_maximum_fusion.7), channel_id=1, source_target_pairs={{9,1},{11,3},{13,5},{15,7},{17,9},{19,11},{21,13},{23,15},{25,17},... | collective-permute-start | bytes 3342344 | tf_op jit(solution)/shard_map/ppermute | solution.py:41
  195.6 26.2 %copy-start.18 = (f32[16,128,128]{2,1,0:T(8,128)S(1)}, f32[16,128,128]{2,1,0:T(8,128)}, u32[]{:S(2)}) copy-start(f32[16,128,128]{2,1,0:T(8,128)} %copy-done.17) | copy-start | bytes 3145732
  220.7 2.5 copy-start.23
  221.9 2.7 copy-start.4
  223.2 18.8 %collective-permute-start.8 = (f32[16,136,128]{2,1,0:T(8,128)}, f32[16,136,128]{2,1,0:T(8,128)}, u32[]{:S(2)}, u32[]{:S(2)}) collective-permute-start(f32[16,136,128]{2,1,0:T(8,128)} %pad_maximum_fusion.8), channel_id=1, source_target_pairs={{17,1},{19,3},{21,5},{23,7},{25,9},{27,11},{29,13},{31,15}} | collective-permute-start | bytes 3342344 | tf_op jit(solution)/shard_map/ppermute | solution.py:41
  228.1 6.9 %copy-start.14 = (f32[16,512,128]{1,2,0:T(8,128)S(1)}, f32[16,512,128]{1,2,0:T(8,128)}, u32[]{:S(2)}) copy-start(f32[16,512,128]{1,2,0:T(8,128)} %fusion.42) | copy-start | bytes 12582916
  228.1 6.9 %copy-start.16 = (f32[16,128,128]{2,1,0:T(8,128)S(1)}, f32[16,128,128]{2,1,0:T(8,128)}, u32[]{:S(2)}) copy-start(f32[16,128,128]{2,1,0:T(8,128)} %copy-done.15) | copy-start | bytes 3145732
  238.0 6.4 %copy-start.12 = (bf16[64,8,16,128]{3,2,1,0:T(8,128)(2,1)S(1)}, bf16[64,8,16,128]{3,2,1,0:T(8,128)(2,1)}, u32[]{:S(2)}) copy-start(bf16[64,8,16,128]{3,2,1,0:T(8,128)(2,1)} %copy-done.9) | copy-start | bytes 6291460
  242.0 3.1 copy-start.2
  248.5 4.1 %copy-start.8 = (bf16[1,512,2048]{1,2,0:T(8,128)(2,1)S(1)}, bf16[1,512,2048]{1,2,0:T(8,128)(2,1)}, u32[]{:S(2)}) copy-start(bf16[1,512,2048]{1,2,0:T(8,128)(2,1)} %copy-done.5) | copy-start | bytes 6291460
  257.5 115.7 %copy-start.1 = (f32[1,512,16]{1,2,0:T(8,128)S(1)}, f32[1,512,16]{1,2,0:T(8,128)}, u32[]{:S(2)}) copy-start(f32[1,512,16]{1,2,0:T(8,128)} %param.13) | copy-start | bytes 98308
Sparse Core Ops, SparseCore 0:
  140.1 233.0 reduce-scatter.1

commit v9 on v7

--- a/solution.py
+++ b/solution.py
@@ -70,7 +70,6 @@
         "shd,she->hde", key_f32 * remain, value_f32, precision=lax.Precision.HIGH
     )
     state_in = carried_in(pack_state(total, state_end), "ctx", packed_join, False)[:, :HD]
-    state_end, upstream, query_heads = lax.optimization_barrier((state_end, upstream, query_heads))
 
     advantage = (2 * signs[0] - 1).astype(jnp.float32) * magnitude[0]
     weighted = (advantage[:, None] * upstream[0].astype(jnp.float32)).astype(jnp.bfloat16)

time: 377 us -> 380 us (level)
  other arithmetic: 13.3 us -> 17.2 us
    unnamed x71 -> x60, local copies, waits for them, and re-layouts: 19.2 us -> 17 us
  transfers between devices with their start and end apart: 7 -> 7, of which waited for: 7 -> 7; matrix products, arithmetic and copies ran while one was open for 22% -> 21% of each run, Pallas kernels for 0% -> 0%
where the time goes in v9:
time: 380 us; the launch traced here: 379 us
  waiting for transfers between devices  236 us (62%)
  matrix products  65 us (17%)
  local copies, waits for them, and re-layouts  27.4 us (7%)
  starting transfers between devices  19.3 us (5%)
  other arithmetic  17.2 us (5%)
  between operations  14.5 us (4%)
    ppermute x6, waiting for transfers between devices, carried_in(): lax.ppermute(part, axis, pairs)  125 us
    reduce_scatter x1, waiting for transfers between devices, on_device(): lax.psum_scatter(partial, ('ctx', 'dp'), scatter_dimension=0, tiled=True)  111 us
    ppermute x6, starting transfers between devices, carried_in(): lax.ppermute(part, axis, pairs)  19.3 us
    unnamed x60, local copies, waits for them, and re-layouts  17 us
    dot_general x1, matrix products, on_device(): lax.dot_general(attn, weighted, (((0,), (0,)), ((), ())), preferred_eleme...  8.14 us
    dot_general x1, matrix products, on_device(): jnp.einsum('thd,shd->hts', query_heads, key_heads, preferred_element_type...  7.68 us
  transfers between devices with their start and end apart: 7, of which 7 were waited for; matrix products, arithmetic and copies ran while one was open for 21% of the time, Pallas kernels for 0%

profile of v9, /device:TPU:11, one launch (start us, length us, event | category | flops | bytes accessed | tf_op | source)
XLA Modules:
  0.0 379.2 jit_solution(6855092686479396516)
XLA Ops:
  7.2 0.7 copy-done
  7.9 1.1 reduce-window.6
  9.6 2.9 copy.95
  12.5 3.0 copy.99
  15.5 2.0 fusion.14
  17.6 1.1 pad_maximum_fusion.1
  18.7 3.2 collective-permute-start
  21.9 2.9 copy.96
  24.9 21.4 %collective-permute-done = f32[16,136,128]{2,1,0:T(8,128)} collective-permute-done((f32[16,136,128]{2,1,0:T(8,128)}, f32[16,136,128]{2,1,0:T(8,128)}, u32[]{:S(2)}, u32[]{:S(2)}) %collective-permute-start) | collective-permute-done | bytes 1114144 | tf_op jit(solution)/shard_map/ppermute | solution.py:19
  46.3 1.4 multiply_add_fusion.3
  47.7 1.0 add_reduce_fusion.1
  48.9 3.5 collective-permute-start.1
  52.4 7.7 %multiply_convert_fusion = bf16[16,512,512]{2,1,0:T(8,128)(2,1)} fusion(bf16[512,16,128]{0,2,1:T(8,128)(2,1)S(1)} %bitcast.107, bf16[512,16,128]{0,2,1:T(8,128)(2,1)S(1)} %bitcast.116, f32[16,512]{1,0:T(8,128)S(1)} %get-tuple-element.33, pred[512,512]{1,0:T(8,128)(4,1)S(1)} %iota_compare_fusion), kind=kOutput, calls=%fused_computation | convolution fusion | flops 1098907648 | bytes 12877824 | tf_op jit(solution)/shard_map/thd,shd->hts/dot_general | solution.py:87
  60.1 15.5 %collective-permute-done.1 = f32[16,136,128]{2,1,0:T(8,128)S(1)} collective-permute-done((f32[16,136,128]{2,1,0:T(8,128)S(1)}, f32[16,136,128]{2,1,0:T(8,128)S(1)}, u32[]{:S(2)}, u32[]{:S(2)}) %collective-permute-start.1) | collective-permute-done | bytes 1114144 | tf_op jit(solution)/shard_map/ppermute | solution.py:19
  75.6 1.1 exponential_reduce_fusion.3
  77.1 5.3 %collective-permute-start.2 = (f32[16,136,128]{2,1,0:T(8,128)S(1)}, f32[16,136,128]{2,1,0:T(8,128)}, u32[]{:S(2)}, u32[]{:S(2)}) collective-permute-start(f32[16,136,128]{2,1,0:T(8,128)S(1)} %pad_maximum_fusion.3), channel_id=1, source_target_pairs={{0,16},{4,20},{8,24},{12,28},{1,17},{5,21},{9,25},{13,29},{2,18},{... | collective-permute-start | bytes 3342344 | tf_op jit(solution)/shard_map/ppermute | solution.py:19
  82.4 5.8 %convolution_convert_fusion = bf16[512,2048]{1,0:T(8,128)(2,1)} fusion(bf16[2048,2048]{1,0:T(8,128)(2,1)S(1)} %bitcast.133, bf16[1,512,2048]{2,1,0:T(8,128)(2,1)S(1)} %copy-done.22, f32[512]{0:T(512)S(1)} %bitcast.130), kind=kOutput, calls=%fused_computation.26 | convolution fusion | flops 4299161600 | bytes 12584960 | tf_op jit(solution)/shard_map/dot_general | solution.py:76
  88.2 3.9 %copy.94 = bf16[512,2048]{0,1:T(8,128)(2,1)} copy(bf16[512,2048]{1,0:T(8,128)(2,1)} %convolution_convert_fusion) | data formatting | bytes 4194304 | tf_op jit(solution)/shard_map/reshape | solution.py:55
  92.2 4.0 %fusion.11 = f32[16,128,128]{2,1,0:T(8,128)} fusion(bf16[512,16,128]{0,2,1:T(8,128)(2,1)} %bitcast.111, bf16[512,16,128]{0,2,1:T(8,128)(2,1)S(1)} %bitcast.108, f32[512,16]{0,1:T(8,128)S(1)} %get-tuple-element.28), kind=kOutput, calls=%fused_computation.20 | convolution fusion | flops 807403520 | bytes 5275648 | tf_op jit(solution)/shard_map/thd,the->hde/dot_general | solution.py:81
  96.1 6.4 %fusion.25 = f32[16,512,128]{1,2,0:T(8,128)S(1)} fusion(bf16[16,512,512]{2,1,0:T(8,128)(2,1)} %multiply_convert_fusion, bf16[512,16,128]{2,1,0:T(8,128)(2,1)S(1)} %bitcast.120), kind=kOutput, calls=%fused_computation.35 | convolution fusion | flops 1073741824 | bytes 14680064 | tf_op jit(solution)/shard_map/hts,shd->thd/dot_general | solution.py:89
  102.5 26.9 %collective-permute-done.2 = f32[16,136,128]{2,1,0:T(8,128)} collective-permute-done((f32[16,136,128]{2,1,0:T(8,128)S(1)}, f32[16,136,128]{2,1,0:T(8,128)}, u32[]{:S(2)}, u32[]{:S(2)}) %collective-permute-start.2) | collective-permute-done | bytes 1114144 | tf_op jit(solution)/shard_map/ppermute | solution.py:19
  129.5 1.8 fusion.31
  131.3 1.5 fusion.8
  132.9 8.1 %fusion.18 = f32[2048,2048]{1,0:T(8,128)} fusion(bf16[512,2048]{0,1:T(8,128)(2,1)S(1)} %bitcast.127, bf16[1,512,2048]{2,1,0:T(8,128)(2,1)S(1)} %copy-done.23, f32[512]{0:T(512)S(1)} %bitcast.131), kind=kOutput, calls=%fused_computation.28 | convolution fusion | flops 4298113024 | bytes 20973568 | tf_op jit(solution)/shard_map/dot_general | solution.py:94
  141.0 1.4 pad_maximum_fusion
  142.4 3.1 collective-permute-start.3
  145.5 35.0 %collective-permute-done.3 = f32[16,136,128]{2,1,0:T(8,128)S(1)} collective-permute-done((f32[16,136,128]{2,1,0:T(8,128)S(1)}, f32[16,136,128]{2,1,0:T(8,128)S(1)}, u32[]{:S(2)}, u32[]{:S(2)}) %collective-permute-start.3) | collective-permute-done | bytes 1114144 | tf_op jit(solution)/shard_map/ppermute | solution.py:19
  181.0 1.1 pad_maximum_fusion.4
  182.2 2.7 collective-permute-start.4
  185.0 7.0 %multiply_convert_fusion.1 = bf16[16,512,512]{2,1,0:T(8,128)(2,1)S(1)} fusion(bf16[512,16,128]{0,2,1:T(8,128)(2,1)S(1)} %bitcast.112, f32[16,512]{1,0:T(8,128)S(1)} %get-tuple-element.33, pred[512,512]{1,0:T(8,128)(4,1)S(1)} %copy-done.19, bf16[512,16,128]{2,1,0:T(8,128)(2,1)S(1)} %bitcast.121), kind=kOutput, calls=%fused_computation.1 | convolution fusion | flops 1098907648 | bytes 12877824 | tf_op jit(solution)/shard_map/thd,shd->hts/dot_general | solution.py:101
  192.0 4.7 %fusion.35 = f32[16,512,128]{1,2,0:T(8,128)} fusion(bf16[16,512,512]{2,1,0:T(8,128)(2,1)S(1)} %multiply_convert_fusion.1, bf16[512,16,128]{0,2,1:T(8,128)(2,1)S(1)} %bitcast.117), kind=kOutput, calls=%fused_computation.74 | convolution fusion | flops 1073741824 | bytes 14680064 | tf_op jit(solution)/shard_map/hts,shd->thd/dot_general | solution.py:105
  196.7 14.1 %collective-permute-done.4 = f32[16,136,128]{2,1,0:T(8,128)} collective-permute-done((f32[16,136,128]{2,1,0:T(8,128)}, f32[16,136,128]{2,1,0:T(8,128)}, u32[]{:S(2)}, u32[]{:S(2)}) %collective-permute-start.4) | collective-permute-done | bytes 1114144 | tf_op jit(solution)/shard_map/ppermute | solution.py:19
  210.8 1.1 exponential_reduce_fusion.1
  211.9 1.8 multiply_add_fusion
  213.7 1.1 pad_maximum_fusion.5
  214.8 1.5 collective-permute-start.5
  216.4 3.3 fusion.37
  219.7 3.2 fusion.36
  222.9 3.1 fusion.10
  225.9 4.1 %copy.89 = bf16[1,512,2048]{2,1,0:T(8,128)(2,1)} copy(bf16[1,512,2048]{1,2,0:T(8,128)(2,1)} %bitcast.123) | data formatting | bytes 4194304
  230.0 12.0 %collective-permute-done.5 = f32[16,136,128]{2,1,0:T(8,128)} collective-permute-done((f32[16,136,128]{2,1,0:T(8,128)}, f32[16,136,128]{2,1,0:T(8,128)}, u32[]{:S(2)}, u32[]{:S(2)}) %collective-permute-start.5) | collective-permute-done | bytes 1114144 | tf_op jit(solution)/shard_map/ppermute | solution.py:19
  242.0 2.3 fusion.30
  244.4 0.9 copy-done.3
  245.3 3.3 fusion.6
  248.5 4.1 %copy.90 = bf16[1,512,2048]{2,1,0:T(8,128)(2,1)} copy(bf16[1,512,2048]{1,2,0:T(8,128)(2,1)} %bitcast.125) | data formatting | bytes 4194304
  252.6 5.0 %fusion.4 = bf16[512,16,128]{0,2,1:T(8,128)(2,1)} fusion(f32[16,128,512]{2,1,0:T(8,128)} %fusion.36, f32[16,128,128]{2,1,0:T(8,128)S(1)} %fusion.30, bf16[512,16,128]{0,2,1:T(8,128)(2,1)S(1)} %bitcast.118, f32[512,16]{0,1:T(8,128)S(1)} %get-tuple-element.26), kind=kOutput, calls=%fused_computation.10 | convolution fusion | flops 808452096 | bytes 9469952 | tf_op jit(solution)/shard_map/hde,shd->she/dot_general | solution.py:114
  257.6 3.9 %copy.91 = bf16[1,512,2048]{2,1,0:T(8,128)(2,1)} copy(bf16[1,512,2048]{1,2,0:T(8,128)(2,1)} %bitcast.124) | data formatting | bytes 4194304
  261.5 110.8 %reduce-scatter.2.cloned.1.call-done = f32[64,2048]{1,0:T(8,128)} async-done(((f32[2048,2048]{1,0:T(8,128)}), f32[64,2048]{1,0:T(8,128)}) %reduce-scatter.2.cloned.1.call-update) | async-done | bytes 524304 | tf_op jit(solution)/shard_map/reduce_scatter | solution.py:98
  (80 shorter events, 2.2 us)
Async XLA Ops:
  7.2 0.8 copy-start
  7.2 365.1 %reduce-scatter.2.cloned.1.call-start = ((), (), s32[]{:S(2)}) async-start(), calls=%async_computation.1 | async-start | bytes 17301504 | tf_op jit(solution)/shard_map/reduce_scatter | solution.py:98
  12.5 3.0 copy-start.4
  15.5 2.0 copy-start.8
  18.7 27.6 %collective-permute-start = (f32[16,136,128]{2,1,0:T(8,128)}, f32[16,136,128]{2,1,0:T(8,128)}, u32[]{:S(2)}, u32[]{:S(2)}) collective-permute-start(f32[16,136,128]{2,1,0:T(8,128)} %pad_maximum_fusion.1), channel_id=1, source_target_pairs={{0,4},{4,8},{8,12},{12,16},{16,20},{20,24},{24,28},{1,5},{5,9},{9,... | collective-permute-start | bytes 3342344 | tf_op jit(solution)/shard_map/ppermute | solution.py:19
  21.9 3.0 copy-start.20
  21.9 3.0 copy-start.21
  24.9 27.5 %copy-start.18 = (pred[512,512]{1,0:T(8,128)(4,1)}, pred[512,512]{1,0:T(8,128)(4,1)S(1)}, u32[]{:S(2)}) copy-start(pred[512,512]{1,0:T(8,128)(4,1)S(1)} %iota_compare_fusion) | copy-start | bytes 786436
  24.9 27.5 %copy-start.5 = (bf16[1,512,2048]{1,2,0:T(8,128)(2,1)S(1)}, bf16[1,512,2048]{1,2,0:T(8,128)(2,1)}, u32[]{:S(2)}) copy-start(bf16[1,512,2048]{1,2,0:T(8,128)(2,1)} %copy-done.4) | copy-start | bytes 6291460
  48.8 33.6 %slice-start.2 = ((s8[8388608]{0:T(1024)(128)(4,1)}), s8[4194304]{0:T(1024)(128)(4,1)S(1)}, s32[]{:S(2)}) async-start(s8[8388608]{0:T(1024)(128)(4,1)} %bitcast.132), calls=%async_computation.4 | async-start | bytes 8388608
  48.9 26.7 %collective-permute-start.1 = (f32[16,136,128]{2,1,0:T(8,128)S(1)}, f32[16,136,128]{2,1,0:T(8,128)S(1)}, u32[]{:S(2)}, u32[]{:S(2)}) collective-permute-start(f32[16,136,128]{2,1,0:T(8,128)S(1)} %pad_maximum_fusion.2), channel_id=1, source_target_pairs={{0,8},{4,12},{8,16},{12,20},{16,24},{20,28},{1,9},{5,13},{9,17},{1... | collective-permute-start | bytes 3342344 | tf_op jit(solution)/shard_map/ppermute | solution.py:19
  52.4 30.0 %slice-start.3 = ((s8[8388608]{0:T(1024)(128)(4,1)}), s8[4194304]{0:T(1024)(128)(4,1)S(1)}, s32[]{:S(2)}) async-start(s8[8388608]{0:T(1024)(128)(4,1)} %bitcast.132), calls=%async_computation.5 | async-start | bytes 8388608
  75.6 1.5 copy-start.16
  76.7 5.7 %copy-start.22 = (bf16[1,512,2048]{2,1,0:T(8,128)(2,1)S(1)}, bf16[1,512,2048]{2,1,0:T(8,128)(2,1)}, u32[]{:S(2)}) copy-start(bf16[1,512,2048]{2,1,0:T(8,128)(2,1)} %param.11) | copy-start | bytes 6291460
  77.1 52.4 %collective-permute-start.2 = (f32[16,136,128]{2,1,0:T(8,128)S(1)}, f32[16,136,128]{2,1,0:T(8,128)}, u32[]{:S(2)}, u32[]{:S(2)}) collective-permute-start(f32[16,136,128]{2,1,0:T(8,128)S(1)} %pad_maximum_fusion.3), channel_id=1, source_target_pairs={{0,16},{4,20},{8,24},{12,28},{1,17},{5,21},{9,25},{13,29},{2,18},{... | collective-permute-start | bytes 3342344 | tf_op jit(solution)/shard_map/ppermute | solution.py:19
  92.2 4.0 %copy-start.9 = (bf16[64,8,16,128]{3,2,1,0:T(8,128)(2,1)S(1)}, bf16[64,8,16,128]{3,2,1,0:T(8,128)(2,1)}, u32[]{:S(2)}) copy-start(bf16[64,8,16,128]{3,2,1,0:T(8,128)(2,1)} %copy-done.8) | copy-start | bytes 6291460
  96.1 33.3 %copy-start.17 = (f32[16,136,128]{2,1,0:T(8,128)S(1)}, f32[16,136,128]{2,1,0:T(8,128)}, u32[]{:S(2)}) copy-start(f32[16,136,128]{2,1,0:T(8,128)} %copy-done.16) | copy-start | bytes 3342340
  131.3 1.6 copy-start.23
  141.0 39.7 %copy-start.13 = (f32[16,128,128]{2,1,0:T(8,128)S(1)}, f32[16,128,128]{2,1,0:T(8,128)}, u32[]{:S(2)}) copy-start(f32[16,128,128]{2,1,0:T(8,128)} %fusion.11) | copy-start | bytes 3145732
  142.4 38.1 %collective-permute-start.3 = (f32[16,136,128]{2,1,0:T(8,128)S(1)}, f32[16,136,128]{2,1,0:T(8,128)S(1)}, u32[]{:S(2)}, u32[]{:S(2)}) collective-permute-start(f32[16,136,128]{2,1,0:T(8,128)S(1)} %pad_maximum_fusion), channel_id=1, source_target_pairs={{4,0},{8,4},{12,8},{16,12},{20,16},{24,20},{28,24},{5,1},{9,5},{13... | collective-permute-start | bytes 3342344 | tf_op jit(solution)/shard_map/ppermute | solution.py:19
  180.5 1.6 copy-start.15
  180.7 4.3 %copy-start.2 = (bf16[512,2048]{0,1:T(8,128)(2,1)S(1)}, bf16[512,2048]{0,1:T(8,128)(2,1)}, u32[]{:S(2)}) copy-start(bf16[512,2048]{0,1:T(8,128)(2,1)} %copy.94) | copy-start | bytes 6291460
  180.7 4.3 %copy-start.10 = (bf16[64,8,16,128]{3,2,1,0:T(8,128)(2,1)S(1)}, bf16[64,8,16,128]{3,2,1,0:T(8,128)(2,1)}, u32[]{:S(2)}) copy-start(bf16[64,8,16,128]{3,2,1,0:T(8,128)(2,1)} %copy-done.8) | copy-start | bytes 6291460
  180.7 4.3 %copy-start.19 = (pred[512,512]{1,0:T(8,128)(4,1)S(1)}, pred[512,512]{1,0:T(8,128)(4,1)}, u32[]{:S(2)}) copy-start(pred[512,512]{1,0:T(8,128)(4,1)} %copy-done.18) | copy-start | bytes 786436
  180.9 1.3 copy-start.14
  182.2 9.7 %copy-start.6 = (bf16[1,512,2048]{1,2,0:T(8,128)(2,1)S(1)}, bf16[1,512,2048]{1,2,0:T(8,128)(2,1)}, u32[]{:S(2)}) copy-start(bf16[1,512,2048]{1,2,0:T(8,128)(2,1)} %copy-done.4) | copy-start | bytes 6291460
  182.2 28.6 %collective-permute-start.4 = (f32[16,136,128]{2,1,0:T(8,128)}, f32[16,136,128]{2,1,0:T(8,128)}, u32[]{:S(2)}, u32[]{:S(2)}) collective-permute-start(f32[16,136,128]{2,1,0:T(8,128)} %pad_maximum_fusion.4), channel_id=1, source_target_pairs={{8,0},{12,4},{16,8},{20,12},{24,16},{28,20},{9,1},{13,5},{17,9},{2... | collective-permute-start | bytes 3342344 | tf_op jit(solution)/shard_map/ppermute | solution.py:19
  213.7 5.9 %slice-start = ((s8[8388608]{0:T(1024)(128)(4,1)}), s8[4194304]{0:T(1024)(128)(4,1)S(1)}, s32[]{:S(2)}) async-start(s8[8388608]{0:T(1024)(128)(4,1)} %bitcast.105), calls=%async_computation.2 | async-start | bytes 8388608
  214.8 4.8 %slice-start.1 = ((s8[8388608]{0:T(1024)(128)(4,1)}), s8[4194304]{0:T(1024)(128)(4,1)S(1)}, s32[]{:S(2)}) async-start(s8[8388608]{0:T(1024)(128)(4,1)} %bitcast.105), calls=%async_computation.3 | async-start | bytes 8388608
  214.8 27.2 %collective-permute-start.5 = (f32[16,136,128]{2,1,0:T(8,128)}, f32[16,136,128]{2,1,0:T(8,128)}, u32[]{:S(2)}, u32[]{:S(2)}) collective-permute-start(f32[16,136,128]{2,1,0:T(8,128)} %pad_maximum_fusion.5), channel_id=1, source_target_pairs={{16,0},{20,4},{24,8},{28,12},{17,1},{21,5},{25,9},{29,13},{18,2},{... | collective-permute-start | bytes 3342344 | tf_op jit(solution)/shard_map/ppermute | solution.py:19
  219.7 3.2 copy-start.12
  225.9 18.4 %copy-start.11 = (bf16[64,8,16,128]{3,2,1,0:T(8,128)(2,1)S(1)}, bf16[64,8,16,128]{3,2,1,0:T(8,128)(2,1)}, u32[]{:S(2)}) copy-start(bf16[64,8,16,128]{3,2,1,0:T(8,128)(2,1)} %copy-done.8) | copy-start | bytes 6291460
  242.0 3.2 copy-start.3
  248.5 4.1 %copy-start.7 = (bf16[1,512,2048]{1,2,0:T(8,128)(2,1)S(1)}, bf16[1,512,2048]{1,2,0:T(8,128)(2,1)}, u32[]{:S(2)}) copy-start(bf16[1,512,2048]{1,2,0:T(8,128)(2,1)} %copy-done.4) | copy-start | bytes 6291460
  257.6 114.7 %copy-start.1 = (f32[1,512,16]{1,2,0:T(8,128)S(1)}, f32[1,512,16]{1,2,0:T(8,128)}, u32[]{:S(2)}) copy-start(f32[1,512,16]{1,2,0:T(8,128)} %param.13) | copy-start | bytes 98308
Sparse Core Ops, SparseCore 0:
  141.1 231.1 reduce-scatter.1

commit v10 on v7

--- a/solution.py
+++ b/solution.py
@@ -16,7 +16,12 @@
     distance = 1
     while distance < count:
         pairs = [(i, i + step * distance) for i in range(count) if 0 <= i + step * distance < count]
-        arrived = jax.tree.map(lambda part: lax.ppermute(part, axis, pairs), partial)
+        if distance * 2 < count:
+            arrived = lax.ppermute(partial, axis, pairs)
+        else:
+            rows = partial.shape[1] - 8
+            arrived = lax.ppermute(partial[:, :rows], axis, pairs)
+            arrived = jnp.concatenate([arrived, jnp.zeros_like(partial[:, rows:])], axis=1)
         gathered = arrived if gathered is None else join(arrived, gathered)
         if distance * 2 < count:
             partial = join(arrived, partial)

time: 377 us -> 378 us (level)
  waiting for transfers between devices: 235 us -> 226 us
  matrix products: 65.6 us -> 73 us
  other arithmetic: 13.3 us -> 18.1 us
    ppermute x6, waiting for transfers between devices: 125 us -> 114 us  [the longest x4 65.8 us: carried_in(): arrived = lax.ppermute(partial, axis, pairs)]
    dot_general x1, matrix products: 5.81 us -> 9.89 us  [on_device(): lax.dot_general(weighted, out_weight, (((1,), (1,)), ((), ())), preferred...]
    unnamed x71 -> x65, local copies, waits for them, and re-layouts: 19.2 us -> 18.5 us
  transfers between devices with their start and end apart: 7 -> 7, of which waited for: 7 -> 7; matrix products, arithmetic and copies ran while one was open for 22% -> 23% of each run, Pallas kernels for 0% -> 0%
where the time goes in v10:
time: 378 us; the launch traced here: 377 us
  waiting for transfers between devices  226 us (60%)
  matrix products  73 us (19%)
  local copies, waits for them, and re-layouts  27.8 us (7%)
  starting transfers between devices  18.2 us (5%)
  other arithmetic  18.1 us (5%)
  between operations  14.5 us (4%)
    reduce_scatter x1, waiting for transfers between devices, on_device(): lax.psum_scatter(partial, ('ctx', 'dp'), scatter_dimension=0, tiled=True)  112 us
    ppermute x4, waiting for transfers between devices, carried_in(): arrived = lax.ppermute(partial, axis, pairs)  65.8 us
    ppermute x2, waiting for transfers between devices, carried_in(): arrived = lax.ppermute(partial[:, :rows], axis, pairs)  48.5 us
    unnamed x65, local copies, waits for them, and re-layouts  18.5 us
    ppermute x4, starting transfers between devices, carried_in(): arrived = lax.ppermute(partial, axis, pairs)  12.4 us
    dot_general x1, matrix products, on_device(): lax.dot_general(weighted, out_weight, (((1,), (1,)), ((), ())), preferred...  9.89 us
    add x6, other arithmetic, chain_join(): jnp.exp(later[0])[:, None, None] * earlier[1] + later[1]  9.54 us
    dot_general x1, matrix products, on_device(): jnp.einsum('hts,shd->thd', dprobs, key_heads, preferred_element_type=jnp....  8.24 us
  transfers between devices with their start and end apart: 7, of which 7 were waited for; matrix products, arithmetic and copies ran while one was open for 23% of the time, Pallas kernels for 0%

profile of v10, /device:TPU:11, one launch (start us, length us, event | category | flops | bytes accessed | tf_op | source)
XLA Modules:
  0.0 377.5 jit_solution(17766368082640626795)
XLA Ops:
  7.2 0.7 copy-done
  7.9 1.1 reduce-window.6
  9.6 2.9 copy.94
  12.5 3.0 copy.98
  15.5 2.0 fusion.14
  17.6 1.1 pad_maximum_fusion.1
  18.7 3.2 collective-permute-start
  22.6 3.0 copy.82
  25.6 9.9 %convolution_convert_fusion = bf16[512,2048]{1,0:T(8,128)(2,1)} fusion(bf16[2048,2048]{1,0:T(8,128)(2,1)} %param.12, bf16[1,512,2048]{2,1,0:T(8,128)(2,1)} %param.11, f32[512]{0:T(512)S(1)} %bitcast.130), kind=kOutput, calls=%fused_computation.26 | convolution fusion | flops 4299161600 | bytes 12584960 | tf_op jit(solution)/shard_map/dot_general | solution.py:82
  35.5 2.9 copy.95
  38.5 7.9 %collective-permute-done = f32[16,136,128]{2,1,0:T(8,128)} collective-permute-done((f32[16,136,128]{2,1,0:T(8,128)}, f32[16,136,128]{2,1,0:T(8,128)}, u32[]{:S(2)}, u32[]{:S(2)}) %collective-permute-start) | collective-permute-done | bytes 1114144 | tf_op jit(solution)/shard_map/ppermute | solution.py:20
  46.3 1.4 multiply_add_fusion.3
  47.7 1.1 exponential_reduce_fusion.3
  48.9 3.2 collective-permute-start.1
  52.2 6.2 %multiply_convert_fusion = bf16[16,512,512]{2,1,0:T(8,128)(2,1)S(1)} fusion(bf16[512,16,128]{0,2,1:T(8,128)(2,1)S(1)} %bitcast.115, f32[16,512]{1,0:T(8,128)S(1)} %get-tuple-element.38, pred[512,512]{1,0:T(8,128)(4,1)S(1)} %iota_compare_fusion, bf16[512,16,128]{2,1,0:T(8,128)(2,1)S(1)} %bitcast.112), kind=kOutput, calls=%fused_computation | convolution fusion | flops 1098907648 | bytes 12877824 | tf_op jit(solution)/shard_map/thd,shd->hts/dot_general | solution.py:93
  58.4 16.9 %collective-permute-done.1 = f32[16,136,128]{2,1,0:T(8,128)S(1)} collective-permute-done((f32[16,136,128]{2,1,0:T(8,128)S(1)}, f32[16,136,128]{2,1,0:T(8,128)S(1)}, u32[]{:S(2)}, u32[]{:S(2)}) %collective-permute-start.1) | collective-permute-done | bytes 1114144 | tf_op jit(solution)/shard_map/ppermute | solution.py:20
  75.4 1.3 multiply_add_fusion.2
  76.7 4.4 %collective-permute-start.2 = (f32[16,128,128]{2,1,0:T(8,128)}, f32[16,128,128]{2,1,0:T(8,128)S(1)}, u32[]{:S(2)}, u32[]{:S(2)}) collective-permute-start(f32[16,128,128]{2,1,0:T(8,128)} %multiply_add_fusion.2), channel_id=1, source_target_pairs={{0,16},{4,20},{8,24},{12,28},{1,17},{5,21},{9,25},{13,29},{2,18},{... | collective-permute-start | bytes 3145736 | tf_op jit(solution)/shard_map/ppermute | solution.py:23
  81.1 2.3 fusion.11
  83.4 6.4 %fusion.28 = f32[16,512,128]{1,2,0:T(8,128)} fusion(bf16[16,512,512]{2,1,0:T(8,128)(2,1)S(1)} %multiply_convert_fusion, bf16[512,16,128]{2,1,0:T(8,128)(2,1)} %bitcast.119), kind=kOutput, calls=%fused_computation.38 | convolution fusion | flops 1073741824 | bytes 14680064 | tf_op jit(solution)/shard_map/hts,shd->thd/dot_general | solution.py:95
  89.8 1.1 fusion.35
  90.9 35.5 %collective-permute-done.2 = f32[16,128,128]{2,1,0:T(8,128)S(1)} collective-permute-done((f32[16,128,128]{2,1,0:T(8,128)}, f32[16,128,128]{2,1,0:T(8,128)S(1)}, u32[]{:S(2)}, u32[]{:S(2)}) %collective-permute-start.2) | collective-permute-done | bytes 1048608 | tf_op jit(solution)/shard_map/ppermute | solution.py:23
  126.4 2.0 add_add_fusion.1
  128.6 3.8 %fusion.8 = bf16[512,16,128]{0,2,1:T(8,128)(2,1)S(1)} fusion(f32[16,512,128]{1,2,0:T(8,128)} %fusion.28, f32[16,128,128]{2,1,0:T(8,128)S(1)} %add_add_fusion.1, bf16[512,16,128]{0,2,1:T(8,128)(2,1)S(1)} %copy-done.16, f32[512,16]{0,1:T(8,128)S(1)} %get-tuple-element.35), kind=kOutput, calls=%fused_computation.16 | convolution fusion | flops 808452096 | bytes 9469952 | tf_op jit(solution)/shard_map/thd,hde->the/dot_general | solution.py:96
  132.5 8.2 %fusion.18 = f32[2048,2048]{1,0:T(8,128)} fusion(bf16[512,2048]{0,1:T(8,128)(2,1)S(1)} %bitcast.127, bf16[1,512,2048]{2,1,0:T(8,128)(2,1)S(1)} %copy-done.27, f32[512]{0:T(512)S(1)} %bitcast.131), kind=kOutput, calls=%fused_computation.28 | convolution fusion | flops 4298113024 | bytes 20973568 | tf_op jit(solution)/shard_map/dot_general | solution.py:100
  140.7 1.5 pad_maximum_fusion
  142.1 3.2 collective-permute-start.3
  145.3 7.9 %multiply_convert_fusion.1 = bf16[16,512,512]{2,1,0:T(8,128)(2,1)S(1)} fusion(bf16[512,16,128]{0,2,1:T(8,128)(2,1)S(1)} %bitcast.108, f32[16,512]{1,0:T(8,128)S(1)} %get-tuple-element.38, pred[512,512]{1,0:T(8,128)(4,1)} %copy-done.24, bf16[512,16,128]{2,1,0:T(8,128)(2,1)S(1)} %bitcast.120), kind=kOutput, calls=%fused_computation.1 | convolution fusion | flops 1098907648 | bytes 12877824 | tf_op jit(solution)/shard_map/thd,shd->hts/dot_general | solution.py:107
  153.3 27.2 %collective-permute-done.3 = f32[16,136,128]{2,1,0:T(8,128)S(1)} collective-permute-done((f32[16,136,128]{2,1,0:T(8,128)S(1)}, f32[16,136,128]{2,1,0:T(8,128)S(1)}, u32[]{:S(2)}, u32[]{:S(2)}) %collective-permute-start.3) | collective-permute-done | bytes 1114144 | tf_op jit(solution)/shard_map/ppermute | solution.py:20
  181.9 1.1 pad_maximum_fusion.3
  183.0 2.9 collective-permute-start.4
  185.9 3.7 fusion.25
  189.5 8.2 %fusion.39 = f32[16,512,128]{1,2,0:T(8,128)} fusion(bf16[16,512,512]{2,1,0:T(8,128)(2,1)} %copy-done.3, bf16[512,16,128]{0,2,1:T(8,128)(2,1)S(1)} %bitcast.116), kind=kOutput, calls=%fused_computation.76 | convolution fusion | flops 1073741824 | bytes 14680064 | tf_op jit(solution)/shard_map/hts,shd->thd/dot_general | solution.py:111
  197.8 13.7 %collective-permute-done.4 = f32[16,136,128]{2,1,0:T(8,128)} collective-permute-done((f32[16,136,128]{2,1,0:T(8,128)}, f32[16,136,128]{2,1,0:T(8,128)}, u32[]{:S(2)}, u32[]{:S(2)}) %collective-permute-start.4) | collective-permute-done | bytes 1114144 | tf_op jit(solution)/shard_map/ppermute | solution.py:20
  211.5 2.4 multiply_add_fusion
  213.9 1.3 collective-permute-start.5
  215.2 3.2 fusion.40
  218.5 3.0 fusion.10
  221.4 4.1 %copy.89 = bf16[1,512,2048]{2,1,0:T(8,128)(2,1)} copy(bf16[1,512,2048]{1,2,0:T(8,128)(2,1)} %bitcast.122) | data formatting | bytes 4194304
  225.5 1.1 fusion.36
  226.6 13.0 %collective-permute-done.5 = f32[16,128,128]{2,1,0:T(8,128)} collective-permute-done((f32[16,128,128]{2,1,0:T(8,128)}, f32[16,128,128]{2,1,0:T(8,128)}, u32[]{:S(2)}, u32[]{:S(2)}) %collective-permute-start.5) | collective-permute-done | bytes 1048608 | tf_op jit(solution)/shard_map/ppermute | solution.py:23
  239.5 2.3 add_add_fusion
  241.9 0.9 copy-done.4
  242.8 3.3 fusion.6
  246.1 4.1 %copy.90 = bf16[1,512,2048]{2,1,0:T(8,128)(2,1)} copy(bf16[1,512,2048]{1,2,0:T(8,128)(2,1)} %bitcast.124) | data formatting | bytes 4194304
  250.1 5.0 %fusion.4 = bf16[512,16,128]{0,2,1:T(8,128)(2,1)} fusion(f32[16,128,512]{2,1,0:T(8,128)} %fusion.40, f32[16,128,128]{2,1,0:T(8,128)S(1)} %add_add_fusion, bf16[512,16,128]{0,2,1:T(8,128)(2,1)S(1)} %bitcast.117, f32[512,16]{0,1:T(8,128)S(1)} %get-tuple-element.32), kind=kOutput, calls=%fused_computation.10 | convolution fusion | flops 808452096 | bytes 9469952 | tf_op jit(solution)/shard_map/hde,shd->she/dot_general | solution.py:120
  255.1 3.9 %copy.91 = bf16[1,512,2048]{2,1,0:T(8,128)(2,1)} copy(bf16[1,512,2048]{1,2,0:T(8,128)(2,1)} %bitcast.123) | data formatting | bytes 4194304
  259.0 111.6 %reduce-scatter.2.cloned.1.call-done = f32[64,2048]{1,0:T(8,128)} async-done(((f32[2048,2048]{1,0:T(8,128)}), f32[64,2048]{1,0:T(8,128)}) %reduce-scatter.2.cloned.1.call-update) | async-done | bytes 524304 | tf_op jit(solution)/shard_map/reduce_scatter | solution.py:104
  (78 shorter events, 3.3 us)
Async XLA Ops:
  7.2 0.8 copy-start
  7.2 363.4 %reduce-scatter.2.cloned.1.call-start = ((), (), s32[]{:S(2)}) async-start(), calls=%async_computation.1 | async-start | bytes 17301504 | tf_op jit(solution)/shard_map/reduce_scatter | solution.py:104
  12.5 3.0 copy-start.8
  15.5 2.0 copy-start.12
  17.5 4.4 %copy-start.23 = (bf16[1,512,2048]{2,1,0:T(8,128)(2,1)S(1)}, bf16[1,512,2048]{2,1,0:T(8,128)(2,1)}, u32[]{:S(2)}) copy-start(bf16[1,512,2048]{2,1,0:T(8,128)(2,1)} %param.8) | copy-start | bytes 6291460
  18.7 27.6 %collective-permute-start = (f32[16,136,128]{2,1,0:T(8,128)}, f32[16,136,128]{2,1,0:T(8,128)}, u32[]{:S(2)}, u32[]{:S(2)}) collective-permute-start(f32[16,136,128]{2,1,0:T(8,128)} %pad_maximum_fusion.1), channel_id=1, source_target_pairs={{0,4},{4,8},{8,12},{12,16},{16,20},{20,24},{24,28},{1,5},{5,9},{9,... | collective-permute-start | bytes 3342344 | tf_op jit(solution)/shard_map/ppermute | solution.py:20
  22.5 3.0 copy-start.5
  22.5 3.0 copy-start.25
  22.5 3.0 copy-start.26
  38.4 13.7 %copy-start.24 = (pred[512,512]{1,0:T(8,128)(4,1)}, pred[512,512]{1,0:T(8,128)(4,1)S(1)}, u32[]{:S(2)}) copy-start(pred[512,512]{1,0:T(8,128)(4,1)S(1)} %iota_compare_fusion) | copy-start | bytes 786436
  38.4 13.7 %copy-start.6 = (bf16[64,8,16,128]{3,2,1,0:T(8,128)(2,1)S(1)}, bf16[64,8,16,128]{3,2,1,0:T(8,128)(2,1)}, u32[]{:S(2)}) copy-start(bf16[64,8,16,128]{3,2,1,0:T(8,128)(2,1)} %copy-done.5) | copy-start | bytes 6291460
  38.4 13.7 %copy-start.9 = (bf16[1,512,2048]{1,2,0:T(8,128)(2,1)S(1)}, bf16[1,512,2048]{1,2,0:T(8,128)(2,1)}, u32[]{:S(2)}) copy-start(bf16[1,512,2048]{1,2,0:T(8,128)(2,1)} %copy-done.8) | copy-start | bytes 6291460
  48.9 26.4 %collective-permute-start.1 = (f32[16,136,128]{2,1,0:T(8,128)S(1)}, f32[16,136,128]{2,1,0:T(8,128)S(1)}, u32[]{:S(2)}, u32[]{:S(2)}) collective-permute-start(f32[16,136,128]{2,1,0:T(8,128)S(1)} %pad_maximum_fusion.2), channel_id=1, source_target_pairs={{0,8},{4,12},{8,16},{12,20},{16,24},{20,28},{1,9},{5,13},{9,17},{1... | collective-permute-start | bytes 3342344 | tf_op jit(solution)/shard_map/ppermute | solution.py:20
  58.4 25.0 %copy-start.2 = (bf16[16,512,512]{2,1,0:T(8,128)(2,1)}, bf16[16,512,512]{2,1,0:T(8,128)(2,1)S(1)}, u32[]{:S(2)}) copy-start(bf16[16,512,512]{2,1,0:T(8,128)(2,1)S(1)} %multiply_convert_fusion) | copy-start | bytes 25165828
  58.4 22.7 %copy-start.15 = (bf16[512,16,128]{0,2,1:T(8,128)(2,1)S(1)}, bf16[512,16,128]{0,2,1:T(8,128)(2,1)}, u32[]{:S(2)}) copy-start(bf16[512,16,128]{0,2,1:T(8,128)(2,1)} %copy.82) | copy-start | bytes 6291460
  75.4 14.5 %copy-start.22 = (f32[16,136,128]{2,1,0:T(8,128)}, f32[16,136,128]{2,1,0:T(8,128)S(1)}, u32[]{:S(2)}) copy-start(f32[16,136,128]{2,1,0:T(8,128)S(1)} %collective-permute-done.1) | copy-start | bytes 3342340
  76.7 49.7 %collective-permute-start.2 = (f32[16,128,128]{2,1,0:T(8,128)}, f32[16,128,128]{2,1,0:T(8,128)S(1)}, u32[]{:S(2)}, u32[]{:S(2)}) collective-permute-start(f32[16,128,128]{2,1,0:T(8,128)} %multiply_add_fusion.2), channel_id=1, source_target_pairs={{0,16},{4,20},{8,24},{12,28},{1,17},{5,21},{9,25},{13,29},{2,18},{... | collective-permute-start | bytes 3145736 | tf_op jit(solution)/shard_map/ppermute | solution.py:23
  126.4 2.2 copy-start.16
  128.6 3.8 %copy-start.27 = (bf16[1,512,2048]{2,1,0:T(8,128)(2,1)S(1)}, bf16[1,512,2048]{2,1,0:T(8,128)(2,1)}, u32[]{:S(2)}) copy-start(bf16[1,512,2048]{2,1,0:T(8,128)(2,1)} %param.11) | copy-start | bytes 6291460
  140.6 4.7 %copy-start.13 = (bf16[64,8,16,128]{3,2,1,0:T(8,128)(2,1)S(1)}, bf16[64,8,16,128]{3,2,1,0:T(8,128)(2,1)}, u32[]{:S(2)}) copy-start(bf16[64,8,16,128]{3,2,1,0:T(8,128)(2,1)} %copy-done.12) | copy-start | bytes 6291460
  142.1 38.6 %copy-start.18 = (f32[16,128,128]{2,1,0:T(8,128)S(1)}, f32[16,128,128]{2,1,0:T(8,128)}, u32[]{:S(2)}) copy-start(f32[16,128,128]{2,1,0:T(8,128)} %fusion.11) | copy-start | bytes 3145732
  142.1 38.4 %collective-permute-start.3 = (f32[16,136,128]{2,1,0:T(8,128)S(1)}, f32[16,136,128]{2,1,0:T(8,128)S(1)}, u32[]{:S(2)}, u32[]{:S(2)}) collective-permute-start(f32[16,136,128]{2,1,0:T(8,128)S(1)} %pad_maximum_fusion), channel_id=1, source_target_pairs={{4,0},{8,4},{12,8},{16,12},{20,16},{24,20},{28,24},{5,1},{9,5},{13... | collective-permute-start | bytes 3342344 | tf_op jit(solution)/shard_map/ppermute | solution.py:20
  153.3 32.6 %copy-start.3 = (bf16[16,512,512]{2,1,0:T(8,128)(2,1)}, bf16[16,512,512]{2,1,0:T(8,128)(2,1)S(1)}, u32[]{:S(2)}) copy-start(bf16[16,512,512]{2,1,0:T(8,128)(2,1)S(1)} %multiply_convert_fusion.1) | copy-start | bytes 25165828
  180.5 1.0 copy-start.21
  180.7 5.1 %copy-start.7 = (bf16[64,8,16,128]{3,2,1,0:T(8,128)(2,1)S(1)}, bf16[64,8,16,128]{3,2,1,0:T(8,128)(2,1)}, u32[]{:S(2)}) copy-start(bf16[64,8,16,128]{3,2,1,0:T(8,128)(2,1)} %copy-done.5) | copy-start | bytes 6291460
  180.9 1.0 copy-start.19
  181.9 33.3 %slice-start = ((s8[8388608]{0:T(1024)(128)(4,1)}), s8[4194304]{0:T(1024)(128)(4,1)S(1)}, s32[]{:S(2)}) async-start(s8[8388608]{0:T(1024)(128)(4,1)} %bitcast.105), calls=%async_computation.2 | async-start | bytes 8388608
  183.0 6.5 %copy-start.10 = (bf16[1,512,2048]{1,2,0:T(8,128)(2,1)S(1)}, bf16[1,512,2048]{1,2,0:T(8,128)(2,1)}, u32[]{:S(2)}) copy-start(bf16[1,512,2048]{1,2,0:T(8,128)(2,1)} %copy-done.8) | copy-start | bytes 6291460
  183.0 32.2 %slice-start.1 = ((s8[8388608]{0:T(1024)(128)(4,1)}), s8[4194304]{0:T(1024)(128)(4,1)S(1)}, s32[]{:S(2)}) async-start(s8[8388608]{0:T(1024)(128)(4,1)} %bitcast.105), calls=%async_computation.3 | async-start | bytes 8388608
  183.0 28.5 %collective-permute-start.4 = (f32[16,136,128]{2,1,0:T(8,128)}, f32[16,136,128]{2,1,0:T(8,128)}, u32[]{:S(2)}, u32[]{:S(2)}) collective-permute-start(f32[16,136,128]{2,1,0:T(8,128)} %pad_maximum_fusion.3), channel_id=1, source_target_pairs={{8,0},{12,4},{16,8},{20,12},{24,16},{28,20},{9,1},{13,5},{17,9},{2... | collective-permute-start | bytes 3342344 | tf_op jit(solution)/shard_map/ppermute | solution.py:20
  189.5 22.0 %copy-start.20 = (f32[16,128,128]{2,1,0:T(8,128)S(1)}, f32[16,128,128]{2,1,0:T(8,128)}, u32[]{:S(2)}) copy-start(f32[16,128,128]{2,1,0:T(8,128)} %copy-done.19) | copy-start | bytes 3145732
  213.9 25.6 %collective-permute-start.5 = (f32[16,128,128]{2,1,0:T(8,128)}, f32[16,128,128]{2,1,0:T(8,128)}, u32[]{:S(2)}, u32[]{:S(2)}) collective-permute-start(f32[16,128,128]{2,1,0:T(8,128)} %multiply_add_fusion), channel_id=1, source_target_pairs={{16,0},{20,4},{24,8},{28,12},{17,1},{21,5},{25,9},{29,13},{18,2},{... | collective-permute-start | bytes 3145736 | tf_op jit(solution)/shard_map/ppermute | solution.py:23
  215.2 3.2 copy-start.17
  221.4 20.5 %copy-start.14 = (bf16[64,8,16,128]{3,2,1,0:T(8,128)(2,1)S(1)}, bf16[64,8,16,128]{3,2,1,0:T(8,128)(2,1)}, u32[]{:S(2)}) copy-start(bf16[64,8,16,128]{3,2,1,0:T(8,128)(2,1)} %copy-done.12) | copy-start | bytes 6291460
  239.5 3.2 copy-start.4
  246.1 4.1 %copy-start.11 = (bf16[1,512,2048]{1,2,0:T(8,128)(2,1)S(1)}, bf16[1,512,2048]{1,2,0:T(8,128)(2,1)}, u32[]{:S(2)}) copy-start(bf16[1,512,2048]{1,2,0:T(8,128)(2,1)} %copy-done.8) | copy-start | bytes 6291460
  255.1 115.5 %copy-start.1 = (f32[1,512,16]{1,2,0:T(8,128)S(1)}, f32[1,512,16]{1,2,0:T(8,128)}, u32[]{:S(2)}) copy-start(f32[1,512,16]{1,2,0:T(8,128)} %param.13) | copy-start | bytes 98308
Sparse Core Ops, SparseCore 0:
  140.8 229.8 reduce-scatter.1
